TPU v7x, 768 devices: a whole 4x8x12 slice. The times are simulated.
768 devices in a mesh: row: 48 (over z_lo, x, core), col: 16 (over y, z_hi).
Axes of the slice: x: 4, y: 8, z: 12 (z_hi: 2, z_lo: 6; z = z_hi * 6 + z_lo), core: 2. Of those that a mesh axis runs over, the one named last changes fastest.
Arguments:
- matrix: float32 [61440, 6144], P('row', 'col'), may hold values from -1 to 96, as said below
Outputs:
- stepped: float32 [61440, 6144], P('row', 'col')
Inputs may be any that keep to these rules, and one draw needn't show every extreme that they name: `matrix`: entries where global row equals global column lie in 64 to 96; all other entries lie in -1 to 1, so the symmetrized first diagonal tile is positive definite.
All inputs are finite; a program needn't handle non-finite values.
Results may differ from a plain program's by a relative error of at most 0.0003.
Values sent between devices are 32-bit elements; how exact they have to be, the bound alone decides.
No kernel may reach another device: no remote copies, remote signals or barrier semaphores. Data moves between devices by JAX's collectives and lax.ppermute only.
A program may use at most 32 MiB of HBM per device.

v0:
```python
import jax
import jax.numpy as jnp
from jax import lax
from jax.sharding import PartitionSpec as P

B = 64


def broadcast(x, axis, root):
    mine = lax.axis_index(axis) == root
    return lax.psum(jnp.where(mine, x, jnp.zeros_like(x)), axis)


def factor_panel(tile, panel_cols, row_id):
    corner = (tile + tile.T) / 2.0
    factor = jnp.linalg.cholesky(corner)
    solved = lax.linalg.triangular_solve(factor, panel_cols, left_side=True, lower=True)
    head = jnp.where(row_id == 0, factor.T, solved[:, :B])
    return jnp.concatenate([head, solved[:, B:]], axis=1)


def shards(matrix):
    rows_dev, cols_dev = matrix.shape
    n_row = lax.axis_size("row")
    n_col = lax.axis_size("col")
    row_id = lax.axis_index("row")
    col_id = lax.axis_index("col")
    panel_cols = matrix[:, :B].T
    corner_raw = matrix[:B, :B]
    tile = broadcast(corner_raw, "row", 0)
    mine = factor_panel(tile, panel_cols, row_id)
    lower_t = broadcast(mine, "col", 0)
    window_cols = cols_dev * n_col // n_row
    owned = lower_t[:, :window_cols]
    gathered = lax.all_gather(owned, "row", axis=1, tiled=True)
    column = jnp.arange(cols_dev, dtype=jnp.int32)
    global_tile = column // B * n_col + col_id
    position = global_tile % n_row * window_cols + global_tile // n_row * B + column % B
    col_factor = jnp.take(gathered, position, axis=1)
    change = lax.dot_general(
        lower_t,
        col_factor,
        (((0,), (0,)), ((), ())),
        precision=lax.Precision.HIGHEST,
        preferred_element_type=jnp.float32,
    )
    local_rows = jnp.arange(rows_dev, dtype=jnp.int32)
    keep_rows = jnp.logical_and(row_id == 0, local_rows < B)
    stepped = jnp.where(keep_rows[:, None], matrix, matrix - change)
    first_cols = jnp.where(col_id == 0, lower_t.T, stepped[:, :B])
    return jnp.concatenate([first_cols, stepped[:, B:]], axis=1)


def solution(mesh):
    placed = (P("row", "col"),)
    return jax.shard_map(
        shards, mesh=mesh, in_specs=placed, out_specs=P("row", "col"), check_vma=False
    )
```

profile of v0, /device:TPU:1, one launch (start us, length us, event | category | flops | bytes accessed | tf_op | source)
XLA Modules:
  0.0 656.4 jit_solution(12405361722574476303)
XLA Ops:
  6.5 0.0 all-reduce.2.cloned.1.call-start
  6.5 1.9 copy.13
  8.4 276.0 %psum.14 = f32[64,64]{0,1:T(8,128)S(1)} all-reduce(f32[64,64]{0,1:T(8,128)S(1)} %slice_select_fusion.1), channel_id=1, replica_groups=mesh['row'=48,'col'=16] {'row'}, use_global_device_ids=true, to_apply=%region_0.1 | all-reduce | flops 4096 | bytes 32768 | tf_op jit(solution)/shard_map/psum | solution.py:11
  284.4 0.1 copy.15
  284.5 0.1 copy.16
  284.6 0.1 copy.17
  284.7 5.9 cholesky.17
  290.6 0.6 compare_reduce_fusion
  291.2 0.7 select_bitcast_fusion
  291.9 4.9 custom-call.6
  296.8 2.0 fusion.1
  298.7 0.1 slice.42
  298.9 0.1 copy.24
  298.9 0.7 bitcast_select_fusion
  299.6 0.1 copy.19
  299.7 0.9 maximum_select_fusion
  300.6 0.0 all-reduce.2.cloned.1.call-update
  300.6 0.0 all-gather.2.cloned.1.call-start
  300.7 238.3 %all-reduce.2.cloned.1.call-done = f32[64,1280]{1,0:T(8,128)} async-done(((f32[64,1280]{1,0:T(8,128)}), f32[64,1280]{1,0:T(8,128)}) %all-reduce.2.cloned.1.call-update) | async-done | bytes 327696 | tf_op jit(solution)/shard_map/psum | solution.py:11
  539.0 1.4 slice.43
  540.4 0.0 all-gather.2.cloned.1.call-update
  540.5 0.0 copy-start
  540.5 98.9 %all-gather.2.cloned.1.call-done = f32[64,6144]{1,0:T(8,128)} async-done(((f32[64,128]{1,0:T(8,128)}), f32[64,6144]{1,0:T(8,128)}) %all-gather.2.cloned.1.call-update) | async-done | bytes 1572880 | tf_op jit(solution)/shard_map/all_gather | solution.py:35
  639.4 3.3 copy.20
  642.7 3.0 gather_fusion
  645.7 0.0 copy-done
  645.7 1.8 fusion
  647.5 0.1 slice.45
  647.7 0.1 pad_maximum_fusion
  647.8 1.8 copy.23
  (10 shorter events, 0.2 us)
Async XLA Ops:
  6.5 532.5 %all-reduce.2.cloned.1.call-start = ((), (), s32[]{:S(2)}) async-start(), calls=%async_computation | async-start | bytes 655360 | tf_op jit(solution)/shard_map/psum | solution.py:11
  300.6 338.8 %all-gather.2.cloned.1.call-start = ((), (), s32[]{:S(2)}) async-start(), calls=%async_computation.1 | async-start | bytes 1605632 | tf_op jit(solution)/shard_map/all_gather | solution.py:35
  540.5 105.2 %copy-start = (f32[64,1280]{1,0:T(8,128)S(1)}, f32[64,1280]{1,0:T(8,128)}, u32[]{:S(2)}) copy-start(f32[64,1280]{1,0:T(8,128)} %all-reduce.2.cloned.1.call-done) | copy-start | bytes 983044
Sparse Core Ops, SparseCore 0:
  300.7 238.2 all-reduce.1
  541.6 97.7 all-gather.1
where the time goes:
time: 657 us; the launch traced here: 656 us
  waiting for transfers between devices  337 us (51%)
  blocking collectives  276 us (42%)
  other arithmetic  13.9 us (2%)
  between operations  13.5 us (2%)
  local copies, waits for them, and re-layouts  11.9 us (2%)
    psum x1, blocking collectives, broadcast(): return lax.psum(jnp.where(mine, x, jnp.zeros_like(x)), axis)  276 us
    psum x1, waiting for transfers between devices, broadcast(): return lax.psum(jnp.where(mine, x, jnp.zeros_like(x)), axis)  238 us
    all_gather x1, waiting for transfers between devices, shards(): gathered = lax.all_gather(owned, 'row', axis=1, tiled=True)  98.9 us
  transfers between devices with their start and end apart: 2, of which 2 were waited for; matrix products, arithmetic and copies ran while one was open for 0% of the time, Pallas kernels for 0%

commit v1 on v0

v1 whole, which is shorter than its diff:
```python
import jax
import jax.numpy as jnp
from jax import lax
from jax.sharding import PartitionSpec as P

B = 64
RADIX = 2


def tree_broadcast(x, axes, size, index_of, member, radix=RADIX):
    have = 1
    while have < size:
        fresh = x
        for c in range(1, radix):
            lo = c * have
            if lo >= size:
                break
            pairs = []
            for src in index_of(None):
                for m in range(have):
                    if m + lo < size:
                        pairs.append((src(m), src(m + lo)))
            got = lax.ppermute(x, axes, pairs)
            take = jnp.logical_and(member >= lo, member < lo + have)
            fresh = jnp.where(take, got, fresh)
        x = fresh
        have *= radix
    return x


def shards(matrix):
    rows_dev, cols_dev = matrix.shape
    n_row = lax.axis_size("row")
    n_col = lax.axis_size("col")
    row_id = lax.axis_index("row")
    col_id = lax.axis_index("col")
    n_src = n_row // n_col
    window_cols = cols_dev * n_col // n_row

    panel_t = matrix[:, :B].T

    def col_groups(_):
        return [lambda m, r=r: r * n_col + m for r in range(n_row)]

    panel_t = tree_broadcast(panel_t, ("row", "col"), n_col, col_groups, col_id)

    head = panel_t[:, :window_cols]
    rel = (row_id - col_id) % n_row
    my_j = rel // n_col
    is_src = rel % n_col == 0
    pieces = [head]
    for c in range(1, n_src):
        pairs = []
        for q in range(n_col):
            for j in range(n_src):
                a = q + n_col * j
                b = q + n_col * ((j + c) % n_src)
                pairs.append((a * n_col + q, b * n_col + q))
        pieces.append(lax.ppermute(head, ("row", "col"), pairs))
    corner_t = panel_t[:, :B]
    got_corner = jnp.zeros_like(corner_t)
    for j in range(n_src):
        pairs = []
        for q in range(n_col):
            b = q + n_col * j
            if b != 0:
                pairs.append((0 * n_col + q, b * n_col + q))
        got_corner = got_corner + lax.ppermute(corner_t, ("row", "col"), pairs)
    corner_t = jnp.where(row_id == 0, corner_t, got_corner)
    ordered = []
    for jj in range(n_src):
        pick = pieces[0]
        for c in range(1, n_src):
            pick = jnp.where((my_j - jj) % n_src == c, pieces[c], pick)
        ordered.append(pick)
    packet = jnp.concatenate(ordered + [corner_t], axis=1)
    packet = jnp.where(is_src, packet, jnp.zeros_like(packet))

    def row_groups(_):
        out = []
        for q in range(n_col):
            for j in range(n_src):
                base = q + n_col * j
                out.append(lambda m, base=base, q=q: ((base + m) % n_row) * n_col + q)
        return out

    packet = tree_broadcast(packet, ("row", "col"), n_col, row_groups, rel % n_col)

    corner_t = packet[:, n_src * window_cols:]
    corner = (corner_t + corner_t.T) / 2.0
    factor = jnp.linalg.cholesky(corner)

    tiles = []
    for k in range(cols_dev // B):
        j = k % n_src
        lt = k // n_src
        tiles.append(packet[:, j * window_cols + lt * B: j * window_cols + (lt + 1) * B])
    window_t = jnp.concatenate(tiles, axis=1)

    both = jnp.concatenate([panel_t, window_t], axis=1)
    solved = lax.linalg.triangular_solve(factor, both, left_side=True, lower=True)
    lower_t = solved[:, :rows_dev]
    lower_t = jnp.concatenate(
        [jnp.where(row_id == 0, factor.T, lower_t[:, :B]), lower_t[:, B:]], axis=1
    )
    col_t = solved[:, rows_dev:]
    col_t = jnp.concatenate(
        [jnp.where(col_id == 0, factor.T, col_t[:, :B]), col_t[:, B:]], axis=1
    )
    change = lax.dot_general(
        lower_t,
        col_t,
        (((0,), (0,)), ((), ())),
        precision=lax.Precision.HIGHEST,
        preferred_element_type=jnp.float32,
    )
    local_rows = jnp.arange(rows_dev, dtype=jnp.int32)
    keep_rows = jnp.logical_and(row_id == 0, local_rows < B)
    stepped = jnp.where(keep_rows[:, None], matrix, matrix - change)
    first_cols = jnp.where(col_id == 0, lower_t.T, stepped[:, :B])
    return jnp.concatenate([first_cols, stepped[:, B:]], axis=1)


def solution(mesh):
    placed = (P("row", "col"),)
    return jax.shard_map(
        shards, mesh=mesh, in_specs=placed, out_specs=P("row", "col"), check_vma=False
    )
```

time: 657 us -> 154 us (0.23)
  the two profiles are of different devices: /device:TPU:1 before, /device:TPU:8 now
where the time goes in v1:
time: 154 us; the launch traced here: 153 us
  waiting for transfers between devices  91.7 us (60%)
  starting transfers between devices  35.7 us (23%)
  other arithmetic  14.6 us (9%)
  local copies, waits for them, and re-layouts  7.46 us (5%)
  matrix products  3.08 us (2%)
    ppermute x8, waiting for transfers between devices, tree_broadcast(): got = lax.ppermute(x, axes, pairs)  91.6 us
    ppermute x3, starting transfers between devices, shards(): got_corner = got_corner + lax.ppermute(corner_t, ('row', 'col'), pairs)  26.5 us
    ppermute x8, starting transfers between devices, tree_broadcast(): got = lax.ppermute(x, axes, pairs)  7.91 us
    another operation x3, other arithmetic, shards(): factor = jnp.linalg.cholesky(corner)  6.53 us
    another operation x2, other arithmetic, shards(): lax.linalg.triangular_solve(factor, both, left_side=True, lower=True)  5.55 us
  transfers between devices with their start and end apart: 13, of which 5 were waited for; matrix products, arithmetic and copies ran while one was open for 1% of the time, Pallas kernels for 0%

profile of v1, /device:TPU:8, one launch (start us, length us, event | category | flops | bytes accessed | tf_op | source)
XLA Modules:
  0.0 153.2 jit_solution(16602501657716732304)
XLA Ops:
  0.0 1.1 slice_bitcast_fusion
  1.1 0.2 copy.12
  1.4 0.7 collective-permute-start
  2.1 0.2 copy.13
  2.3 1.2 broadcast_select_fusion
  3.5 0.2 copy.14
  3.7 1.3 collective-permute-start.1
  5.0 28.6 %collective-permute-done.1 = f32[64,1280]{1,0:T(8,128)S(1)} collective-permute-done((f32[64,1280]{1,0:T(8,128)S(1)}, f32[64,1280]{1,0:T(8,128)S(1)}, u32[]{:S(2)}, u32[]{:S(2)}) %collective-permute-start.1) | collective-permute-done | bytes 327712 | tf_op jit(solution)/shard_map/ppermute | solution.py:23
  33.6 0.2 copy.15
  33.9 0.2 copy.16
  34.2 1.3 collective-permute-start.2
  35.5 18.8 %collective-permute-done.2 = f32[64,1280]{1,0:T(8,128)S(1)} collective-permute-done((f32[64,1280]{1,0:T(8,128)S(1)}, f32[64,1280]{1,0:T(8,128)S(1)}, u32[]{:S(2)}, u32[]{:S(2)}) %collective-permute-start.2) | collective-permute-done | bytes 327712 | tf_op jit(solution)/shard_map/ppermute | solution.py:23
  54.3 0.2 copy.17
  54.6 0.2 copy.18
  54.8 1.3 collective-permute-start.3
  56.1 14.4 %collective-permute-done.3 = f32[64,1280]{1,0:T(8,128)S(1)} collective-permute-done((f32[64,1280]{1,0:T(8,128)S(1)}, f32[64,1280]{1,0:T(8,128)S(1)}, u32[]{:S(2)}, u32[]{:S(2)}) %collective-permute-start.3) | collective-permute-done | bytes 327712 | tf_op jit(solution)/shard_map/ppermute | solution.py:23
  70.5 0.2 copy.19
  70.8 0.1 constant_dynamic-update-slice_fusion
  70.9 23.9 %collective-permute-start.8 = (f32[64,64]{0,1:T(8,128)S(1)}, f32[64,64]{0,1:T(8,128)S(1)}, u32[]{:S(2)}, u32[]{:S(2)}) collective-permute-start(f32[64,64]{0,1:T(8,128)S(1)} %slice.81), channel_id=1, source_target_pairs={{0,512},{1,529},{2,546},{3,563},{4,580},{5,597},{6,614},{7,631},{8... | collective-permute-start | bytes 49160 | tf_op jit(solution)/shard_map/ppermute | solution.py:68
  94.8 1.3 collective-permute-start.7
  96.1 1.3 collective-permute-start.6
  97.5 0.7 collective-permute-start.5
  98.2 0.7 collective-permute-start.4
  98.9 0.1 collective-permute-done.6
  99.0 0.7 collective-permute-start.9
  99.8 0.7 collective-permute-start.10
  100.5 0.7 collective-permute-start.11
  101.2 1.3 collective-permute-start.12
  102.6 1.9 %copy.28 = f32[1280,384]{0,1:T(8,128)S(1)} copy(f32[1280,384]{1,0:T(8,128)} %param.1) | data formatting | bytes 3932160 | tf_op args[0]
  104.5 29.7 %collective-permute-done.12 = f32[64,448]{0,1:T(8,128)S(1)} collective-permute-done((f32[64,448]{0,1:T(8,128)S(1)}, f32[64,448]{0,1:T(8,128)S(1)}, u32[]{:S(2)}, u32[]{:S(2)}) %collective-permute-start.12) | collective-permute-done | bytes 114720 | tf_op jit(solution)/shard_map/ppermute | solution.py:23
  134.4 0.1 copy.21
  134.5 0.1 copy.22
  134.6 5.9 %cholesky.18 = f32[64,64]{1,0:T(8,128)S(1)} custom-call(f32[64,64]{1,0:T(8,128)S(1)} %copy.22), custom_call_target="Cholesky" | custom-call | tf_op jit(solution)/shard_map/jit(cholesky)/cholesky | solution.py:91
  140.5 0.6 compare_reduce_fusion
  141.1 0.7 select_bitcast_fusion
  141.8 4.9 %custom-call.6 = f32[1,64,64]{1,2,0:T(8,128)S(1)} custom-call(f32[1,64,64]{2,1,0:T(8,128)S(1)} %select_bitcast_fusion), custom_call_target="InvertDiagBlocksLowerTriangular" | custom-call | tf_op jit(solution)/shard_map/triangular_solve | solution.py:101
  146.7 1.1 fusion.4
  147.8 0.1 slice.92
  147.9 0.1 slice.90
  148.1 0.1 copy.30
  148.2 0.7 bitcast_select_fusion
  148.9 0.1 copy.26
  149.0 0.1 copy.24
  149.1 1.9 %fusion = f32[1280,384]{0,1:T(8,128)S(1)} fusion(f32[1280,384]{0,1:T(8,128)S(1)} %copy.28, pred[1280]{0:T(1024)(128)(4,1)S(1)} %fusion.8, f32[64,1216]{1,0:T(8,128)S(1)} %slice.90, f32[64,64]{1,0:T(8,128)S(1)} %copy.24, f32[64,320]{1,0:T(8,128)S(1)} %slice.92, f32[64,64]{1,0:T(8,128)S(1)} %copy.26), kind=kOutput, calls=%fused_computation.1 | convolution fusion | flops 378576896 | bytes 4359424 | tf_op jit(solution)/shard_map/dot_general | solution.py:110
  151.0 0.2 slice_select_fusion
  151.2 0.1 slice.94
  151.3 0.1 pad_maximum_fusion
  151.4 1.8 %copy.29 = f32[1280,384]{1,0:T(8,128)} copy(f32[1280,384]{0,1:T(8,128)S(1)} %pad_maximum_fusion) | data formatting | bytes 3932160 | tf_op jit(solution)/shard_map/concatenate | solution.py:121
  (31 shorter events, 0.6 us)
Async XLA Ops:
  1.4 0.7 collective-permute-start
  3.7 29.9 %collective-permute-start.1 = (f32[64,1280]{1,0:T(8,128)S(1)}, f32[64,1280]{1,0:T(8,128)S(1)}, u32[]{:S(2)}, u32[]{:S(2)}) collective-permute-start(f32[64,1280]{1,0:T(8,128)S(1)} %copy.14), channel_id=1, source_target_pairs={{0,2},{1,3},{16,18},{17,19},{32,34},{33,35},{48,50},{49,51},{64,66... | collective-permute-start | bytes 983048 | tf_op jit(solution)/shard_map/ppermute | solution.py:23
  34.2 20.1 %collective-permute-start.2 = (f32[64,1280]{1,0:T(8,128)S(1)}, f32[64,1280]{1,0:T(8,128)S(1)}, u32[]{:S(2)}, u32[]{:S(2)}) collective-permute-start(f32[64,1280]{1,0:T(8,128)S(1)} %copy.16), channel_id=1, source_target_pairs={{0,4},{1,5},{2,6},{3,7},{16,20},{17,21},{18,22},{19,23},{32,36},{3... | collective-permute-start | bytes 983048 | tf_op jit(solution)/shard_map/ppermute | solution.py:23
  54.8 15.7 %collective-permute-start.3 = (f32[64,1280]{1,0:T(8,128)S(1)}, f32[64,1280]{1,0:T(8,128)S(1)}, u32[]{:S(2)}, u32[]{:S(2)}) collective-permute-start(f32[64,1280]{1,0:T(8,128)S(1)} %copy.18), channel_id=1, source_target_pairs={{0,8},{1,9},{2,10},{3,11},{4,12},{5,13},{6,14},{7,15},{16,24},{17,... | collective-permute-start | bytes 983048 | tf_op jit(solution)/shard_map/ppermute | solution.py:23
  70.9 28.0 %collective-permute-start.8 = (f32[64,64]{0,1:T(8,128)S(1)}, f32[64,64]{0,1:T(8,128)S(1)}, u32[]{:S(2)}, u32[]{:S(2)}) collective-permute-start(f32[64,64]{0,1:T(8,128)S(1)} %slice.81), channel_id=1, source_target_pairs={{0,512},{1,529},{2,546},{3,563},{4,580},{5,597},{6,614},{7,631},{8... | collective-permute-start | bytes 49160 | tf_op jit(solution)/shard_map/ppermute | solution.py:68
  94.8 4.1 %collective-permute-start.7 = (f32[64,64]{0,1:T(8,128)S(1)}, f32[64,64]{0,1:T(8,128)S(1)}, u32[]{:S(2)}, u32[]{:S(2)}) collective-permute-start(f32[64,64]{0,1:T(8,128)S(1)} %slice.81), channel_id=1, source_target_pairs={{0,256},{1,273},{2,290},{3,307},{4,324},{5,341},{6,358},{7,375},{8... | collective-permute-start | bytes 49160 | tf_op jit(solution)/shard_map/ppermute | solution.py:68
  96.1 2.9 %collective-permute-start.6 = (f32[64,64]{0,1:T(8,128)S(1)}, f32[64,64]{0,1:T(8,128)S(1)}, u32[]{:S(2)}, u32[]{:S(2)}) collective-permute-start(f32[64,64]{0,1:T(8,128)S(1)} %slice.81), channel_id=1, source_target_pairs={{1,17},{2,34},{3,51},{4,68},{5,85},{6,102},{7,119},{8,136},{9,153}... | collective-permute-start | bytes 49160 | tf_op jit(solution)/shard_map/ppermute | solution.py:68
  97.5 1.5 collective-permute-start.5
  98.2 0.8 collective-permute-start.4
  99.0 0.7 collective-permute-start.9
  99.8 0.7 collective-permute-start.10
  100.5 0.7 collective-permute-start.11
  101.2 33.0 %collective-permute-start.12 = (f32[64,448]{0,1:T(8,128)S(1)}, f32[64,448]{0,1:T(8,128)S(1)}, u32[]{:S(2)}, u32[]{:S(2)}) collective-permute-start(f32[64,448]{0,1:T(8,128)S(1)} %broadcast_select_fusion.6), channel_id=1, source_target_pairs={{0,128},{16,144},{32,160},{48,176},{64,192},{80,208},{96,224},{112... | collective-permute-start | bytes 344072 | tf_op jit(solution)/shard_map/ppermute | solution.py:23

commit v2 on v1

--- a/solution.py
+++ b/solution.py
@@ -4,7 +4,7 @@
 from jax.sharding import PartitionSpec as P
 
 B = 64
-RADIX = 2
+RADIX = 4
 
 
 def tree_broadcast(x, axes, size, index_of, member, radix=RADIX):

time: 154 us -> 145 us (0.942)
  the two profiles are of different devices: /device:TPU:8 before, /device:TPU:39 now
where the time goes in v2:
time: 145 us; the launch traced here: 144 us
  waiting for transfers between devices  101 us (70%)
  other arithmetic  17.1 us (12%)
  starting transfers between devices  13.3 us (9%)
  local copies, waits for them, and re-layouts  9.16 us (6%)
  matrix products  3.07 us (2%)
    ppermute x12, waiting for transfers between devices, tree_broadcast(): got = lax.ppermute(x, axes, pairs)  101 us
    ppermute x12, starting transfers between devices, tree_broadcast(): got = lax.ppermute(x, axes, pairs)  10 us
    another operation x3, other arithmetic, shards(): factor = jnp.linalg.cholesky(corner)  6.53 us
    another operation x2, other arithmetic, shards(): lax.linalg.triangular_solve(factor, both, left_side=True, lower=True)  5.55 us
  transfers between devices with their start and end apart: 17, of which 2 were waited for; matrix products, arithmetic and copies ran while one was open for 3% of the time, Pallas kernels for 0%

profile of v2, /device:TPU:39, one launch (start us, length us, event | category | flops | bytes accessed | tf_op | source)
XLA Modules:
  0.0 143.9 jit_solution(8452854787780400079)
XLA Ops:
  0.0 1.1 slice_bitcast_fusion
  1.1 0.2 copy.12
  1.4 0.7 collective-permute-start.2
  2.0 0.7 collective-permute-start.1
  2.7 0.7 collective-permute-start
  3.5 0.2 copy.15
  3.7 0.2 copy.16
  3.9 0.2 copy.17
  4.2 1.2 select_select_fusion.1
  5.4 0.2 copy.18
  5.6 0.7 collective-permute-start.5
  6.3 1.3 collective-permute-start.4
  7.6 0.7 collective-permute-start.3
  8.3 0.2 copy.21
  8.6 37.4 %collective-permute-done.4 = f32[64,1280]{1,0:T(8,128)S(1)} collective-permute-done((f32[64,1280]{1,0:T(8,128)S(1)}, f32[64,1280]{1,0:T(8,128)S(1)}, u32[]{:S(2)}, u32[]{:S(2)}) %collective-permute-start.4) | collective-permute-done | bytes 327712 | tf_op jit(solution)/shard_map/ppermute | solution.py:23
  46.0 0.2 copy.22
  46.2 0.2 copy.23
  46.4 0.1 constant_dynamic-update-slice_fusion
  46.6 0.8 copy-done
  47.4 0.7 collective-permute-start.10
  48.1 0.7 collective-permute-start.9
  48.8 0.7 collective-permute-start.8
  49.6 0.8 slice.80
  50.4 0.7 collective-permute-start.7
  51.1 0.7 collective-permute-start.6
  51.8 0.8 add_select_fusion
  52.6 0.9 select_select_fusion.6
  53.5 0.7 collective-permute-start.13
  54.2 0.7 collective-permute-start.12
  54.8 0.7 collective-permute-start.11
  55.6 0.7 collective-permute-start.16
  56.3 1.4 collective-permute-start.15
  57.7 1.3 collective-permute-start.14
  59.0 1.9 %copy.32 = f32[1280,384]{0,1:T(8,128)S(1)} copy(f32[1280,384]{1,0:T(8,128)} %param.1) | data formatting | bytes 3932160 | tf_op args[0]
  60.9 63.1 %collective-permute-done.14 = f32[64,448]{0,1:T(8,128)} collective-permute-done((f32[64,448]{0,1:T(8,128)S(1)}, f32[64,448]{0,1:T(8,128)}, u32[]{:S(2)}, u32[]{:S(2)}) %collective-permute-start.14) | collective-permute-done | bytes 114720 | tf_op jit(solution)/shard_map/ppermute | solution.py:23
  124.0 1.0 select_select_fusion.2
  125.3 5.9 %cholesky.18 = f32[64,64]{1,0:T(8,128)S(1)} custom-call(f32[64,64]{1,0:T(8,128)S(1)} %copy.26), custom_call_target="Cholesky" | custom-call | tf_op jit(solution)/shard_map/jit(cholesky)/cholesky | solution.py:91
  131.2 0.6 compare_reduce_fusion
  131.8 0.7 select_bitcast_fusion
  132.5 4.9 %custom-call.6 = f32[1,64,64]{1,2,0:T(8,128)S(1)} custom-call(f32[1,64,64]{2,1,0:T(8,128)S(1)} %select_bitcast_fusion), custom_call_target="InvertDiagBlocksLowerTriangular" | custom-call | tf_op jit(solution)/shard_map/triangular_solve | solution.py:101
  137.4 1.1 fusion.4
  138.6 0.1 slice.90
  138.9 0.7 bitcast_select_fusion
  139.8 1.9 %fusion = f32[1280,384]{0,1:T(8,128)S(1)} fusion(f32[1280,384]{0,1:T(8,128)S(1)} %copy.32, pred[1280]{0:T(1024)(128)(4,1)S(1)} %fusion.8, f32[64,1216]{1,0:T(8,128)S(1)} %slice.90, f32[64,64]{1,0:T(8,128)S(1)} %copy.28, f32[64,320]{1,0:T(8,128)S(1)} %slice.92, f32[64,64]{1,0:T(8,128)S(1)} %copy.30), kind=kOutput, calls=%fused_computation.1 | convolution fusion | flops 378576896 | bytes 4359424 | tf_op jit(solution)/shard_map/dot_general | solution.py:110
  141.7 0.2 slice_select_fusion
  141.9 0.1 slice.94
  142.0 0.1 pad_maximum_fusion
  142.1 1.8 %copy.33 = f32[1280,384]{1,0:T(8,128)} copy(f32[1280,384]{0,1:T(8,128)S(1)} %pad_maximum_fusion) | data formatting | bytes 3932160 | tf_op jit(solution)/shard_map/concatenate | solution.py:121
  (37 shorter events, 0.8 us)
Async XLA Ops:
  1.4 2.1 %collective-permute-start.2 = (f32[64,1280]{1,0:T(8,128)S(1)}, f32[64,1280]{1,0:T(8,128)S(1)}, u32[]{:S(2)}, u32[]{:S(2)}) collective-permute-start(f32[64,1280]{1,0:T(8,128)S(1)} %copy.12), channel_id=1, source_target_pairs={{0,1},{16,17},{32,33},{48,49},{64,65},{80,81},{96,97},{112,113},{1... | collective-permute-start | bytes 983048 | tf_op jit(solution)/shard_map/ppermute | solution.py:23
  2.0 1.6 %collective-permute-start.1 = (f32[64,1280]{1,0:T(8,128)S(1)}, f32[64,1280]{1,0:T(8,128)S(1)}, u32[]{:S(2)}, u32[]{:S(2)}) collective-permute-start(f32[64,1280]{1,0:T(8,128)S(1)} %copy.12), channel_id=1, source_target_pairs={{0,2},{16,18},{32,34},{48,50},{64,66},{80,82},{96,98},{112,114},{1... | collective-permute-start | bytes 983048 | tf_op jit(solution)/shard_map/ppermute | solution.py:23
  2.7 1.2 collective-permute-start
  5.6 2.7 %collective-permute-start.5 = (f32[64,1280]{1,0:T(8,128)S(1)}, f32[64,1280]{1,0:T(8,128)S(1)}, u32[]{:S(2)}, u32[]{:S(2)}) collective-permute-start(f32[64,1280]{1,0:T(8,128)S(1)} %copy.18), channel_id=1, source_target_pairs={{0,4},{1,5},{2,6},{3,7},{16,20},{17,21},{18,22},{19,23},{32,36},{3... | collective-permute-start | bytes 983048 | tf_op jit(solution)/shard_map/ppermute | solution.py:23
  6.3 39.7 %collective-permute-start.4 = (f32[64,1280]{1,0:T(8,128)S(1)}, f32[64,1280]{1,0:T(8,128)S(1)}, u32[]{:S(2)}, u32[]{:S(2)}) collective-permute-start(f32[64,1280]{1,0:T(8,128)S(1)} %copy.18), channel_id=1, source_target_pairs={{0,8},{1,9},{2,10},{3,11},{16,24},{17,25},{18,26},{19,27},{32,40},... | collective-permute-start | bytes 983048 | tf_op jit(solution)/shard_map/ppermute | solution.py:23
  7.6 38.6 %collective-permute-start.3 = (f32[64,1280]{1,0:T(8,128)S(1)}, f32[64,1280]{1,0:T(8,128)S(1)}, u32[]{:S(2)}, u32[]{:S(2)}) collective-permute-start(f32[64,1280]{1,0:T(8,128)S(1)} %copy.18), channel_id=1, source_target_pairs={{0,12},{1,13},{2,14},{3,15},{16,28},{17,29},{18,30},{19,31},{32,44... | collective-permute-start | bytes 983048 | tf_op jit(solution)/shard_map/ppermute | solution.py:23
  46.6 0.8 copy-start
  47.4 4.3 %collective-permute-start.10 = (f32[64,64]{0,1:T(8,128)S(1)}, f32[64,64]{0,1:T(8,128)S(1)}, u32[]{:S(2)}, u32[]{:S(2)}) collective-permute-start(f32[64,64]{0,1:T(8,128)S(1)} %slice.81), channel_id=1, source_target_pairs={{0,512},{1,529},{2,546},{3,563},{4,580},{5,597},{6,614},{7,631},{8... | collective-permute-start | bytes 49160 | tf_op jit(solution)/shard_map/ppermute | solution.py:68
  48.1 3.7 %collective-permute-start.9 = (f32[64,64]{0,1:T(8,128)S(1)}, f32[64,64]{0,1:T(8,128)S(1)}, u32[]{:S(2)}, u32[]{:S(2)}) collective-permute-start(f32[64,64]{0,1:T(8,128)S(1)} %slice.81), channel_id=1, source_target_pairs={{0,256},{1,273},{2,290},{3,307},{4,324},{5,341},{6,358},{7,375},{8... | collective-permute-start | bytes 49160 | tf_op jit(solution)/shard_map/ppermute | solution.py:68
  48.8 3.0 %collective-permute-start.8 = (f32[64,64]{0,1:T(8,128)S(1)}, f32[64,64]{0,1:T(8,128)S(1)}, u32[]{:S(2)}, u32[]{:S(2)}) collective-permute-start(f32[64,64]{0,1:T(8,128)S(1)} %slice.81), channel_id=1, source_target_pairs={{1,17},{2,34},{3,51},{4,68},{5,85},{6,102},{7,119},{8,136},{9,153}... | collective-permute-start | bytes 49160 | tf_op jit(solution)/shard_map/ppermute | solution.py:68
  50.4 2.1 %collective-permute-start.7 = (f32[64,128]{0,1:T(8,128)S(1)}, f32[64,128]{0,1:T(8,128)S(1)}, u32[]{:S(2)}, u32[]{:S(2)}) collective-permute-start(f32[64,128]{0,1:T(8,128)S(1)} %slice.80), channel_id=1, source_target_pairs={{0,256},{256,512},{512,0},{17,273},{273,529},{529,17},{34,290},{29... | collective-permute-start | bytes 98312 | tf_op jit(solution)/shard_map/ppermute | solution.py:59
  51.1 1.5 %collective-permute-start.6 = (f32[64,128]{0,1:T(8,128)S(1)}, f32[64,128]{0,1:T(8,128)S(1)}, u32[]{:S(2)}, u32[]{:S(2)}) collective-permute-start(f32[64,128]{0,1:T(8,128)S(1)} %slice.80), channel_id=1, source_target_pairs={{0,512},{256,0},{512,256},{17,529},{273,17},{529,273},{34,546},{29... | collective-permute-start | bytes 98312 | tf_op jit(solution)/shard_map/ppermute | solution.py:59
  53.5 2.1 %collective-permute-start.13 = (f32[64,448]{0,1:T(8,128)S(1)}, f32[64,448]{0,1:T(8,128)S(1)}, u32[]{:S(2)}, u32[]{:S(2)}) collective-permute-start(f32[64,448]{0,1:T(8,128)S(1)} %maximum_select_fusion), channel_id=1, source_target_pairs={{0,16},{256,272},{512,528},{17,33},{273,289},{529,545},{34,50},{29... | collective-permute-start | bytes 344072 | tf_op jit(solution)/shard_map/ppermute | solution.py:23
  54.2 1.4 collective-permute-start.12
  54.8 0.7 collective-permute-start.11
  55.6 5.3 %collective-permute-start.16 = (f32[64,448]{0,1:T(8,128)S(1)}, f32[64,448]{0,1:T(8,128)S(1)}, u32[]{:S(2)}, u32[]{:S(2)}) collective-permute-start(f32[64,448]{0,1:T(8,128)S(1)} %select_select_fusion.3), channel_id=1, source_target_pairs={{0,64},{16,80},{32,96},{48,112},{256,320},{272,336},{288,352},{304... | collective-permute-start | bytes 344072 | tf_op jit(solution)/shard_map/ppermute | solution.py:23
  56.3 4.6 %collective-permute-start.15 = (f32[64,448]{0,1:T(8,128)S(1)}, f32[64,448]{0,1:T(8,128)}, u32[]{:S(2)}, u32[]{:S(2)}) collective-permute-start(f32[64,448]{0,1:T(8,128)S(1)} %select_select_fusion.3), channel_id=1, source_target_pairs={{0,128},{16,144},{32,160},{48,176},{256,384},{272,400},{288,416},{... | collective-permute-start | bytes 344072 | tf_op jit(solution)/shard_map/ppermute | solution.py:23
  57.7 66.3 %collective-permute-start.14 = (f32[64,448]{0,1:T(8,128)S(1)}, f32[64,448]{0,1:T(8,128)}, u32[]{:S(2)}, u32[]{:S(2)}) collective-permute-start(f32[64,448]{0,1:T(8,128)S(1)} %select_select_fusion.3), channel_id=1, source_target_pairs={{0,192},{16,208},{32,224},{48,240},{256,448},{272,464},{288,480},{... | collective-permute-start | bytes 344072 | tf_op jit(solution)/shard_map/ppermute | solution.py:23

commit v3 on v1

--- a/solution.py
+++ b/solution.py
@@ -38,13 +38,24 @@
     window_cols = cols_dev * n_col // n_row
 
     panel_t = matrix[:, :B].T
+    head = panel_t[:, :window_cols]
+
+    def col0_group(_):
+        return [lambda m: m * n_col]
+
+    corner_t = tree_broadcast(panel_t[:, :B], ("row", "col"), n_row, col0_group, row_id, radix=4)
 
     def col_groups(_):
         return [lambda m, r=r: r * n_col + m for r in range(n_row)]
 
-    panel_t = tree_broadcast(panel_t, ("row", "col"), n_col, col_groups, col_id)
+    with_corner = jnp.concatenate([panel_t, corner_t], axis=1)
+    with_corner = tree_broadcast(with_corner, ("row", "col"), n_col, col_groups, col_id)
+    panel_t = with_corner[:, :rows_dev]
+    corner_t = with_corner[:, rows_dev:]
 
-    head = panel_t[:, :window_cols]
+    pairs = [(r * n_col, r * n_col + r % n_col) for r in range(n_row) if r % n_col]
+    got = lax.ppermute(head, ("row", "col"), pairs)
+    head = jnp.where(col_id == 0, head, got)
     rel = (row_id - col_id) % n_row
     my_j = rel // n_col
     is_src = rel % n_col == 0
@@ -57,23 +68,13 @@
                 b = q + n_col * ((j + c) % n_src)
                 pairs.append((a * n_col + q, b * n_col + q))
         pieces.append(lax.ppermute(head, ("row", "col"), pairs))
-    corner_t = panel_t[:, :B]
-    got_corner = jnp.zeros_like(corner_t)
-    for j in range(n_src):
-        pairs = []
-        for q in range(n_col):
-            b = q + n_col * j
-            if b != 0:
-                pairs.append((0 * n_col + q, b * n_col + q))
-        got_corner = got_corner + lax.ppermute(corner_t, ("row", "col"), pairs)
-    corner_t = jnp.where(row_id == 0, corner_t, got_corner)
     ordered = []
     for jj in range(n_src):
         pick = pieces[0]
         for c in range(1, n_src):
             pick = jnp.where((my_j - jj) % n_src == c, pieces[c], pick)
         ordered.append(pick)
-    packet = jnp.concatenate(ordered + [corner_t], axis=1)
+    packet = jnp.concatenate(ordered, axis=1)
     packet = jnp.where(is_src, packet, jnp.zeros_like(packet))
 
     def row_groups(_):
@@ -86,7 +87,6 @@
 
     packet = tree_broadcast(packet, ("row", "col"), n_col, row_groups, rel % n_col)
 
-    corner_t = packet[:, n_src * window_cols:]
     corner = (corner_t + corner_t.T) / 2.0
     factor = jnp.linalg.cholesky(corner)
 

time: 154 us -> 136 us (0.88)
  the two profiles are of different devices: /device:TPU:8 before, /device:TPU:104 now
where the time goes in v3:
time: 136 us; the launch traced here: 135 us
  waiting for transfers between devices  83.7 us (62%)
  other arithmetic  17.1 us (13%)
  local copies, waits for them, and re-layouts  16 us (12%)
  starting transfers between devices  14.6 us (11%)
  matrix products  3.06 us (2%)
    ppermute x16, waiting for transfers between devices, tree_broadcast(): got = lax.ppermute(x, axes, pairs)  83.7 us
    ppermute x16, starting transfers between devices, tree_broadcast(): got = lax.ppermute(x, axes, pairs)  12.6 us
    another operation x3, other arithmetic, shards(): factor = jnp.linalg.cholesky(corner)  6.52 us
    unnamed x9, local copies, waits for them, and re-layouts  5.9 us
    another operation x2, other arithmetic, shards(): lax.linalg.triangular_solve(factor, both, left_side=True, lower=True)  5.55 us
    select_n x11, other arithmetic, tree_broadcast(): fresh = jnp.where(take, got, fresh)  3.16 us
  transfers between devices with their start and end apart: 19, of which 2 were waited for; matrix products, arithmetic and copies ran while one was open for 6% of the time, Pallas kernels for 0%

profile of v3, /device:TPU:104, one launch (start us, length us, event | category | flops | bytes accessed | tf_op | source)
XLA Modules:
  0.0 135.2 jit_solution(12874921549067248172)
XLA Ops:
  0.0 1.1 slice_bitcast_fusion
  1.1 0.7 collective-permute-start.2
  1.8 0.7 collective-permute-start.1
  2.5 0.7 collective-permute-start
  3.2 0.7 collective-permute-start.5
  3.9 0.7 collective-permute-start.4
  4.6 0.7 collective-permute-start.3
  5.3 0.7 collective-permute-start.7
  6.0 0.7 collective-permute-start.6
  6.7 0.7 collective-permute-start.12
  7.5 0.2 copy.11
  7.7 0.7 collective-permute-start.8
  8.4 0.7 collective-permute-start.14
  9.1 0.7 collective-permute-start.13
  9.9 0.2 copy.12
  10.3 0.2 copy.13
  10.5 0.7 collective-permute-start.9
  11.2 0.7 collective-permute-start.15
  12.0 0.7 collective-permute-start.16
  13.0 1.0 copy.15
  14.0 0.7 collective-permute-start.10
  14.7 1.3 collective-permute-start.17
  16.1 1.9 %copy.26 = f32[1280,384]{0,1:T(8,128)S(1)} copy(f32[1280,384]{1,0:T(8,128)} %param.1) | data formatting | bytes 3932160 | tf_op args[0]
  18.0 1.3 collective-permute-start.18
  19.3 1.1 copy.16
  20.5 1.0 copy.17
  21.5 1.3 collective-permute-start.11
  22.8 48.3 %collective-permute-done.18 = f32[64,384]{0,1:T(8,128)} collective-permute-done((f32[64,384]{0,1:T(8,128)S(1)}, f32[64,384]{0,1:T(8,128)}, u32[]{:S(2)}, u32[]{:S(2)}) %collective-permute-start.18) | collective-permute-done | bytes 98336 | tf_op jit(solution)/shard_map/ppermute | solution.py:23
  71.1 1.6 %broadcast_select_fusion.7 = f32[64,384]{0,1:T(8,128)} fusion(f32[64,384]{0,1:T(8,128)} %collective-permute-done.18, f32[64,384]{0,1:T(8,128)S(1)} %broadcast_select_fusion.6, pred[]{:T(512)S(6)} %and.99), kind=kLoop, calls=%fused_computation.19 | loop fusion | flops 24576 | bytes 294913 | tf_op jit(solution)/shard_map/jit(_where)/select_n | solution.py:25
  72.8 35.3 %collective-permute-done.11 = f32[64,1344]{1,0:T(8,128)S(1)} collective-permute-done((f32[64,1344]{1,0:T(8,128)}, f32[64,1344]{1,0:T(8,128)S(1)}, u32[]{:S(2)}, u32[]{:S(2)}) %collective-permute-start.11) | collective-permute-done | bytes 344096 | tf_op jit(solution)/shard_map/ppermute | solution.py:23
  108.1 1.1 copy.18
  109.2 1.2 broadcast_select_fusion.3
  110.5 0.7 copy.19
  111.2 0.8 fusion.7
  112.0 5.8 %cholesky.18 = f32[64,64]{1,0:T(8,128)S(1)} custom-call(f32[64,64]{1,0:T(8,128)S(1)} %fusion.6), custom_call_target="Cholesky" | custom-call | tf_op jit(solution)/shard_map/jit(cholesky)/cholesky | solution.py:91
  117.9 0.6 compare_reduce_fusion
  118.5 0.7 select_bitcast_fusion
  119.2 4.9 %custom-call.6 = f32[1,64,64]{1,2,0:T(8,128)S(1)} custom-call(f32[1,64,64]{2,1,0:T(8,128)S(1)} %select_bitcast_fusion), custom_call_target="InvertDiagBlocksLowerTriangular" | custom-call | tf_op jit(solution)/shard_map/triangular_solve | solution.py:101
  124.1 0.8 slice_dynamic-update-slice_fusion.6
  124.9 0.8 slice_dynamic-update-slice_fusion.5
  125.6 0.8 slice_dynamic-update-slice_fusion.4
  126.4 0.8 slice_dynamic-update-slice_fusion.3
  127.2 0.8 slice_dynamic-update-slice_fusion.2
  127.9 0.8 slice_dynamic-update-slice_fusion.1
  128.7 1.1 fusion.4
  130.2 0.7 bitcast_select_fusion
  131.0 1.9 %fusion = f32[1280,384]{0,1:T(8,128)S(1)} fusion(f32[1280,384]{0,1:T(8,128)S(1)} %copy.26, pred[1280]{0:T(1024)(128)(4,1)S(1)} %fusion.8, f32[64,1216]{1,0:T(8,128)S(1)} %slice.95, f32[64,64]{1,0:T(8,128)S(1)} %copy.22, f32[64,320]{1,0:T(8,128)S(1)} %slice.97, f32[64,64]{1,0:T(8,128)S(1)} %copy.24), kind=kOutput, calls=%fused_computation.1 | convolution fusion | flops 378576896 | bytes 4359424 | tf_op jit(solution)/shard_map/dot_general | solution.py:110
  133.4 1.8 %copy.27 = f32[1280,384]{1,0:T(8,128)} copy(f32[1280,384]{0,1:T(8,128)S(1)} %pad_maximum_fusion) | data formatting | bytes 3932160 | tf_op jit(solution)/shard_map/concatenate | solution.py:121
  (49 shorter events, 1.8 us)
Async XLA Ops:
  1.1 2.0 %collective-permute-start.2 = (f32[64,64]{0,1:T(8,128)S(1)}, f32[64,64]{0,1:T(8,128)S(1)}, u32[]{:S(2)}, u32[]{:S(2)}) collective-permute-start(f32[64,64]{0,1:T(8,128)S(1)} %slice.84), channel_id=1, source_target_pairs={{0,16}} | collective-permute-start | bytes 49160 | tf_op jit(solution)/shard_map/ppermute | solution.py:23
  1.8 1.4 %collective-permute-start.1 = (f32[64,64]{0,1:T(8,128)S(1)}, f32[64,64]{0,1:T(8,128)S(1)}, u32[]{:S(2)}, u32[]{:S(2)}) collective-permute-start(f32[64,64]{0,1:T(8,128)S(1)} %slice.84), channel_id=1, source_target_pairs={{0,32}} | collective-permute-start | bytes 49160 | tf_op jit(solution)/shard_map/ppermute | solution.py:23
  2.5 0.7 collective-permute-start
  3.2 2.0 %collective-permute-start.5 = (f32[64,64]{0,1:T(8,128)S(1)}, f32[64,64]{0,1:T(8,128)S(1)}, u32[]{:S(2)}, u32[]{:S(2)}) collective-permute-start(f32[64,64]{0,1:T(8,128)S(1)} %select_select_fusion.6), channel_id=1, source_target_pairs={{0,64},{16,80},{32,96},{48,112}} | collective-permute-start | bytes 49160 | tf_op jit(solution)/shard_map/ppermute | solution.py:23
  3.9 1.4 %collective-permute-start.4 = (f32[64,64]{0,1:T(8,128)S(1)}, f32[64,64]{0,1:T(8,128)S(1)}, u32[]{:S(2)}, u32[]{:S(2)}) collective-permute-start(f32[64,64]{0,1:T(8,128)S(1)} %select_select_fusion.6), channel_id=1, source_target_pairs={{0,128},{16,144},{32,160},{48,176}} | collective-permute-start | bytes 49160 | tf_op jit(solution)/shard_map/ppermute | solution.py:23
  4.6 0.7 collective-permute-start.3
  5.3 2.1 %collective-permute-start.7 = (f32[64,64]{0,1:T(8,128)S(1)}, f32[64,64]{0,1:T(8,128)S(1)}, u32[]{:S(2)}, u32[]{:S(2)}) collective-permute-start(f32[64,64]{0,1:T(8,128)S(1)} %select_select_fusion.5), channel_id=1, source_target_pairs={{0,256},{16,272},{32,288},{48,304},{64,320},{80,336},{96,352},{112... | collective-permute-start | bytes 49160 | tf_op jit(solution)/shard_map/ppermute | solution.py:23
  6.0 1.4 %collective-permute-start.6 = (f32[64,64]{0,1:T(8,128)S(1)}, f32[64,64]{0,1:T(8,128)S(1)}, u32[]{:S(2)}, u32[]{:S(2)}) collective-permute-start(f32[64,64]{0,1:T(8,128)S(1)} %select_select_fusion.5), channel_id=1, source_target_pairs={{0,512},{16,528},{32,544},{48,560},{64,576},{80,592},{96,608},{112... | collective-permute-start | bytes 49160 | tf_op jit(solution)/shard_map/ppermute | solution.py:23
  6.7 1.7 %collective-permute-start.12 = (f32[64,128]{0,1:T(8,128)S(1)}, f32[64,128]{0,1:T(8,128)S(1)}, u32[]{:S(2)}, u32[]{:S(2)}) collective-permute-start(f32[64,128]{0,1:T(8,128)S(1)} %slice.87), channel_id=1, source_target_pairs={{16,17},{32,34},{48,51},{64,68},{80,85},{96,102},{112,119},{128,13... | collective-permute-start | bytes 98312 | tf_op jit(solution)/shard_map/ppermute | solution.py:57
  7.7 2.2 %collective-permute-start.8 = (f32[64,1344]{1,0:T(8,128)S(1)}, f32[64,1344]{1,0:T(8,128)S(1)}, u32[]{:S(2)}, u32[]{:S(2)}) collective-permute-start(f32[64,1344]{1,0:T(8,128)S(1)} %copy.11), channel_id=1, source_target_pairs={{0,1},{16,17},{32,33},{48,49},{64,65},{80,81},{96,97},{112,113},{1... | collective-permute-start | bytes 1032200 | tf_op jit(solution)/shard_map/ppermute | solution.py:23
  8.4 1.5 %collective-permute-start.14 = (f32[64,128]{0,1:T(8,128)S(1)}, f32[64,128]{0,1:T(8,128)S(1)}, u32[]{:S(2)}, u32[]{:S(2)}) collective-permute-start(f32[64,128]{0,1:T(8,128)S(1)} %broadcast_select_fusion.8), channel_id=1, source_target_pairs={{0,256},{256,512},{512,0},{17,273},{273,529},{529,17},{34,290},{29... | collective-permute-start | bytes 98312 | tf_op jit(solution)/shard_map/ppermute | solution.py:70
  9.1 0.8 collective-permute-start.13
  10.5 2.1 %collective-permute-start.9 = (f32[64,1344]{1,0:T(8,128)S(1)}, f32[64,1344]{1,0:T(8,128)S(1)}, u32[]{:S(2)}, u32[]{:S(2)}) collective-permute-start(f32[64,1344]{1,0:T(8,128)S(1)} %copy.13), channel_id=1, source_target_pairs={{0,2},{1,3},{16,18},{17,19},{32,34},{33,35},{48,50},{49,51},{64,66... | collective-permute-start | bytes 1032200 | tf_op jit(solution)/shard_map/ppermute | solution.py:23
  11.2 0.7 collective-permute-start.15
  12.0 2.7 %collective-permute-start.16 = (f32[64,384]{0,1:T(8,128)S(1)}, f32[64,384]{0,1:T(8,128)S(1)}, u32[]{:S(2)}, u32[]{:S(2)}) collective-permute-start(f32[64,384]{0,1:T(8,128)S(1)} %broadcast_select_fusion.4), channel_id=1, source_target_pairs={{0,32},{16,48},{256,288},{272,304},{512,544},{528,560},{17,49},{33... | collective-permute-start | bytes 294920 | tf_op jit(solution)/shard_map/ppermute | solution.py:23
  14.0 5.3 %collective-permute-start.10 = (f32[64,1344]{1,0:T(8,128)}, f32[64,1344]{1,0:T(8,128)S(1)}, u32[]{:S(2)}, u32[]{:S(2)}) collective-permute-start(f32[64,1344]{1,0:T(8,128)} %copy.15), channel_id=1, source_target_pairs={{0,4},{1,5},{2,6},{3,7},{16,20},{17,21},{18,22},{19,23},{32,36},{3... | collective-permute-start | bytes 1032200 | tf_op jit(solution)/shard_map/ppermute | solution.py:23
  14.7 3.3 %collective-permute-start.17 = (f32[64,384]{0,1:T(8,128)S(1)}, f32[64,384]{0,1:T(8,128)}, u32[]{:S(2)}, u32[]{:S(2)}) collective-permute-start(f32[64,384]{0,1:T(8,128)S(1)} %broadcast_select_fusion.5), channel_id=1, source_target_pairs={{0,64},{16,80},{32,96},{48,112},{256,320},{272,336},{288,352},{304... | collective-permute-start | bytes 294920 | tf_op jit(solution)/shard_map/ppermute | solution.py:23
  18.0 53.1 %collective-permute-start.18 = (f32[64,384]{0,1:T(8,128)S(1)}, f32[64,384]{0,1:T(8,128)}, u32[]{:S(2)}, u32[]{:S(2)}) collective-permute-start(f32[64,384]{0,1:T(8,128)S(1)} %broadcast_select_fusion.6), channel_id=1, source_target_pairs={{0,128},{16,144},{32,160},{48,176},{64,192},{80,208},{96,224},{112... | collective-permute-start | bytes 294920 | tf_op jit(solution)/shard_map/ppermute | solution.py:23
  21.5 86.6 %collective-permute-start.11 = (f32[64,1344]{1,0:T(8,128)}, f32[64,1344]{1,0:T(8,128)S(1)}, u32[]{:S(2)}, u32[]{:S(2)}) collective-permute-start(f32[64,1344]{1,0:T(8,128)} %copy.17), channel_id=1, source_target_pairs={{0,8},{1,9},{2,10},{3,11},{4,12},{5,13},{6,14},{7,15},{16,24},{17,... | collective-permute-start | bytes 1032200 | tf_op jit(solution)/shard_map/ppermute | solution.py:23

commit v4 on v3

--- a/solution.py
+++ b/solution.py
@@ -10,6 +10,13 @@
 def tree_broadcast(x, axes, size, index_of, member, radix=RADIX):
     have = 1
     while have < size:
+        x = tree_round(x, axes, size, index_of, member, have, radix)
+        have *= radix
+    return x
+
+
+def tree_round(x, axes, size, index_of, member, have, radix=RADIX):
+    if True:
         fresh = x
         for c in range(1, radix):
             lo = c * have
@@ -23,9 +30,7 @@
             got = lax.ppermute(x, axes, pairs)
             take = jnp.logical_and(member >= lo, member < lo + have)
             fresh = jnp.where(take, got, fresh)
-        x = fresh
-        have *= radix
-    return x
+    return fresh
 
 
 def shards(matrix):
@@ -40,21 +45,14 @@
     panel_t = matrix[:, :B].T
     head = panel_t[:, :window_cols]
 
-    def col0_group(_):
-        return [lambda m: m * n_col]
-
-    corner_t = tree_broadcast(panel_t[:, :B], ("row", "col"), n_row, col0_group, row_id, radix=4)
-
     def col_groups(_):
         return [lambda m, r=r: r * n_col + m for r in range(n_row)]
 
-    with_corner = jnp.concatenate([panel_t, corner_t], axis=1)
-    with_corner = tree_broadcast(with_corner, ("row", "col"), n_col, col_groups, col_id)
-    panel_t = with_corner[:, :rows_dev]
-    corner_t = with_corner[:, rows_dev:]
+    full_t = tree_round(panel_t, ("row", "col"), n_col, col_groups, col_id, 1)
+    full_t, head, corner_in = lax.optimization_barrier((full_t, head, panel_t[:, :B]))
 
-    pairs = [(r * n_col, r * n_col + r % n_col) for r in range(n_row) if r % n_col]
-    got = lax.ppermute(head, ("row", "col"), pairs)
+    to_owner = [(r * n_col, r * n_col + r % n_col) for r in range(n_row) if r % n_col]
+    got = lax.ppermute(head, ("row", "col"), to_owner)
     head = jnp.where(col_id == 0, head, got)
     rel = (row_id - col_id) % n_row
     my_j = rel // n_col
@@ -74,7 +72,29 @@
         for c in range(1, n_src):
             pick = jnp.where((my_j - jj) % n_src == c, pieces[c], pick)
         ordered.append(pick)
-    packet = jnp.concatenate(ordered, axis=1)
+
+    def col0_group(_):
+        return [lambda m: m * n_col]
+
+    corner_t = tree_broadcast(corner_in, ("row", "col"), n_row, col0_group, row_id, radix=4)
+    full_t = tree_round(full_t, ("row", "col"), n_col, col_groups, col_id, 2)
+    full_t, corner_t = lax.optimization_barrier((full_t, corner_t))
+    corner = (corner_t + corner_t.T) / 2.0
+    factor = jnp.linalg.cholesky(corner)
+    inverse = lax.linalg.triangular_solve(
+        factor, jnp.eye(B, dtype=factor.dtype), left_side=True, lower=True
+    )
+    fpack = jnp.concatenate([factor.T, inverse], axis=1)
+    full_t = tree_round(full_t, ("row", "col"), n_col, col_groups, col_id, 4)
+    full_t, fpack = lax.optimization_barrier((full_t, fpack))
+    have = 8
+    while have < n_col:
+        full_t = tree_round(full_t, ("row", "col"), n_col, col_groups, col_id, have)
+        have *= 2
+    got = lax.ppermute(fpack, ("row", "col"), to_owner)
+    fpack = jnp.where(col_id == 0, fpack, got)
+
+    packet = jnp.concatenate(ordered + [fpack], axis=1)
     packet = jnp.where(is_src, packet, jnp.zeros_like(packet))
 
     def row_groups(_):
@@ -86,9 +106,8 @@
         return out
 
     packet = tree_broadcast(packet, ("row", "col"), n_col, row_groups, rel % n_col)
-
-    corner = (corner_t + corner_t.T) / 2.0
-    factor = jnp.linalg.cholesky(corner)
+    factor_t = packet[:, n_src * window_cols: n_src * window_cols + B]
+    inverse = packet[:, n_src * window_cols + B: n_src * window_cols + 2 * B]
 
     tiles = []
     for k in range(cols_dev // B):
@@ -97,15 +116,17 @@
         tiles.append(packet[:, j * window_cols + lt * B: j * window_cols + (lt + 1) * B])
     window_t = jnp.concatenate(tiles, axis=1)
 
-    both = jnp.concatenate([panel_t, window_t], axis=1)
-    solved = lax.linalg.triangular_solve(factor, both, left_side=True, lower=True)
-    lower_t = solved[:, :rows_dev]
+    def apply(x):
+        return lax.dot(inverse, x, precision=lax.Precision.HIGHEST,
+                       preferred_element_type=jnp.float32)
+
+    lower_t = apply(full_t)
     lower_t = jnp.concatenate(
-        [jnp.where(row_id == 0, factor.T, lower_t[:, :B]), lower_t[:, B:]], axis=1
+        [jnp.where(row_id == 0, factor_t, lower_t[:, :B]), lower_t[:, B:]], axis=1
     )
-    col_t = solved[:, rows_dev:]
+    col_t = apply(window_t)
     col_t = jnp.concatenate(
-        [jnp.where(col_id == 0, factor.T, col_t[:, :B]), col_t[:, B:]], axis=1
+        [jnp.where(col_id == 0, factor_t, col_t[:, :B]), col_t[:, B:]], axis=1
     )
     change = lax.dot_general(
         lower_t,

time: 136 us -> 143 us (1.051)
  the two profiles are of different devices: /device:TPU:104 before, /device:TPU:412 now
where the time goes in v4:
time: 143 us
  waiting for transfers between devices  96 us (67%)
  starting transfers between devices  16 us (11%)
  other arithmetic  14.9 us (10%)
  local copies, waits for them, and re-layouts  10.5 us (7%)
  matrix products  4.29 us (3%)
    ppermute x16, waiting for transfers between devices, tree_round(): got = lax.ppermute(x, axes, pairs)  96 us
    ppermute x16, starting transfers between devices, tree_round(): got = lax.ppermute(x, axes, pairs)  13.3 us
    another operation x3, other arithmetic, shards(): factor = jnp.linalg.cholesky(corner)  6.53 us
    another operation x1, other arithmetic, shards(): lax.linalg.triangular_solve(factor, jnp.eye(B, dtype=factor.dtype), left_...  4.9 us
  transfers between devices with their start and end apart: 20, of which 3 were waited for; matrix products, arithmetic and copies ran while one was open for 12% of the time, Pallas kernels for 0%

profile of v4, /device:TPU:412, one launch (start us, length us, event | category | flops | bytes accessed | tf_op | source)
XLA Modules:
  0.0 142.6 jit_solution(8741003682833222926)
XLA Ops:
  0.0 1.1 slice_bitcast_fusion
  1.1 0.2 copy.13
  1.4 0.7 collective-permute-start
  2.1 0.2 copy.14
  2.3 1.2 broadcast_select_fusion.2
  3.5 0.7 collective-permute-start.7
  4.2 0.7 collective-permute-start.6
  4.8 0.7 collective-permute-start.5
  5.6 0.7 collective-permute-start.10
  6.3 0.7 collective-permute-start.9
  6.9 0.7 collective-permute-start.8
  7.7 0.7 collective-permute-start.1
  8.4 0.2 copy.15
  8.6 0.7 collective-permute-start.4
  9.4 0.7 collective-permute-start.12
  10.1 0.7 collective-permute-start.11
  10.7 0.7 collective-permute-start.3
  11.4 0.7 collective-permute-start.2
  12.1 0.2 copy.16
  12.7 5.9 %cholesky.20 = f32[64,64]{1,0:T(8,128)S(1)} custom-call(f32[64,64]{1,0:T(8,128)S(1)} %copy.21), custom_call_target="Cholesky" | custom-call | tf_op jit(solution)/shard_map/jit(cholesky)/cholesky | solution.py:83
  18.6 0.6 compare_reduce_fusion
  19.3 0.7 fusion.14
  19.9 4.9 %custom-call.6 = f32[1,64,64]{1,2,0:T(8,128)S(1)} custom-call(f32[1,64,64]{2,1,0:T(8,128)S(1)} %get-tuple-element.25), custom_call_target="InvertDiagBlocksLowerTriangular" | custom-call | tf_op jit(solution)/shard_map/triangular_solve | solution.py:84
  24.8 0.2 copy.17
  25.1 1.3 collective-permute-start.13
  26.4 0.2 fusion.7
  26.6 31.5 %collective-permute-done.13 = f32[64,1280]{1,0:T(8,128)S(1)} collective-permute-done((f32[64,1280]{1,0:T(8,128)S(1)}, f32[64,1280]{1,0:T(8,128)S(1)}, u32[]{:S(2)}, u32[]{:S(2)}) %collective-permute-start.13) | collective-permute-done | bytes 327712 | tf_op jit(solution)/shard_map/ppermute | solution.py:30
  58.1 0.2 copy.18
  58.5 0.7 collective-permute-start.14
  59.2 0.7 collective-permute-start.15
  60.0 0.7 collective-permute-start.16
  60.7 0.7 collective-permute-start.17
  61.4 0.2 copy.23
  61.6 2.0 %collective-permute-start.19 = (f32[64,1280]{1,0:T(8,128)S(1)}, f32[64,1280]{1,0:T(8,128)}, u32[]{:S(2)}, u32[]{:S(2)}) collective-permute-start(f32[64,1280]{1,0:T(8,128)S(1)} %copy.23), channel_id=1, source_target_pairs={{0,8},{1,9},{2,10},{3,11},{4,12},{5,13},{6,14},{7,15},{16,24},{17,... | collective-permute-start | bytes 983048 | tf_op jit(solution)/shard_map/ppermute | solution.py:30
  63.7 1.3 collective-permute-start.18
  65.0 1.9 %copy.30 = f32[1280,384]{0,1:T(8,128)S(1)} copy(f32[1280,384]{1,0:T(8,128)} %param.1) | data formatting | bytes 3932160 | tf_op args[0]
  67.0 1.8 %collective-permute-done.19 = f32[64,1280]{1,0:T(8,128)} collective-permute-done((f32[64,1280]{1,0:T(8,128)S(1)}, f32[64,1280]{1,0:T(8,128)}, u32[]{:S(2)}, u32[]{:S(2)}) %collective-permute-start.19) | collective-permute-done | bytes 327712 | tf_op jit(solution)/shard_map/ppermute | solution.py:30
  68.7 1.2 copy.24
  69.9 62.7 %collective-permute-done.18 = f32[64,512]{0,1:T(8,128)} collective-permute-done((f32[64,512]{0,1:T(8,128)S(1)}, f32[64,512]{0,1:T(8,128)}, u32[]{:S(2)}, u32[]{:S(2)}) %collective-permute-start.18) | collective-permute-done | bytes 131104 | tf_op jit(solution)/shard_map/ppermute | solution.py:30
  132.6 1.0 broadcast_select_fusion.6
  133.7 0.4 fusion.11
  134.1 0.6 slice.90
  134.7 0.7 slice.91
  135.5 0.8 fusion.1
  136.4 0.8 copy.34
  137.5 2.8 %fusion = f32[1280,384]{0,1:T(8,128)S(1)} fusion(f32[1280,384]{0,1:T(8,128)S(1)} %copy.30, pred[1280]{0:T(1024)(128)(4,1)S(1)} %fusion.15, f32[64,1216]{1,0:T(8,128)S(1)} %slice.83, f32[64,64]{1,0:T(8,128)S(1)} %copy.26, f32[64,320]{1,0:T(8,128)} %slice.91, f32[64,64]{1,0:T(8,128)S(1)} %copy.28), kind=kOutput, calls=%fused_computation.1 | convolution fusion | flops 378576896 | bytes 4359424 | tf_op jit(solution)/shard_map/dot_general | solution.py:131
  140.4 0.2 slice_select_fusion
  140.8 1.8 %copy.31 = f32[1280,384]{1,0:T(8,128)} copy(f32[1280,384]{0,1:T(8,128)S(1)} %pad_maximum_fusion) | data formatting | bytes 3932160 | tf_op jit(solution)/shard_map/concatenate | solution.py:142
  (55 shorter events, 1.4 us)
Async XLA Ops:
  1.4 0.7 collective-permute-start
  3.5 2.0 %collective-permute-start.7 = (f32[64,64]{0,1:T(8,128)S(1)}, f32[64,64]{0,1:T(8,128)S(1)}, u32[]{:S(2)}, u32[]{:S(2)}) collective-permute-start(f32[64,64]{0,1:T(8,128)S(1)} %slice.79), channel_id=1, source_target_pairs={{0,16}} | collective-permute-start | bytes 49160 | tf_op jit(solution)/shard_map/ppermute | solution.py:30
  4.2 1.4 collective-permute-start.6
  4.8 0.7 collective-permute-start.5
  5.6 3.7 %collective-permute-start.10 = (f32[64,64]{0,1:T(8,128)S(1)}, f32[64,64]{0,1:T(8,128)S(1)}, u32[]{:S(2)}, u32[]{:S(2)}) collective-permute-start(f32[64,64]{0,1:T(8,128)S(1)} %select_select_fusion.6), channel_id=1, source_target_pairs={{0,64},{16,80},{32,96},{48,112}} | collective-permute-start | bytes 49160 | tf_op jit(solution)/shard_map/ppermute | solution.py:30
  6.3 3.1 %collective-permute-start.9 = (f32[64,64]{0,1:T(8,128)S(1)}, f32[64,64]{0,1:T(8,128)S(1)}, u32[]{:S(2)}, u32[]{:S(2)}) collective-permute-start(f32[64,64]{0,1:T(8,128)S(1)} %select_select_fusion.6), channel_id=1, source_target_pairs={{0,128},{16,144},{32,160},{48,176}} | collective-permute-start | bytes 49160 | tf_op jit(solution)/shard_map/ppermute | solution.py:30
  6.9 2.4 %collective-permute-start.8 = (f32[64,64]{0,1:T(8,128)S(1)}, f32[64,64]{0,1:T(8,128)S(1)}, u32[]{:S(2)}, u32[]{:S(2)}) collective-permute-start(f32[64,64]{0,1:T(8,128)S(1)} %select_select_fusion.6), channel_id=1, source_target_pairs={{0,192},{16,208},{32,224},{48,240}} | collective-permute-start | bytes 49160 | tf_op jit(solution)/shard_map/ppermute | solution.py:30
  7.7 3.0 %collective-permute-start.1 = (f32[64,128]{0,1:T(8,128)S(1)}, f32[64,128]{0,1:T(8,128)S(1)}, u32[]{:S(2)}, u32[]{:S(2)}) collective-permute-start(f32[64,128]{0,1:T(8,128)S(1)} %slice.78), channel_id=1, source_target_pairs={{16,17},{32,34},{48,51},{64,68},{80,85},{96,102},{112,119},{128,13... | collective-permute-start | bytes 98312 | tf_op jit(solution)/shard_map/ppermute | solution.py:55
  8.6 3.5 %collective-permute-start.4 = (f32[64,1280]{1,0:T(8,128)S(1)}, f32[64,1280]{1,0:T(8,128)S(1)}, u32[]{:S(2)}, u32[]{:S(2)}) collective-permute-start(f32[64,1280]{1,0:T(8,128)S(1)} %copy.15), channel_id=1, source_target_pairs={{0,2},{1,3},{16,18},{17,19},{32,34},{33,35},{48,50},{49,51},{64,66... | collective-permute-start | bytes 983048 | tf_op jit(solution)/shard_map/ppermute | solution.py:30
  9.4 2.7 %collective-permute-start.12 = (f32[64,64]{0,1:T(8,128)S(1)}, f32[64,64]{0,1:T(8,128)S(1)}, u32[]{:S(2)}, u32[]{:S(2)}) collective-permute-start(f32[64,64]{0,1:T(8,128)S(1)} %select_select_fusion.5), channel_id=1, source_target_pairs={{0,256},{16,272},{32,288},{48,304},{64,320},{80,336},{96,352},{112... | collective-permute-start | bytes 49160 | tf_op jit(solution)/shard_map/ppermute | solution.py:30
  10.1 2.1 %collective-permute-start.11 = (f32[64,64]{0,1:T(8,128)S(1)}, f32[64,64]{0,1:T(8,128)S(1)}, u32[]{:S(2)}, u32[]{:S(2)}) collective-permute-start(f32[64,64]{0,1:T(8,128)S(1)} %select_select_fusion.5), channel_id=1, source_target_pairs={{0,512},{16,528},{32,544},{48,560},{64,576},{80,592},{96,608},{112... | collective-permute-start | bytes 49160 | tf_op jit(solution)/shard_map/ppermute | solution.py:30
  10.7 48.4 %collective-permute-start.3 = (f32[64,128]{0,1:T(8,128)S(1)}, f32[64,128]{0,1:T(8,128)S(1)}, u32[]{:S(2)}, u32[]{:S(2)}) collective-permute-start(f32[64,128]{0,1:T(8,128)S(1)} %broadcast_select_fusion.8), channel_id=1, source_target_pairs={{0,256},{256,512},{512,0},{17,273},{273,529},{529,17},{34,290},{29... | collective-permute-start | bytes 98312 | tf_op jit(solution)/shard_map/ppermute | solution.py:68
  11.4 47.7 %collective-permute-start.2 = (f32[64,128]{0,1:T(8,128)S(1)}, f32[64,128]{0,1:T(8,128)S(1)}, u32[]{:S(2)}, u32[]{:S(2)}) collective-permute-start(f32[64,128]{0,1:T(8,128)S(1)} %broadcast_select_fusion.8), channel_id=1, source_target_pairs={{0,512},{256,0},{512,256},{17,529},{273,17},{529,273},{34,546},{29... | collective-permute-start | bytes 98312 | tf_op jit(solution)/shard_map/ppermute | solution.py:68
  25.1 33.1 %collective-permute-start.13 = (f32[64,1280]{1,0:T(8,128)S(1)}, f32[64,1280]{1,0:T(8,128)S(1)}, u32[]{:S(2)}, u32[]{:S(2)}) collective-permute-start(f32[64,1280]{1,0:T(8,128)S(1)} %copy.17), channel_id=1, source_target_pairs={{0,4},{1,5},{2,6},{3,7},{16,20},{17,21},{18,22},{19,23},{32,36},{3... | collective-permute-start | bytes 983048 | tf_op jit(solution)/shard_map/ppermute | solution.py:30
  58.5 0.7 collective-permute-start.14
  59.2 0.7 collective-permute-start.15
  60.0 0.7 collective-permute-start.16
  60.7 2.9 %collective-permute-start.17 = (f32[64,512]{0,1:T(8,128)S(1)}, f32[64,512]{0,1:T(8,128)S(1)}, u32[]{:S(2)}, u32[]{:S(2)}) collective-permute-start(f32[64,512]{0,1:T(8,128)S(1)} %broadcast_select_fusion.4), channel_id=1, source_target_pairs={{0,64},{16,80},{32,96},{48,112},{256,320},{272,336},{288,352},{304... | collective-permute-start | bytes 393224 | tf_op jit(solution)/shard_map/ppermute | solution.py:30
  61.6 7.1 %collective-permute-start.19 = (f32[64,1280]{1,0:T(8,128)S(1)}, f32[64,1280]{1,0:T(8,128)}, u32[]{:S(2)}, u32[]{:S(2)}) collective-permute-start(f32[64,1280]{1,0:T(8,128)S(1)} %copy.23), channel_id=1, source_target_pairs={{0,8},{1,9},{2,10},{3,11},{4,12},{5,13},{6,14},{7,15},{16,24},{17,... | collective-permute-start | bytes 983048 | tf_op jit(solution)/shard_map/ppermute | solution.py:30
  63.7 3.2 %copy-start = (f32[64,512]{0,1:T(8,128)}, f32[64,512]{0,1:T(8,128)S(1)}, u32[]{:S(2)}) copy-start(f32[64,512]{0,1:T(8,128)S(1)} %broadcast_select_fusion.5) | copy-start | bytes 393220
  63.7 68.9 %collective-permute-start.18 = (f32[64,512]{0,1:T(8,128)S(1)}, f32[64,512]{0,1:T(8,128)}, u32[]{:S(2)}, u32[]{:S(2)}) collective-permute-start(f32[64,512]{0,1:T(8,128)S(1)} %broadcast_select_fusion.5), channel_id=1, source_target_pairs={{0,128},{16,144},{32,160},{48,176},{64,192},{80,208},{96,224},{112... | collective-permute-start | bytes 393224 | tf_op jit(solution)/shard_map/ppermute | solution.py:30

commit v5 on v3

--- a/solution.py
+++ b/solution.py
@@ -10,6 +10,13 @@
 def tree_broadcast(x, axes, size, index_of, member, radix=RADIX):
     have = 1
     while have < size:
+        x = tree_round(x, axes, size, index_of, member, have, radix)
+        have *= radix
+    return x
+
+
+def tree_round(x, axes, size, index_of, member, have, radix=RADIX):
+    if True:
         fresh = x
         for c in range(1, radix):
             lo = c * have
@@ -23,9 +30,7 @@
             got = lax.ppermute(x, axes, pairs)
             take = jnp.logical_and(member >= lo, member < lo + have)
             fresh = jnp.where(take, got, fresh)
-        x = fresh
-        have *= radix
-    return x
+    return fresh
 
 
 def shards(matrix):
@@ -44,18 +49,24 @@
         return [lambda m: m * n_col]
 
     corner_t = tree_broadcast(panel_t[:, :B], ("row", "col"), n_row, col0_group, row_id, radix=4)
+    panel_t, head, corner_t = lax.optimization_barrier((panel_t, head, corner_t))
 
     def col_groups(_):
         return [lambda m, r=r: r * n_col + m for r in range(n_row)]
 
-    with_corner = jnp.concatenate([panel_t, corner_t], axis=1)
-    with_corner = tree_broadcast(with_corner, ("row", "col"), n_col, col_groups, col_id)
-    panel_t = with_corner[:, :rows_dev]
-    corner_t = with_corner[:, rows_dev:]
+    def panel_round(x, have):
+        return tree_round(x, ("row", "col"), n_col, col_groups, col_id, have)
+
+    panel_t = panel_round(panel_t, 1)
 
     pairs = [(r * n_col, r * n_col + r % n_col) for r in range(n_row) if r % n_col]
-    got = lax.ppermute(head, ("row", "col"), pairs)
-    head = jnp.where(col_id == 0, head, got)
+    first = jnp.concatenate([head, corner_t], axis=1)
+    got = lax.ppermute(first, ("row", "col"), pairs)
+    first = jnp.where(col_id == 0, first, got)
+    panel_t, first = lax.optimization_barrier((panel_t, first))
+    panel_t = panel_round(panel_t, 2)
+    head = first[:, :window_cols]
+    corner_t = first[:, window_cols:]
     rel = (row_id - col_id) % n_row
     my_j = rel // n_col
     is_src = rel % n_col == 0
@@ -74,8 +85,9 @@
         for c in range(1, n_src):
             pick = jnp.where((my_j - jj) % n_src == c, pieces[c], pick)
         ordered.append(pick)
-    packet = jnp.concatenate(ordered, axis=1)
+    packet = jnp.concatenate(ordered + [corner_t], axis=1)
     packet = jnp.where(is_src, packet, jnp.zeros_like(packet))
+    panel_t, packet = lax.optimization_barrier((panel_t, packet))
 
     def row_groups(_):
         out = []
@@ -85,10 +97,20 @@
                 out.append(lambda m, base=base, q=q: ((base + m) % n_row) * n_col + q)
         return out
 
-    packet = tree_broadcast(packet, ("row", "col"), n_col, row_groups, rel % n_col)
+    have = 1
+    while have < n_col:
+        packet = tree_round(packet, ("row", "col"), n_col, row_groups, rel % n_col, have)
+        if 4 * have < n_col:
+            panel_t = panel_round(panel_t, 4 * have)
+            panel_t, packet = lax.optimization_barrier((panel_t, packet))
+        have *= 2
 
+    corner_t = packet[:, n_src * window_cols:]
     corner = (corner_t + corner_t.T) / 2.0
     factor = jnp.linalg.cholesky(corner)
+    inverse = lax.linalg.triangular_solve(
+        factor, jnp.eye(B, dtype=factor.dtype), left_side=True, lower=True
+    )
 
     tiles = []
     for k in range(cols_dev // B):
@@ -97,15 +119,17 @@
         tiles.append(packet[:, j * window_cols + lt * B: j * window_cols + (lt + 1) * B])
     window_t = jnp.concatenate(tiles, axis=1)
 
-    both = jnp.concatenate([panel_t, window_t], axis=1)
-    solved = lax.linalg.triangular_solve(factor, both, left_side=True, lower=True)
-    lower_t = solved[:, :rows_dev]
+    def apply(x):
+        return lax.dot(inverse, x, precision=lax.Precision.HIGHEST,
+                       preferred_element_type=jnp.float32)
+
+    col_t = apply(window_t)
+    col_t = jnp.concatenate(
+        [jnp.where(col_id == 0, factor.T, col_t[:, :B]), col_t[:, B:]], axis=1
+    )
+    lower_t = apply(panel_t)
     lower_t = jnp.concatenate(
         [jnp.where(row_id == 0, factor.T, lower_t[:, :B]), lower_t[:, B:]], axis=1
-    )
-    col_t = solved[:, rows_dev:]
-    col_t = jnp.concatenate(
-        [jnp.where(col_id == 0, factor.T, col_t[:, :B]), col_t[:, B:]], axis=1
     )
     change = lax.dot_general(
         lower_t,

time: 136 us -> 141 us (1.037)
  the two profiles are of different devices: /device:TPU:104 before, /device:TPU:174 now
where the time goes in v5:
time: 141 us
  waiting for transfers between devices  101 us (72%)
  starting transfers between devices  14 us (10%)
  other arithmetic  13.5 us (10%)
  local copies, waits for them, and re-layouts  7.41 us (5%)
  matrix products  3.33 us (2%)
    ppermute x16, waiting for transfers between devices, tree_round(): got = lax.ppermute(x, axes, pairs)  101 us
    ppermute x16, starting transfers between devices, tree_round(): got = lax.ppermute(x, axes, pairs)  12 us
    another operation x3, other arithmetic, shards(): factor = jnp.linalg.cholesky(corner)  6.52 us
    another operation x2, other arithmetic, shards(): lax.linalg.triangular_solve(factor, jnp.eye(B, dtype=factor.dtype), left_...  5.55 us
  transfers between devices with their start and end apart: 19, of which 2 were waited for; matrix products, arithmetic and copies ran while one was open for 2% of the time, Pallas kernels for 0%

profile of v5, /device:TPU:174, one launch (start us, length us, event | category | flops | bytes accessed | tf_op | source)
XLA Modules:
  0.0 140.7 jit_solution(7991742786187586982)
XLA Ops:
  0.0 1.1 slice_bitcast_fusion
  1.1 0.7 collective-permute-start.2
  1.8 0.7 collective-permute-start.1
  2.5 0.7 collective-permute-start
  3.2 0.7 collective-permute-start.5
  3.9 0.7 collective-permute-start.4
  4.6 0.7 collective-permute-start.3
  5.3 0.7 collective-permute-start.7
  6.0 0.7 collective-permute-start.6
  6.7 0.2 copy.11
  7.0 0.7 collective-permute-start.8
  7.7 0.7 collective-permute-start.9
  8.4 0.2 copy.12
  8.7 0.7 collective-permute-start.12
  9.4 0.7 collective-permute-start.11
  10.2 0.2 copy.13
  10.4 0.7 collective-permute-start.10
  11.2 0.2 copy.14
  11.5 0.7 collective-permute-start.14
  12.2 0.2 copy.15
  12.4 0.7 collective-permute-start.13
  13.2 0.2 copy.16
  13.5 0.7 collective-permute-start.16
  14.2 0.2 copy.17
  14.4 1.3 collective-permute-start.15
  15.8 77.7 %collective-permute-done.15 = f32[64,1280]{1,0:T(8,128)S(1)} collective-permute-done((f32[64,1280]{1,0:T(8,128)S(1)}, f32[64,1280]{1,0:T(8,128)S(1)}, u32[]{:S(2)}, u32[]{:S(2)}) %collective-permute-start.15) | collective-permute-done | bytes 327712 | tf_op jit(solution)/shard_map/ppermute | solution.py:30
  93.4 0.2 copy.18
  93.7 0.7 collective-permute-start.17
  94.5 1.3 collective-permute-start.18
  95.8 1.9 %copy.26 = f32[1280,384]{0,1:T(8,128)S(1)} copy(f32[1280,384]{1,0:T(8,128)} %param.1) | data formatting | bytes 3932160 | tf_op args[0]
  97.7 23.8 %collective-permute-done.18 = f32[64,448]{0,1:T(8,128)S(1)} collective-permute-done((f32[64,448]{0,1:T(8,128)S(1)}, f32[64,448]{0,1:T(8,128)S(1)}, u32[]{:S(2)}, u32[]{:S(2)}) %collective-permute-start.18) | collective-permute-done | bytes 114720 | tf_op jit(solution)/shard_map/ppermute | solution.py:30
  121.8 5.8 %cholesky.20 = f32[64,64]{1,0:T(8,128)S(1)} custom-call(f32[64,64]{1,0:T(8,128)S(1)} %fusion.6), custom_call_target="Cholesky" | custom-call | tf_op jit(solution)/shard_map/jit(cholesky)/cholesky | solution.py:110
  127.7 0.6 compare_reduce_fusion
  128.3 0.7 select_bitcast_fusion
  129.0 4.9 %custom-call.6 = f32[1,64,64]{1,2,0:T(8,128)S(1)} custom-call(f32[1,64,64]{2,1,0:T(8,128)S(1)} %select_bitcast_fusion), custom_call_target="InvertDiagBlocksLowerTriangular" | custom-call | tf_op jit(solution)/shard_map/triangular_solve | solution.py:111
  133.9 0.2 fusion.4
  134.1 0.4 fusion.11
  134.5 0.1 slice.94
  134.6 0.8 fusion.10
  135.4 0.1 slice.86
  135.6 0.1 copy.28
  135.7 0.7 bitcast_select_fusion
  136.5 0.1 copy.22
  136.5 1.9 %fusion = f32[1280,384]{0,1:T(8,128)S(1)} fusion(f32[1280,384]{0,1:T(8,128)S(1)} %copy.26, pred[1280]{0:T(1024)(128)(4,1)S(1)} %fusion.8, f32[64,1216]{1,0:T(8,128)S(1)} %slice.86, f32[64,64]{1,0:T(8,128)S(1)} %copy.22, f32[64,320]{1,0:T(8,128)S(1)} %slice.94, f32[64,64]{1,0:T(8,128)S(1)} %copy.24), kind=kOutput, calls=%fused_computation.1 | convolution fusion | flops 378576896 | bytes 4359424 | tf_op jit(solution)/shard_map/dot_general | solution.py:134
  138.5 0.2 slice_select_fusion
  138.6 0.1 slice.96
  138.8 0.1 pad_maximum_fusion
  138.9 1.8 %copy.27 = f32[1280,384]{1,0:T(8,128)} copy(f32[1280,384]{0,1:T(8,128)S(1)} %pad_maximum_fusion) | data formatting | bytes 3932160 | tf_op jit(solution)/shard_map/concatenate | solution.py:145
  (53 shorter events, 1.0 us)
Async XLA Ops:
  1.1 2.0 %collective-permute-start.2 = (f32[64,64]{0,1:T(8,128)S(1)}, f32[64,64]{0,1:T(8,128)S(1)}, u32[]{:S(2)}, u32[]{:S(2)}) collective-permute-start(f32[64,64]{0,1:T(8,128)S(1)} %slice.83), channel_id=1, source_target_pairs={{0,16}} | collective-permute-start | bytes 49160 | tf_op jit(solution)/shard_map/ppermute | solution.py:30
  1.8 1.4 collective-permute-start.1
  2.5 0.7 collective-permute-start
  3.2 2.0 %collective-permute-start.5 = (f32[64,64]{0,1:T(8,128)S(1)}, f32[64,64]{0,1:T(8,128)S(1)}, u32[]{:S(2)}, u32[]{:S(2)}) collective-permute-start(f32[64,64]{0,1:T(8,128)S(1)} %select_select_fusion.6), channel_id=1, source_target_pairs={{0,64},{16,80},{32,96},{48,112}} | collective-permute-start | bytes 49160 | tf_op jit(solution)/shard_map/ppermute | solution.py:30
  3.9 1.4 collective-permute-start.4
  4.6 0.7 collective-permute-start.3
  5.3 1.4 collective-permute-start.7
  6.0 0.7 collective-permute-start.6
  7.0 1.4 %collective-permute-start.8 = (f32[64,1280]{1,0:T(8,128)S(1)}, f32[64,1280]{1,0:T(8,128)S(1)}, u32[]{:S(2)}, u32[]{:S(2)}) collective-permute-start(f32[64,1280]{1,0:T(8,128)S(1)} %copy.11), channel_id=1, source_target_pairs={{0,1},{16,17},{32,33},{48,49},{64,65},{80,81},{96,97},{112,113},{1... | collective-permute-start | bytes 983048 | tf_op jit(solution)/shard_map/ppermute | solution.py:30
  7.7 0.7 collective-permute-start.9
  8.7 2.4 %collective-permute-start.12 = (f32[64,128]{0,1:T(8,128)S(1)}, f32[64,128]{0,1:T(8,128)S(1)}, u32[]{:S(2)}, u32[]{:S(2)}) collective-permute-start(f32[64,128]{0,1:T(8,128)S(1)} %slice.67), channel_id=1, source_target_pairs={{0,256},{256,512},{512,0},{17,273},{273,529},{529,17},{34,290},{29... | collective-permute-start | bytes 98312 | tf_op jit(solution)/shard_map/ppermute | solution.py:81
  9.4 1.7 %collective-permute-start.11 = (f32[64,128]{0,1:T(8,128)S(1)}, f32[64,128]{0,1:T(8,128)S(1)}, u32[]{:S(2)}, u32[]{:S(2)}) collective-permute-start(f32[64,128]{0,1:T(8,128)S(1)} %slice.67), channel_id=1, source_target_pairs={{0,512},{256,0},{512,256},{17,529},{273,17},{529,273},{34,546},{29... | collective-permute-start | bytes 98312 | tf_op jit(solution)/shard_map/ppermute | solution.py:81
  10.4 0.8 collective-permute-start.10
  11.5 1.6 %collective-permute-start.14 = (f32[64,448]{0,1:T(8,128)S(1)}, f32[64,448]{0,1:T(8,128)S(1)}, u32[]{:S(2)}, u32[]{:S(2)}) collective-permute-start(f32[64,448]{0,1:T(8,128)S(1)} %maximum_select_fusion), channel_id=1, source_target_pairs={{0,16},{256,272},{512,528},{17,33},{273,289},{529,545},{34,50},{29... | collective-permute-start | bytes 344072 | tf_op jit(solution)/shard_map/ppermute | solution.py:30
  12.4 0.8 collective-permute-start.13
  13.5 2.2 %collective-permute-start.16 = (f32[64,448]{0,1:T(8,128)S(1)}, f32[64,448]{0,1:T(8,128)S(1)}, u32[]{:S(2)}, u32[]{:S(2)}) collective-permute-start(f32[64,448]{0,1:T(8,128)S(1)} %broadcast_select_fusion.5), channel_id=1, source_target_pairs={{0,32},{16,48},{256,288},{272,304},{512,544},{528,560},{17,49},{33... | collective-permute-start | bytes 344072 | tf_op jit(solution)/shard_map/ppermute | solution.py:30
  14.4 79.0 %collective-permute-start.15 = (f32[64,1280]{1,0:T(8,128)S(1)}, f32[64,1280]{1,0:T(8,128)S(1)}, u32[]{:S(2)}, u32[]{:S(2)}) collective-permute-start(f32[64,1280]{1,0:T(8,128)S(1)} %copy.17), channel_id=1, source_target_pairs={{0,8},{1,9},{2,10},{3,11},{4,12},{5,13},{6,14},{7,15},{16,24},{17,... | collective-permute-start | bytes 983048 | tf_op jit(solution)/shard_map/ppermute | solution.py:30
  93.7 0.7 collective-permute-start.17
  94.5 27.0 %collective-permute-start.18 = (f32[64,448]{0,1:T(8,128)S(1)}, f32[64,448]{0,1:T(8,128)S(1)}, u32[]{:S(2)}, u32[]{:S(2)}) collective-permute-start(f32[64,448]{0,1:T(8,128)S(1)} %broadcast_select_fusion.6), channel_id=1, source_target_pairs={{0,128},{16,144},{32,160},{48,176},{64,192},{80,208},{96,224},{112... | collective-permute-start | bytes 344072 | tf_op jit(solution)/shard_map/ppermute | solution.py:30

commit v6 on v3

--- a/solution.py
+++ b/solution.py
@@ -53,21 +53,20 @@
     panel_t = with_corner[:, :rows_dev]
     corner_t = with_corner[:, rows_dev:]
 
-    pairs = [(r * n_col, r * n_col + r % n_col) for r in range(n_row) if r % n_col]
-    got = lax.ppermute(head, ("row", "col"), pairs)
-    head = jnp.where(col_id == 0, head, got)
     rel = (row_id - col_id) % n_row
     my_j = rel // n_col
     is_src = rel % n_col == 0
-    pieces = [head]
-    for c in range(1, n_src):
+    pieces = []
+    for c in range(n_src):
         pairs = []
-        for q in range(n_col):
-            for j in range(n_src):
-                a = q + n_col * j
-                b = q + n_col * ((j + c) % n_src)
-                pairs.append((a * n_col + q, b * n_col + q))
-        pieces.append(lax.ppermute(head, ("row", "col"), pairs))
+        for r in range(n_row):
+            q = r % n_col
+            if c or q:
+                pairs.append((r * n_col, ((r + n_col * c) % n_row) * n_col + q))
+        got = lax.ppermute(head, ("row", "col"), pairs)
+        if c == 0:
+            got = jnp.where(col_id == 0, head, got)
+        pieces.append(got)
     ordered = []
     for jj in range(n_src):
         pick = pieces[0]

time: 136 us -> 141 us (1.037)
  waiting for transfers between devices: 83.7 us -> 88.6 us
    ppermute x16, waiting for transfers between devices: 83.7 us -> 88.6 us  [tree_broadcast(): got = lax.ppermute(x, axes, pairs)]
  transfers between devices with their start and end apart: 19 -> 19, of which waited for: 2 -> 2; matrix products, arithmetic and copies ran while one was open for 6% -> 5% of each run, Pallas kernels for 0% -> 0%
where the time goes in v6:
time: 141 us; the launch traced here: 140 us
  waiting for transfers between devices  88.6 us (63%)
  other arithmetic  17.1 us (12%)
  local copies, waits for them, and re-layouts  16 us (11%)
  starting transfers between devices  14.6 us (10%)
  matrix products  3.06 us (2%)
    ppermute x16, waiting for transfers between devices, tree_broadcast(): got = lax.ppermute(x, axes, pairs)  88.6 us
    ppermute x16, starting transfers between devices, tree_broadcast(): got = lax.ppermute(x, axes, pairs)  12.6 us
    another operation x3, other arithmetic, shards(): factor = jnp.linalg.cholesky(corner)  6.52 us
    unnamed x9, local copies, waits for them, and re-layouts  5.9 us
    another operation x2, other arithmetic, shards(): lax.linalg.triangular_solve(factor, both, left_side=True, lower=True)  5.55 us
    select_n x11, other arithmetic, tree_broadcast(): fresh = jnp.where(take, got, fresh)  3.14 us
  transfers between devices with their start and end apart: 19, of which 2 were waited for; matrix products, arithmetic and copies ran while one was open for 5% of the time, Pallas kernels for 0%

profile of v6, /device:TPU:104, one launch (start us, length us, event | category | flops | bytes accessed | tf_op | source)
XLA Modules:
  0.0 140.1 jit_solution(12252375378180197082)
XLA Ops:
  0.0 1.1 slice_bitcast_fusion
  1.1 0.7 collective-permute-start.2
  1.8 0.7 collective-permute-start.1
  2.5 0.7 collective-permute-start
  3.2 0.7 collective-permute-start.5
  3.9 0.7 collective-permute-start.4
  4.6 0.7 collective-permute-start.3
  5.3 0.7 collective-permute-start.7
  6.0 0.7 collective-permute-start.6
  6.7 0.7 collective-permute-start.14
  7.3 0.7 collective-permute-start.13
  8.0 0.7 collective-permute-start.12
  8.9 0.2 copy.11
  9.2 0.7 collective-permute-start.8
  9.9 0.2 copy.12
  10.3 0.2 copy.13
  10.5 0.7 collective-permute-start.9
  11.2 0.7 collective-permute-start.15
  12.0 0.7 collective-permute-start.16
  13.0 1.0 copy.15
  14.0 0.7 collective-permute-start.10
  14.7 1.3 collective-permute-start.17
  16.1 1.9 %copy.26 = f32[1280,384]{0,1:T(8,128)S(1)} copy(f32[1280,384]{1,0:T(8,128)} %param.1) | data formatting | bytes 3932160 | tf_op args[0]
  18.0 1.3 collective-permute-start.18
  19.3 1.1 copy.16
  20.5 1.0 copy.17
  21.5 1.3 collective-permute-start.11
  22.8 39.4 %collective-permute-done.18 = f32[64,384]{0,1:T(8,128)} collective-permute-done((f32[64,384]{0,1:T(8,128)S(1)}, f32[64,384]{0,1:T(8,128)}, u32[]{:S(2)}, u32[]{:S(2)}) %collective-permute-start.18) | collective-permute-done | bytes 98336 | tf_op jit(solution)/shard_map/ppermute | solution.py:23
  62.2 1.6 %broadcast_select_fusion.7 = f32[64,384]{0,1:T(8,128)} fusion(f32[64,384]{0,1:T(8,128)} %collective-permute-done.18, f32[64,384]{0,1:T(8,128)S(1)} %broadcast_select_fusion.6, pred[]{:T(512)S(6)} %and.99), kind=kLoop, calls=%fused_computation.19 | loop fusion | flops 24576 | bytes 294913 | tf_op jit(solution)/shard_map/jit(_where)/select_n | solution.py:25
  63.8 49.1 %collective-permute-done.11 = f32[64,1344]{1,0:T(8,128)S(1)} collective-permute-done((f32[64,1344]{1,0:T(8,128)}, f32[64,1344]{1,0:T(8,128)S(1)}, u32[]{:S(2)}, u32[]{:S(2)}) %collective-permute-start.11) | collective-permute-done | bytes 344096 | tf_op jit(solution)/shard_map/ppermute | solution.py:23
  113.0 1.1 copy.18
  114.1 1.2 broadcast_select_fusion.3
  115.3 0.7 copy.19
  116.0 0.8 fusion.7
  116.9 5.8 %cholesky.18 = f32[64,64]{1,0:T(8,128)S(1)} custom-call(f32[64,64]{1,0:T(8,128)S(1)} %fusion.6), custom_call_target="Cholesky" | custom-call | tf_op jit(solution)/shard_map/jit(cholesky)/cholesky | solution.py:90
  122.8 0.6 compare_reduce_fusion
  123.4 0.7 select_bitcast_fusion
  124.1 4.9 %custom-call.6 = f32[1,64,64]{1,2,0:T(8,128)S(1)} custom-call(f32[1,64,64]{2,1,0:T(8,128)S(1)} %select_bitcast_fusion), custom_call_target="InvertDiagBlocksLowerTriangular" | custom-call | tf_op jit(solution)/shard_map/triangular_solve | solution.py:100
  129.0 0.8 slice_dynamic-update-slice_fusion.6
  129.8 0.8 slice_dynamic-update-slice_fusion.5
  130.5 0.8 slice_dynamic-update-slice_fusion.4
  131.3 0.8 slice_dynamic-update-slice_fusion.3
  132.0 0.8 slice_dynamic-update-slice_fusion.2
  132.8 0.8 slice_dynamic-update-slice_fusion.1
  133.6 1.1 fusion.4
  135.1 0.7 bitcast_select_fusion
  135.9 1.9 %fusion = f32[1280,384]{0,1:T(8,128)S(1)} fusion(f32[1280,384]{0,1:T(8,128)S(1)} %copy.26, pred[1280]{0:T(1024)(128)(4,1)S(1)} %fusion.8, f32[64,1216]{1,0:T(8,128)S(1)} %slice.95, f32[64,64]{1,0:T(8,128)S(1)} %copy.22, f32[64,320]{1,0:T(8,128)S(1)} %slice.97, f32[64,64]{1,0:T(8,128)S(1)} %copy.24), kind=kOutput, calls=%fused_computation.1 | convolution fusion | flops 378576896 | bytes 4359424 | tf_op jit(solution)/shard_map/dot_general | solution.py:109
  138.3 1.8 %copy.27 = f32[1280,384]{1,0:T(8,128)} copy(f32[1280,384]{0,1:T(8,128)S(1)} %pad_maximum_fusion) | data formatting | bytes 3932160 | tf_op jit(solution)/shard_map/concatenate | solution.py:120
  (49 shorter events, 1.8 us)
Async XLA Ops:
  1.1 2.0 %collective-permute-start.2 = (f32[64,64]{0,1:T(8,128)S(1)}, f32[64,64]{0,1:T(8,128)S(1)}, u32[]{:S(2)}, u32[]{:S(2)}) collective-permute-start(f32[64,64]{0,1:T(8,128)S(1)} %slice.84), channel_id=1, source_target_pairs={{0,16}} | collective-permute-start | bytes 49160 | tf_op jit(solution)/shard_map/ppermute | solution.py:23
  1.8 1.4 collective-permute-start.1
  2.5 0.7 collective-permute-start
  3.2 2.0 %collective-permute-start.5 = (f32[64,64]{0,1:T(8,128)S(1)}, f32[64,64]{0,1:T(8,128)S(1)}, u32[]{:S(2)}, u32[]{:S(2)}) collective-permute-start(f32[64,64]{0,1:T(8,128)S(1)} %select_select_fusion.6), channel_id=1, source_target_pairs={{0,64},{16,80},{32,96},{48,112}} | collective-permute-start | bytes 49160 | tf_op jit(solution)/shard_map/ppermute | solution.py:23
  3.9 1.4 collective-permute-start.4
  4.6 0.7 collective-permute-start.3
  5.3 3.5 %collective-permute-start.7 = (f32[64,64]{0,1:T(8,128)S(1)}, f32[64,64]{0,1:T(8,128)S(1)}, u32[]{:S(2)}, u32[]{:S(2)}) collective-permute-start(f32[64,64]{0,1:T(8,128)S(1)} %select_select_fusion.5), channel_id=1, source_target_pairs={{0,256},{16,272},{32,288},{48,304},{64,320},{80,336},{96,352},{112... | collective-permute-start | bytes 49160 | tf_op jit(solution)/shard_map/ppermute | solution.py:23
  6.0 2.8 %collective-permute-start.6 = (f32[64,64]{0,1:T(8,128)S(1)}, f32[64,64]{0,1:T(8,128)S(1)}, u32[]{:S(2)}, u32[]{:S(2)}) collective-permute-start(f32[64,64]{0,1:T(8,128)S(1)} %select_select_fusion.5), channel_id=1, source_target_pairs={{0,512},{16,528},{32,544},{48,560},{64,576},{80,592},{96,608},{112... | collective-permute-start | bytes 49160 | tf_op jit(solution)/shard_map/ppermute | solution.py:23
  6.7 3.2 %collective-permute-start.14 = (f32[64,128]{0,1:T(8,128)S(1)}, f32[64,128]{0,1:T(8,128)S(1)}, u32[]{:S(2)}, u32[]{:S(2)}) collective-permute-start(f32[64,128]{0,1:T(8,128)S(1)} %slice.87), channel_id=1, source_target_pairs={{16,17},{32,34},{48,51},{64,68},{80,85},{96,102},{112,119},{128,13... | collective-permute-start | bytes 98312 | tf_op jit(solution)/shard_map/ppermute | solution.py:66
  7.3 2.5 %collective-permute-start.13 = (f32[64,128]{0,1:T(8,128)S(1)}, f32[64,128]{0,1:T(8,128)S(1)}, u32[]{:S(2)}, u32[]{:S(2)}) collective-permute-start(f32[64,128]{0,1:T(8,128)S(1)} %slice.87), channel_id=1, source_target_pairs={{0,256},{16,273},{32,290},{48,307},{64,324},{80,341},{96,358},{112... | collective-permute-start | bytes 98312 | tf_op jit(solution)/shard_map/ppermute | solution.py:66
  8.0 1.9 %collective-permute-start.12 = (f32[64,128]{0,1:T(8,128)S(1)}, f32[64,128]{0,1:T(8,128)S(1)}, u32[]{:S(2)}, u32[]{:S(2)}) collective-permute-start(f32[64,128]{0,1:T(8,128)S(1)} %slice.87), channel_id=1, source_target_pairs={{0,512},{16,529},{32,546},{48,563},{64,580},{80,597},{96,614},{112... | collective-permute-start | bytes 98312 | tf_op jit(solution)/shard_map/ppermute | solution.py:66
  9.2 0.8 collective-permute-start.8
  10.5 2.1 %collective-permute-start.9 = (f32[64,1344]{1,0:T(8,128)S(1)}, f32[64,1344]{1,0:T(8,128)S(1)}, u32[]{:S(2)}, u32[]{:S(2)}) collective-permute-start(f32[64,1344]{1,0:T(8,128)S(1)} %copy.13), channel_id=1, source_target_pairs={{0,2},{1,3},{16,18},{17,19},{32,34},{33,35},{48,50},{49,51},{64,66... | collective-permute-start | bytes 1032200 | tf_op jit(solution)/shard_map/ppermute | solution.py:23
  11.2 0.7 collective-permute-start.15
  12.0 2.7 %collective-permute-start.16 = (f32[64,384]{0,1:T(8,128)S(1)}, f32[64,384]{0,1:T(8,128)S(1)}, u32[]{:S(2)}, u32[]{:S(2)}) collective-permute-start(f32[64,384]{0,1:T(8,128)S(1)} %broadcast_select_fusion.4), channel_id=1, source_target_pairs={{0,32},{16,48},{256,288},{272,304},{512,544},{528,560},{17,49},{33... | collective-permute-start | bytes 294920 | tf_op jit(solution)/shard_map/ppermute | solution.py:23
  14.0 5.3 %collective-permute-start.10 = (f32[64,1344]{1,0:T(8,128)}, f32[64,1344]{1,0:T(8,128)S(1)}, u32[]{:S(2)}, u32[]{:S(2)}) collective-permute-start(f32[64,1344]{1,0:T(8,128)} %copy.15), channel_id=1, source_target_pairs={{0,4},{1,5},{2,6},{3,7},{16,20},{17,21},{18,22},{19,23},{32,36},{3... | collective-permute-start | bytes 1032200 | tf_op jit(solution)/shard_map/ppermute | solution.py:23
  14.7 3.3 %collective-permute-start.17 = (f32[64,384]{0,1:T(8,128)S(1)}, f32[64,384]{0,1:T(8,128)}, u32[]{:S(2)}, u32[]{:S(2)}) collective-permute-start(f32[64,384]{0,1:T(8,128)S(1)} %broadcast_select_fusion.5), channel_id=1, source_target_pairs={{0,64},{16,80},{32,96},{48,112},{256,320},{272,336},{288,352},{304... | collective-permute-start | bytes 294920 | tf_op jit(solution)/shard_map/ppermute | solution.py:23
  18.0 44.2 %collective-permute-start.18 = (f32[64,384]{0,1:T(8,128)S(1)}, f32[64,384]{0,1:T(8,128)}, u32[]{:S(2)}, u32[]{:S(2)}) collective-permute-start(f32[64,384]{0,1:T(8,128)S(1)} %broadcast_select_fusion.6), channel_id=1, source_target_pairs={{0,128},{16,144},{32,160},{48,176},{64,192},{80,208},{96,224},{112... | collective-permute-start | bytes 294920 | tf_op jit(solution)/shard_map/ppermute | solution.py:23
  21.5 91.5 %collective-permute-start.11 = (f32[64,1344]{1,0:T(8,128)}, f32[64,1344]{1,0:T(8,128)S(1)}, u32[]{:S(2)}, u32[]{:S(2)}) collective-permute-start(f32[64,1344]{1,0:T(8,128)} %copy.17), channel_id=1, source_target_pairs={{0,8},{1,9},{2,10},{3,11},{4,12},{5,13},{6,14},{7,15},{16,24},{17,... | collective-permute-start | bytes 1032200 | tf_op jit(solution)/shard_map/ppermute | solution.py:23

commit v7 on v6

--- a/solution.py
+++ b/solution.py
@@ -7,8 +7,7 @@
 RADIX = 2
 
 
-def tree_broadcast(x, axes, size, index_of, member, radix=RADIX):
-    have = 1
+def tree_broadcast(x, axes, size, index_of, member, radix=RADIX, have=1):
     while have < size:
         fresh = x
         for c in range(1, radix):
@@ -48,14 +47,13 @@
     def col_groups(_):
         return [lambda m, r=r: r * n_col + m for r in range(n_row)]
 
-    with_corner = jnp.concatenate([panel_t, corner_t], axis=1)
-    with_corner = tree_broadcast(with_corner, ("row", "col"), n_col, col_groups, col_id)
-    panel_t = with_corner[:, :rows_dev]
-    corner_t = with_corner[:, rows_dev:]
+    panel_t, corner_t = lax.optimization_barrier((panel_t, corner_t))
+    panel_t = tree_broadcast(panel_t, ("row", "col"), 2, col_groups, col_id, radix=2, have=1)
 
     rel = (row_id - col_id) % n_row
     my_j = rel // n_col
     is_src = rel % n_col == 0
+    first = jnp.concatenate([head, corner_t], axis=1)
     pieces = []
     for c in range(n_src):
         pairs = []
@@ -63,17 +61,21 @@
             q = r % n_col
             if c or q:
                 pairs.append((r * n_col, ((r + n_col * c) % n_row) * n_col + q))
-        got = lax.ppermute(head, ("row", "col"), pairs)
+        got = lax.ppermute(first, ("row", "col"), pairs)
         if c == 0:
-            got = jnp.where(col_id == 0, head, got)
+            got = jnp.where(col_id == 0, first, got)
         pieces.append(got)
+    panel_t, pieces = lax.optimization_barrier((panel_t, pieces))
+    panel_t = tree_broadcast(panel_t, ("row", "col"), n_col, col_groups, col_id, radix=2, have=2)
+    corner_t = pieces[0][:, window_cols:]
+    pieces = [p[:, :window_cols] for p in pieces]
     ordered = []
     for jj in range(n_src):
         pick = pieces[0]
         for c in range(1, n_src):
             pick = jnp.where((my_j - jj) % n_src == c, pieces[c], pick)
         ordered.append(pick)
-    packet = jnp.concatenate(ordered, axis=1)
+    packet = jnp.concatenate(ordered + [corner_t], axis=1)
     packet = jnp.where(is_src, packet, jnp.zeros_like(packet))
 
     def row_groups(_):
@@ -86,8 +88,12 @@
 
     packet = tree_broadcast(packet, ("row", "col"), n_col, row_groups, rel % n_col)
 
+    corner_t = packet[:, n_src * window_cols:]
     corner = (corner_t + corner_t.T) / 2.0
     factor = jnp.linalg.cholesky(corner)
+    inverse = lax.linalg.triangular_solve(
+        factor, jnp.eye(B, dtype=factor.dtype), left_side=True, lower=True
+    )
 
     tiles = []
     for k in range(cols_dev // B):
@@ -96,15 +102,17 @@
         tiles.append(packet[:, j * window_cols + lt * B: j * window_cols + (lt + 1) * B])
     window_t = jnp.concatenate(tiles, axis=1)
 
-    both = jnp.concatenate([panel_t, window_t], axis=1)
-    solved = lax.linalg.triangular_solve(factor, both, left_side=True, lower=True)
-    lower_t = solved[:, :rows_dev]
+    def apply(x):
+        return lax.dot(inverse, x, precision=lax.Precision.HIGHEST,
+                       preferred_element_type=jnp.float32)
+
+    col_t = apply(window_t)
+    col_t = jnp.concatenate(
+        [jnp.where(col_id == 0, factor.T, col_t[:, :B]), col_t[:, B:]], axis=1
+    )
+    lower_t = apply(panel_t)
     lower_t = jnp.concatenate(
         [jnp.where(row_id == 0, factor.T, lower_t[:, :B]), lower_t[:, B:]], axis=1
-    )
-    col_t = solved[:, rows_dev:]
-    col_t = jnp.concatenate(
-        [jnp.where(col_id == 0, factor.T, col_t[:, :B]), col_t[:, B:]], axis=1
     )
     change = lax.dot_general(
         lower_t,

time: 141 us -> 127 us (0.901)
  waiting for transfers between devices: 88.6 us -> 76 us
  other arithmetic: 17.1 us -> 14.2 us
    ppermute x16, waiting for transfers between devices: 88.6 us -> 76 us  [tree_broadcast(): got = lax.ppermute(x, axes, pairs)]
    dot_general x0 -> x2, matrix products: none -> 2.11 us  [apply(): lax.dot(inverse, x, precision=lax.Precision.HIGHEST, preferred_element_ty...]
    ppermute x4, local copies, waits for them, and re-layouts: 2.7 us -> 4.55 us  [tree_broadcast(): got = lax.ppermute(x, axes, pairs)]
    select_n x11 -> x10, other arithmetic: 3.14 us -> 1.3 us  [tree_broadcast(): fresh = jnp.where(take, got, fresh)]
    unnamed x9 -> x8, local copies, waits for them, and re-layouts: 5.9 us -> 5.1 us
  transfers between devices with their start and end apart: 19 -> 19, of which waited for: 2 -> 2; matrix products, arithmetic and copies ran while one was open for 5% -> 20% of each run, Pallas kernels for 0% -> 0%
where the time goes in v7:
time: 127 us; the launch traced here: 126 us
  waiting for transfers between devices  76 us (60%)
  local copies, waits for them, and re-layouts  16.1 us (13%)
  starting transfers between devices  14.6 us (11%)
  other arithmetic  14.2 us (11%)
  matrix products  4.27 us (3%)
    ppermute x16, waiting for transfers between devices, tree_broadcast(): got = lax.ppermute(x, axes, pairs)  76 us
    ppermute x16, starting transfers between devices, tree_broadcast(): got = lax.ppermute(x, axes, pairs)  12.6 us
    another operation x3, other arithmetic, shards(): factor = jnp.linalg.cholesky(corner)  6.49 us
    another operation x2, other arithmetic, shards(): lax.linalg.triangular_solve(factor, jnp.eye(B, dtype=factor.dtype), left_...  5.45 us
    unnamed x8, local copies, waits for them, and re-layouts  5.1 us
    ppermute x4, local copies, waits for them, and re-layouts, tree_broadcast(): got = lax.ppermute(x, axes, pairs)  4.55 us
  transfers between devices with their start and end apart: 19, of which 2 were waited for; matrix products, arithmetic and copies ran while one was open for 20% of the time, Pallas kernels for 0%

profile of v7, /device:TPU:104, one launch (start us, length us, event | category | flops | bytes accessed | tf_op | source)
XLA Modules:
  0.0 126.1 jit_solution(11573166951234797404)
XLA Ops:
  0.0 1.1 slice_bitcast_fusion
  1.1 0.7 collective-permute-start.2
  1.8 0.7 collective-permute-start.1
  2.5 0.7 collective-permute-start
  3.2 0.7 collective-permute-start.5
  3.9 0.7 collective-permute-start.4
  4.6 0.7 collective-permute-start.3
  5.3 0.7 collective-permute-start.7
  6.0 0.7 collective-permute-start.6
  6.7 0.2 copy.11
  7.0 0.7 collective-permute-start.8
  7.7 0.7 collective-permute-start.9
  8.5 0.7 collective-permute-start.10
  9.1 0.7 collective-permute-start.11
  9.8 0.2 copy.12
  10.3 0.7 collective-permute-start.12
  11.0 0.7 collective-permute-start.13
  11.7 0.9 copy.15
  12.6 1.4 %collective-permute-start.16 = (f32[64,1280]{1,0:T(8,128)}, f32[64,1280]{1,0:T(8,128)}, u32[]{:S(2)}, u32[]{:S(2)}) collective-permute-start(f32[64,1280]{1,0:T(8,128)} %copy.15), channel_id=1, source_target_pairs={{0,2},{1,3},{16,18},{17,19},{32,34},{33,35},{48,50},{49,51},{64,66... | collective-permute-start | bytes 983048 | tf_op jit(solution)/shard_map/ppermute | solution.py:22
  14.0 0.7 collective-permute-start.14
  14.8 1.9 %copy.26 = f32[1280,384]{0,1:T(8,128)S(1)} copy(f32[1280,384]{1,0:T(8,128)} %param.1) | data formatting | bytes 3932160 | tf_op args[0]
  16.7 2.0 %copy.16 = f32[64,1280]{0,1:T(8,128)} copy(f32[64,1280]{1,0:T(8,128)} %collective-permute-done.16) | data formatting | bytes 655360 | tf_op jit(solution)/shard_map/ppermute | solution.py:22
  18.8 1.3 %collective-permute-start.15 = (f32[64,448]{0,1:T(8,128)S(1)}, f32[64,448]{0,1:T(8,128)}, u32[]{:S(2)}, u32[]{:S(2)}) collective-permute-start(f32[64,448]{0,1:T(8,128)S(1)} %broadcast_select_fusion.5), channel_id=1, source_target_pairs={{0,128},{16,144},{32,160},{48,176},{64,192},{80,208},{96,224},{112... | collective-permute-start | bytes 344072 | tf_op jit(solution)/shard_map/ppermute | solution.py:22
  20.2 0.9 copy.17
  21.1 0.7 collective-permute-start.17
  21.8 59.8 %collective-permute-done.15 = f32[64,448]{0,1:T(8,128)} collective-permute-done((f32[64,448]{0,1:T(8,128)S(1)}, f32[64,448]{0,1:T(8,128)}, u32[]{:S(2)}, u32[]{:S(2)}) %collective-permute-start.15) | collective-permute-done | bytes 114720 | tf_op jit(solution)/shard_map/ppermute | solution.py:22
  81.6 1.0 broadcast_select_fusion.6
  82.6 0.6 slice_dynamic-update-slice_fusion.5
  83.2 0.6 slice_dynamic-update-slice_fusion.4
  83.8 0.6 slice_dynamic-update-slice_fusion.3
  84.4 0.6 slice_dynamic-update-slice_fusion.2
  85.0 0.6 slice_dynamic-update-slice_fusion.1
  85.6 0.6 slice_dynamic-update-slice_fusion
  86.4 5.8 %cholesky.20 = f32[64,64]{1,0:T(8,128)S(1)} custom-call(f32[64,64]{1,0:T(8,128)S(1)} %fusion.9), custom_call_target="Cholesky" | custom-call | tf_op jit(solution)/shard_map/jit(cholesky)/cholesky | solution.py:93
  92.3 0.6 compare_reduce_fusion
  92.9 0.6 select_bitcast_fusion
  93.5 4.9 %custom-call.6 = f32[1,64,64]{1,2,0:T(8,128)S(1)} custom-call(f32[1,64,64]{2,1,0:T(8,128)S(1)} %select_bitcast_fusion), custom_call_target="InvertDiagBlocksLowerTriangular" | custom-call | tf_op jit(solution)/shard_map/triangular_solve | solution.py:94
  98.4 1.1 copy.18
  99.5 0.2 copy.19
  99.8 1.3 %collective-permute-start.18 = (f32[64,1280]{1,0:T(8,128)S(1)}, f32[64,1280]{1,0:T(8,128)}, u32[]{:S(2)}, u32[]{:S(2)}) collective-permute-start(f32[64,1280]{1,0:T(8,128)S(1)} %copy.19), channel_id=1, source_target_pairs={{0,8},{1,9},{2,10},{3,11},{4,12},{5,13},{6,14},{7,15},{16,24},{17,... | collective-permute-start | bytes 983048 | tf_op jit(solution)/shard_map/ppermute | solution.py:22
  101.1 0.2 fusion.7
  101.3 1.3 %fusion.13 = f32[64,384]{1,0:T(8,128)S(1)} fusion(f32[64,64]{1,0:T(8,128)S(1)} %fusion.7, f32[64,384]{0,1:T(8,128)} %get-tuple-element.20), kind=kOutput, calls=%fused_computation.51 | convolution fusion | flops 18874368 | bytes 212992 | tf_op jit(solution)/shard_map/dot_general | solution.py:106
  102.8 16.2 %collective-permute-done.18 = f32[64,1280]{1,0:T(8,128)} collective-permute-done((f32[64,1280]{1,0:T(8,128)S(1)}, f32[64,1280]{1,0:T(8,128)}, u32[]{:S(2)}, u32[]{:S(2)}) %collective-permute-start.18) | collective-permute-done | bytes 327712 | tf_op jit(solution)/shard_map/ppermute | solution.py:22
  119.0 1.2 copy.20
  120.2 0.8 fusion.1
  121.2 0.6 bitcast_select_fusion
  122.0 1.9 %fusion = f32[1280,384]{0,1:T(8,128)S(1)} fusion(f32[1280,384]{0,1:T(8,128)S(1)} %copy.26, pred[1280]{0:T(1024)(128)(4,1)S(1)} %fusion.11, f32[64,1216]{1,0:T(8,128)S(1)} %slice.94, f32[64,64]{1,0:T(8,128)S(1)} %copy.22, f32[64,320]{1,0:T(8,128)S(1)} %slice.102, f32[64,64]{1,0:T(8,128)S(1)} %copy.24), kind=kOutput, calls=%fused_computation.1 | convolution fusion | flops 378576896 | bytes 4359424 | tf_op jit(solution)/shard_map/dot_general | solution.py:117
  124.3 1.8 %copy.27 = f32[1280,384]{1,0:T(8,128)} copy(f32[1280,384]{0,1:T(8,128)S(1)} %pad_maximum_fusion) | data formatting | bytes 3932160 | tf_op jit(solution)/shard_map/concatenate | solution.py:128
  (50 shorter events, 1.6 us)
Async XLA Ops:
  1.1 2.0 %collective-permute-start.2 = (f32[64,64]{0,1:T(8,128)S(1)}, f32[64,64]{0,1:T(8,128)S(1)}, u32[]{:S(2)}, u32[]{:S(2)}) collective-permute-start(f32[64,64]{0,1:T(8,128)S(1)} %slice.90), channel_id=1, source_target_pairs={{0,16}} | collective-permute-start | bytes 49160 | tf_op jit(solution)/shard_map/ppermute | solution.py:22
  1.8 1.4 %collective-permute-start.1 = (f32[64,64]{0,1:T(8,128)S(1)}, f32[64,64]{0,1:T(8,128)S(1)}, u32[]{:S(2)}, u32[]{:S(2)}) collective-permute-start(f32[64,64]{0,1:T(8,128)S(1)} %slice.90), channel_id=1, source_target_pairs={{0,32}} | collective-permute-start | bytes 49160 | tf_op jit(solution)/shard_map/ppermute | solution.py:22
  2.5 0.7 collective-permute-start
  3.2 2.0 %collective-permute-start.5 = (f32[64,64]{0,1:T(8,128)S(1)}, f32[64,64]{0,1:T(8,128)S(1)}, u32[]{:S(2)}, u32[]{:S(2)}) collective-permute-start(f32[64,64]{0,1:T(8,128)S(1)} %select_select_fusion.6), channel_id=1, source_target_pairs={{0,64},{16,80},{32,96},{48,112}} | collective-permute-start | bytes 49160 | tf_op jit(solution)/shard_map/ppermute | solution.py:22
  3.9 1.4 %collective-permute-start.4 = (f32[64,64]{0,1:T(8,128)S(1)}, f32[64,64]{0,1:T(8,128)S(1)}, u32[]{:S(2)}, u32[]{:S(2)}) collective-permute-start(f32[64,64]{0,1:T(8,128)S(1)} %select_select_fusion.6), channel_id=1, source_target_pairs={{0,128},{16,144},{32,160},{48,176}} | collective-permute-start | bytes 49160 | tf_op jit(solution)/shard_map/ppermute | solution.py:22
  4.6 0.7 collective-permute-start.3
  5.3 1.4 %collective-permute-start.7 = (f32[64,64]{0,1:T(8,128)S(1)}, f32[64,64]{0,1:T(8,128)S(1)}, u32[]{:S(2)}, u32[]{:S(2)}) collective-permute-start(f32[64,64]{0,1:T(8,128)S(1)} %select_select_fusion.5), channel_id=1, source_target_pairs={{0,256},{16,272},{32,288},{48,304},{64,320},{80,336},{96,352},{112... | collective-permute-start | bytes 49160 | tf_op jit(solution)/shard_map/ppermute | solution.py:22
  6.0 0.7 collective-permute-start.6
  7.0 2.9 %collective-permute-start.8 = (f32[64,1280]{1,0:T(8,128)S(1)}, f32[64,1280]{1,0:T(8,128)S(1)}, u32[]{:S(2)}, u32[]{:S(2)}) collective-permute-start(f32[64,1280]{1,0:T(8,128)S(1)} %copy.11), channel_id=1, source_target_pairs={{0,1},{16,17},{32,33},{48,49},{64,65},{80,81},{96,97},{112,113},{1... | collective-permute-start | bytes 983048 | tf_op jit(solution)/shard_map/ppermute | solution.py:22
  7.7 2.1 %collective-permute-start.9 = (f32[64,192]{0,1:T(8,128)S(1)}, f32[64,192]{0,1:T(8,128)S(1)}, u32[]{:S(2)}, u32[]{:S(2)}) collective-permute-start(f32[64,192]{0,1:T(8,128)S(1)} %pad_maximum_fusion.3), channel_id=1, source_target_pairs={{16,17},{32,34},{48,51},{64,68},{80,85},{96,102},{112,119},{128,13... | collective-permute-start | bytes 147464 | tf_op jit(solution)/shard_map/ppermute | solution.py:64
  8.5 1.7 %collective-permute-start.10 = (f32[64,192]{0,1:T(8,128)S(1)}, f32[64,192]{0,1:T(8,128)S(1)}, u32[]{:S(2)}, u32[]{:S(2)}) collective-permute-start(f32[64,192]{0,1:T(8,128)S(1)} %pad_maximum_fusion.3), channel_id=1, source_target_pairs={{0,256},{16,273},{32,290},{48,307},{64,324},{80,341},{96,358},{112... | collective-permute-start | bytes 147464 | tf_op jit(solution)/shard_map/ppermute | solution.py:64
  9.1 1.0 collective-permute-start.11
  10.3 0.7 collective-permute-start.12
  11.0 3.0 %collective-permute-start.13 = (f32[64,448]{0,1:T(8,128)S(1)}, f32[64,448]{0,1:T(8,128)S(1)}, u32[]{:S(2)}, u32[]{:S(2)}) collective-permute-start(f32[64,448]{0,1:T(8,128)S(1)} %broadcast_select_fusion.3), channel_id=1, source_target_pairs={{0,32},{16,48},{256,288},{272,304},{512,544},{528,560},{17,49},{33... | collective-permute-start | bytes 344072 | tf_op jit(solution)/shard_map/ppermute | solution.py:22
  12.6 4.1 %collective-permute-start.16 = (f32[64,1280]{1,0:T(8,128)}, f32[64,1280]{1,0:T(8,128)}, u32[]{:S(2)}, u32[]{:S(2)}) collective-permute-start(f32[64,1280]{1,0:T(8,128)} %copy.15), channel_id=1, source_target_pairs={{0,2},{1,3},{16,18},{17,19},{32,34},{33,35},{48,50},{49,51},{64,66... | collective-permute-start | bytes 983048 | tf_op jit(solution)/shard_map/ppermute | solution.py:22
  14.0 4.7 %collective-permute-start.14 = (f32[64,448]{0,1:T(8,128)S(1)}, f32[64,448]{0,1:T(8,128)S(1)}, u32[]{:S(2)}, u32[]{:S(2)}) collective-permute-start(f32[64,448]{0,1:T(8,128)S(1)} %broadcast_select_fusion.4), channel_id=1, source_target_pairs={{0,64},{16,80},{32,96},{48,112},{256,320},{272,336},{288,352},{304... | collective-permute-start | bytes 344072 | tf_op jit(solution)/shard_map/ppermute | solution.py:22
  18.8 62.8 %collective-permute-start.15 = (f32[64,448]{0,1:T(8,128)S(1)}, f32[64,448]{0,1:T(8,128)}, u32[]{:S(2)}, u32[]{:S(2)}) collective-permute-start(f32[64,448]{0,1:T(8,128)S(1)} %broadcast_select_fusion.5), channel_id=1, source_target_pairs={{0,128},{16,144},{32,160},{48,176},{64,192},{80,208},{96,224},{112... | collective-permute-start | bytes 344072 | tf_op jit(solution)/shard_map/ppermute | solution.py:22
  21.1 77.3 %collective-permute-start.17 = (f32[64,1280]{1,0:T(8,128)}, f32[64,1280]{1,0:T(8,128)S(1)}, u32[]{:S(2)}, u32[]{:S(2)}) collective-permute-start(f32[64,1280]{1,0:T(8,128)} %copy.17), channel_id=1, source_target_pairs={{0,4},{1,5},{2,6},{3,7},{16,20},{17,21},{18,22},{19,23},{32,36},{3... | collective-permute-start | bytes 983048 | tf_op jit(solution)/shard_map/ppermute | solution.py:22
  99.8 19.2 %collective-permute-start.18 = (f32[64,1280]{1,0:T(8,128)S(1)}, f32[64,1280]{1,0:T(8,128)}, u32[]{:S(2)}, u32[]{:S(2)}) collective-permute-start(f32[64,1280]{1,0:T(8,128)S(1)} %copy.19), channel_id=1, source_target_pairs={{0,8},{1,9},{2,10},{3,11},{4,12},{5,13},{6,14},{7,15},{16,24},{17,... | collective-permute-start | bytes 983048 | tf_op jit(solution)/shard_map/ppermute | solution.py:22

commit v8 on v7

--- a/solution.py
+++ b/solution.py
@@ -66,7 +66,7 @@
             got = jnp.where(col_id == 0, first, got)
         pieces.append(got)
     panel_t, pieces = lax.optimization_barrier((panel_t, pieces))
-    panel_t = tree_broadcast(panel_t, ("row", "col"), n_col, col_groups, col_id, radix=2, have=2)
+    panel_t = tree_broadcast(panel_t, ("row", "col"), n_col // 2, col_groups, col_id, radix=2, have=2)
     corner_t = pieces[0][:, window_cols:]
     pieces = [p[:, :window_cols] for p in pieces]
     ordered = []
@@ -87,6 +87,8 @@
         return out
 
     packet = tree_broadcast(packet, ("row", "col"), n_col, row_groups, rel % n_col)
+    panel_t = tree_broadcast(panel_t, ("row", "col"), n_col, col_groups, col_id, radix=2, have=n_col // 2)
+    panel_t, packet = lax.optimization_barrier((panel_t, packet))
 
     corner_t = packet[:, n_src * window_cols:]
     corner = (corner_t + corner_t.T) / 2.0

time: 127 us -> 130 us (1.024)
  the two profiles are of different devices: /device:TPU:104 before, /device:TPU:682 now
where the time goes in v8:
time: 130 us
  waiting for transfers between devices  84 us (65%)
  other arithmetic  17.2 us (13%)
  starting transfers between devices  15.3 us (12%)
  local copies, waits for them, and re-layouts  9.09 us (7%)
  matrix products  3.33 us (3%)
    ppermute x16, waiting for transfers between devices, tree_broadcast(): got = lax.ppermute(x, axes, pairs)  84 us
    ppermute x16, starting transfers between devices, tree_broadcast(): got = lax.ppermute(x, axes, pairs)  13.3 us
    another operation x3, other arithmetic, shards(): factor = jnp.linalg.cholesky(corner)  6.52 us
    another operation x2, other arithmetic, shards(): lax.linalg.triangular_solve(factor, jnp.eye(B, dtype=factor.dtype), left_...  5.55 us
    select_n x11, other arithmetic, tree_broadcast(): fresh = jnp.where(take, got, fresh)  4.09 us
    ppermute x4, local copies, waits for them, and re-layouts, tree_broadcast(): got = lax.ppermute(x, axes, pairs)  2.61 us
  transfers between devices with their start and end apart: 19, of which 3 were waited for; matrix products, arithmetic and copies ran while one was open for 5% of the time, Pallas kernels for 0%

profile of v8, /device:TPU:682, one launch (start us, length us, event | category | flops | bytes accessed | tf_op | source)
XLA Modules:
  0.0 129.7 jit_solution(3514526175696453932)
XLA Ops:
  0.0 1.1 slice_bitcast_fusion
  1.1 0.7 collective-permute-start.2
  1.8 0.7 collective-permute-start.1
  2.5 0.7 collective-permute-start
  3.2 0.7 collective-permute-start.5
  3.9 0.7 collective-permute-start.4
  4.6 0.7 collective-permute-start.3
  5.3 0.7 collective-permute-start.7
  6.0 0.7 collective-permute-start.6
  6.7 0.2 copy.11
  7.0 0.7 collective-permute-start.8
  7.7 0.7 collective-permute-start.9
  8.5 0.7 collective-permute-start.10
  9.1 0.7 collective-permute-start.11
  9.8 0.2 copy.12
  10.3 0.7 collective-permute-start.15
  11.0 0.7 collective-permute-start.16
  11.7 0.2 copy.13
  11.9 0.7 collective-permute-start.12
  12.7 1.3 collective-permute-start.17
  14.0 0.2 copy.14
  14.3 0.2 copy.15
  14.5 0.7 collective-permute-start.13
  15.2 1.9 %copy.26 = f32[1280,384]{0,1:T(8,128)S(1)} copy(f32[1280,384]{1,0:T(8,128)} %param.1) | data formatting | bytes 3932160 | tf_op args[0]
  17.1 50.2 %collective-permute-done.17 = f32[64,448]{0,1:T(8,128)} collective-permute-done((f32[64,448]{0,1:T(8,128)S(1)}, f32[64,448]{0,1:T(8,128)}, u32[]{:S(2)}, u32[]{:S(2)}) %collective-permute-start.17) | collective-permute-done | bytes 114720 | tf_op jit(solution)/shard_map/ppermute | solution.py:22
  67.4 1.7 %broadcast_select_fusion.6 = f32[64,448]{0,1:T(8,128)} fusion(f32[64,448]{0,1:T(8,128)} %collective-permute-done.17, f32[64,448]{0,1:T(8,128)S(1)} %broadcast_select_fusion.5, pred[]{:T(512)S(6)} %and.100), kind=kLoop, calls=%fused_computation.13 | loop fusion | flops 28672 | bytes 344065 | tf_op jit(solution)/shard_map/jit(_where)/select_n | solution.py:24
  69.0 2.0 %collective-permute-start.18 = (f32[64,448]{0,1:T(8,128)}, f32[64,448]{0,1:T(8,128)}, u32[]{:S(2)}, u32[]{:S(2)}) collective-permute-start(f32[64,448]{0,1:T(8,128)} %broadcast_select_fusion.6), channel_id=1, source_target_pairs={{0,128},{16,144},{32,160},{48,176},{64,192},{80,208},{96,224},{112... | collective-permute-start | bytes 344072 | tf_op jit(solution)/shard_map/ppermute | solution.py:22
  71.0 1.1 copy.16
  72.2 0.2 copy.17
  72.4 1.3 collective-permute-start.14
  73.7 0.5 collective-permute-done.18
  74.2 1.0 broadcast_select_fusion.7
  75.1 33.2 %collective-permute-done.14 = f32[64,1280]{1,0:T(8,128)S(1)} collective-permute-done((f32[64,1280]{1,0:T(8,128)S(1)}, f32[64,1280]{1,0:T(8,128)S(1)}, u32[]{:S(2)}, u32[]{:S(2)}) %collective-permute-start.14) | collective-permute-done | bytes 327712 | tf_op jit(solution)/shard_map/ppermute | solution.py:22
  108.3 1.1 copy.18
  109.4 1.2 broadcast_select_fusion.3
  110.9 5.8 %cholesky.20 = f32[64,64]{1,0:T(8,128)S(1)} custom-call(f32[64,64]{1,0:T(8,128)S(1)} %fusion.6), custom_call_target="Cholesky" | custom-call | tf_op jit(solution)/shard_map/jit(cholesky)/cholesky | solution.py:95
  116.7 0.6 compare_reduce_fusion
  117.4 0.7 select_bitcast_fusion
  118.0 4.9 %custom-call.6 = f32[1,64,64]{1,2,0:T(8,128)S(1)} custom-call(f32[1,64,64]{2,1,0:T(8,128)S(1)} %select_bitcast_fusion), custom_call_target="InvertDiagBlocksLowerTriangular" | custom-call | tf_op jit(solution)/shard_map/triangular_solve | solution.py:96
  122.9 0.2 fusion.4
  123.2 0.4 fusion.11
  123.7 0.8 fusion.10
  124.5 0.1 slice.93
  124.8 0.7 bitcast_select_fusion
  125.6 1.9 %fusion = f32[1280,384]{0,1:T(8,128)S(1)} fusion(f32[1280,384]{0,1:T(8,128)S(1)} %copy.26, pred[1280]{0:T(1024)(128)(4,1)S(1)} %fusion.8, f32[64,1216]{1,0:T(8,128)S(1)} %slice.93, f32[64,64]{1,0:T(8,128)S(1)} %copy.22, f32[64,320]{1,0:T(8,128)S(1)} %slice.95, f32[64,64]{1,0:T(8,128)S(1)} %copy.24), kind=kOutput, calls=%fused_computation.1 | convolution fusion | flops 378576896 | bytes 4359424 | tf_op jit(solution)/shard_map/dot_general | solution.py:119
  127.6 0.2 slice_select_fusion
  127.8 0.1 pad_maximum_fusion
  128.0 1.8 %copy.27 = f32[1280,384]{1,0:T(8,128)} copy(f32[1280,384]{0,1:T(8,128)S(1)} %pad_maximum_fusion) | data formatting | bytes 3932160 | tf_op jit(solution)/shard_map/concatenate | solution.py:130
  (51 shorter events, 1.2 us)
Async XLA Ops:
  1.1 2.0 %collective-permute-start.2 = (f32[64,64]{0,1:T(8,128)S(1)}, f32[64,64]{0,1:T(8,128)S(1)}, u32[]{:S(2)}, u32[]{:S(2)}) collective-permute-start(f32[64,64]{0,1:T(8,128)S(1)} %slice.90), channel_id=1, source_target_pairs={{0,16}} | collective-permute-start | bytes 49160 | tf_op jit(solution)/shard_map/ppermute | solution.py:22
  1.8 1.4 %collective-permute-start.1 = (f32[64,64]{0,1:T(8,128)S(1)}, f32[64,64]{0,1:T(8,128)S(1)}, u32[]{:S(2)}, u32[]{:S(2)}) collective-permute-start(f32[64,64]{0,1:T(8,128)S(1)} %slice.90), channel_id=1, source_target_pairs={{0,32}} | collective-permute-start | bytes 49160 | tf_op jit(solution)/shard_map/ppermute | solution.py:22
  2.5 0.7 collective-permute-start
  3.2 2.0 %collective-permute-start.5 = (f32[64,64]{0,1:T(8,128)S(1)}, f32[64,64]{0,1:T(8,128)S(1)}, u32[]{:S(2)}, u32[]{:S(2)}) collective-permute-start(f32[64,64]{0,1:T(8,128)S(1)} %select_select_fusion.6), channel_id=1, source_target_pairs={{0,64},{16,80},{32,96},{48,112}} | collective-permute-start | bytes 49160 | tf_op jit(solution)/shard_map/ppermute | solution.py:22
  3.9 1.4 %collective-permute-start.4 = (f32[64,64]{0,1:T(8,128)S(1)}, f32[64,64]{0,1:T(8,128)S(1)}, u32[]{:S(2)}, u32[]{:S(2)}) collective-permute-start(f32[64,64]{0,1:T(8,128)S(1)} %select_select_fusion.6), channel_id=1, source_target_pairs={{0,128},{16,144},{32,160},{48,176}} | collective-permute-start | bytes 49160 | tf_op jit(solution)/shard_map/ppermute | solution.py:22
  4.6 0.7 collective-permute-start.3
  5.3 1.4 %collective-permute-start.7 = (f32[64,64]{0,1:T(8,128)S(1)}, f32[64,64]{0,1:T(8,128)S(1)}, u32[]{:S(2)}, u32[]{:S(2)}) collective-permute-start(f32[64,64]{0,1:T(8,128)S(1)} %select_select_fusion.5), channel_id=1, source_target_pairs={{0,256},{16,272},{32,288},{48,304},{64,320},{80,336},{96,352},{112... | collective-permute-start | bytes 49160 | tf_op jit(solution)/shard_map/ppermute | solution.py:22
  6.0 0.7 collective-permute-start.6
  7.0 2.9 %collective-permute-start.8 = (f32[64,1280]{1,0:T(8,128)S(1)}, f32[64,1280]{1,0:T(8,128)S(1)}, u32[]{:S(2)}, u32[]{:S(2)}) collective-permute-start(f32[64,1280]{1,0:T(8,128)S(1)} %copy.11), channel_id=1, source_target_pairs={{0,1},{16,17},{32,33},{48,49},{64,65},{80,81},{96,97},{112,113},{1... | collective-permute-start | bytes 983048 | tf_op jit(solution)/shard_map/ppermute | solution.py:22
  7.7 2.1 %collective-permute-start.9 = (f32[64,192]{0,1:T(8,128)S(1)}, f32[64,192]{0,1:T(8,128)S(1)}, u32[]{:S(2)}, u32[]{:S(2)}) collective-permute-start(f32[64,192]{0,1:T(8,128)S(1)} %pad_maximum_fusion.3), channel_id=1, source_target_pairs={{16,17},{32,34},{48,51},{64,68},{80,85},{96,102},{112,119},{128,13... | collective-permute-start | bytes 147464 | tf_op jit(solution)/shard_map/ppermute | solution.py:64
  8.5 1.7 %collective-permute-start.10 = (f32[64,192]{0,1:T(8,128)S(1)}, f32[64,192]{0,1:T(8,128)S(1)}, u32[]{:S(2)}, u32[]{:S(2)}) collective-permute-start(f32[64,192]{0,1:T(8,128)S(1)} %pad_maximum_fusion.3), channel_id=1, source_target_pairs={{0,256},{16,273},{32,290},{48,307},{64,324},{80,341},{96,358},{112... | collective-permute-start | bytes 147464 | tf_op jit(solution)/shard_map/ppermute | solution.py:64
  9.1 1.0 collective-permute-start.11
  10.3 0.7 collective-permute-start.15
  11.0 1.6 %collective-permute-start.16 = (f32[64,448]{0,1:T(8,128)S(1)}, f32[64,448]{0,1:T(8,128)S(1)}, u32[]{:S(2)}, u32[]{:S(2)}) collective-permute-start(f32[64,448]{0,1:T(8,128)S(1)} %broadcast_select_fusion.4), channel_id=1, source_target_pairs={{0,32},{16,48},{256,288},{272,304},{512,544},{528,560},{17,49},{33... | collective-permute-start | bytes 344072 | tf_op jit(solution)/shard_map/ppermute | solution.py:22
  11.9 2.1 %collective-permute-start.12 = (f32[64,1280]{1,0:T(8,128)S(1)}, f32[64,1280]{1,0:T(8,128)S(1)}, u32[]{:S(2)}, u32[]{:S(2)}) collective-permute-start(f32[64,1280]{1,0:T(8,128)S(1)} %copy.13), channel_id=1, source_target_pairs={{0,2},{1,3},{16,18},{17,19},{32,34},{33,35},{48,50},{49,51},{64,66... | collective-permute-start | bytes 983048 | tf_op jit(solution)/shard_map/ppermute | solution.py:22
  12.7 54.7 %collective-permute-start.17 = (f32[64,448]{0,1:T(8,128)S(1)}, f32[64,448]{0,1:T(8,128)}, u32[]{:S(2)}, u32[]{:S(2)}) collective-permute-start(f32[64,448]{0,1:T(8,128)S(1)} %broadcast_select_fusion.5), channel_id=1, source_target_pairs={{0,64},{16,80},{32,96},{48,112},{256,320},{272,336},{288,352},{304... | collective-permute-start | bytes 344072 | tf_op jit(solution)/shard_map/ppermute | solution.py:22
  14.5 56.5 %collective-permute-start.13 = (f32[64,1280]{1,0:T(8,128)S(1)}, f32[64,1280]{1,0:T(8,128)S(1)}, u32[]{:S(2)}, u32[]{:S(2)}) collective-permute-start(f32[64,1280]{1,0:T(8,128)S(1)} %copy.15), channel_id=1, source_target_pairs={{0,4},{1,5},{2,6},{3,7},{16,20},{17,21},{18,22},{19,23},{32,36},{3... | collective-permute-start | bytes 983048 | tf_op jit(solution)/shard_map/ppermute | solution.py:22
  69.0 5.1 %collective-permute-start.18 = (f32[64,448]{0,1:T(8,128)}, f32[64,448]{0,1:T(8,128)}, u32[]{:S(2)}, u32[]{:S(2)}) collective-permute-start(f32[64,448]{0,1:T(8,128)} %broadcast_select_fusion.6), channel_id=1, source_target_pairs={{0,128},{16,144},{32,160},{48,176},{64,192},{80,208},{96,224},{112... | collective-permute-start | bytes 344072 | tf_op jit(solution)/shard_map/ppermute | solution.py:22
  72.4 36.0 %collective-permute-start.14 = (f32[64,1280]{1,0:T(8,128)S(1)}, f32[64,1280]{1,0:T(8,128)S(1)}, u32[]{:S(2)}, u32[]{:S(2)}) collective-permute-start(f32[64,1280]{1,0:T(8,128)S(1)} %copy.17), channel_id=1, source_target_pairs={{0,8},{1,9},{2,10},{3,11},{4,12},{5,13},{6,14},{7,15},{16,24},{17,... | collective-permute-start | bytes 983048 | tf_op jit(solution)/shard_map/ppermute | solution.py:22

commit v9 on v7

--- a/solution.py
+++ b/solution.py
@@ -47,13 +47,17 @@
     def col_groups(_):
         return [lambda m, r=r: r * n_col + m for r in range(n_row)]
 
-    panel_t, corner_t = lax.optimization_barrier((panel_t, corner_t))
     panel_t = tree_broadcast(panel_t, ("row", "col"), 2, col_groups, col_id, radix=2, have=1)
 
     rel = (row_id - col_id) % n_row
     my_j = rel // n_col
     is_src = rel % n_col == 0
-    first = jnp.concatenate([head, corner_t], axis=1)
+    corner = (corner_t + corner_t.T) / 2.0
+    factor = jnp.linalg.cholesky(corner)
+    inverse = lax.linalg.triangular_solve(
+        factor, jnp.eye(B, dtype=factor.dtype), left_side=True, lower=True
+    )
+    first = jnp.concatenate([head, factor.T, inverse], axis=1)
     pieces = []
     for c in range(n_src):
         pairs = []
@@ -67,7 +71,7 @@
         pieces.append(got)
     panel_t, pieces = lax.optimization_barrier((panel_t, pieces))
     panel_t = tree_broadcast(panel_t, ("row", "col"), n_col, col_groups, col_id, radix=2, have=2)
-    corner_t = pieces[0][:, window_cols:]
+    fpack = pieces[0][:, window_cols:]
     pieces = [p[:, :window_cols] for p in pieces]
     ordered = []
     for jj in range(n_src):
@@ -75,7 +79,7 @@
         for c in range(1, n_src):
             pick = jnp.where((my_j - jj) % n_src == c, pieces[c], pick)
         ordered.append(pick)
-    packet = jnp.concatenate(ordered + [corner_t], axis=1)
+    packet = jnp.concatenate(ordered + [fpack], axis=1)
     packet = jnp.where(is_src, packet, jnp.zeros_like(packet))
 
     def row_groups(_):
@@ -87,13 +91,8 @@
         return out
 
     packet = tree_broadcast(packet, ("row", "col"), n_col, row_groups, rel % n_col)
-
-    corner_t = packet[:, n_src * window_cols:]
-    corner = (corner_t + corner_t.T) / 2.0
-    factor = jnp.linalg.cholesky(corner)
-    inverse = lax.linalg.triangular_solve(
-        factor, jnp.eye(B, dtype=factor.dtype), left_side=True, lower=True
-    )
+    factor_t = packet[:, n_src * window_cols: n_src * window_cols + B]
+    inverse = packet[:, n_src * window_cols + B:]
 
     tiles = []
     for k in range(cols_dev // B):
@@ -108,11 +107,11 @@
 
     col_t = apply(window_t)
     col_t = jnp.concatenate(
-        [jnp.where(col_id == 0, factor.T, col_t[:, :B]), col_t[:, B:]], axis=1
+        [jnp.where(col_id == 0, factor_t, col_t[:, :B]), col_t[:, B:]], axis=1
     )
     lower_t = apply(panel_t)
     lower_t = jnp.concatenate(
-        [jnp.where(row_id == 0, factor.T, lower_t[:, :B]), lower_t[:, B:]], axis=1
+        [jnp.where(row_id == 0, factor_t, lower_t[:, :B]), lower_t[:, B:]], axis=1
     )
     change = lax.dot_general(
         lower_t,

time: 127 us -> 125 us (0.984)
  waiting for transfers between devices: 76 us -> 73.3 us
  other arithmetic: 14.2 us -> 15.7 us
    ppermute x16, waiting for transfers between devices: 76 us -> 73.3 us  [tree_broadcast(): got = lax.ppermute(x, axes, pairs)]
    unnamed x8 -> x10, local copies, waits for them, and re-layouts: 5.1 us -> 5.67 us
    another operation x2 -> x1, other arithmetic: 5.45 us -> 4.9 us  [shards(): lax.linalg.triangular_solve(factor, jnp.eye(B, dtype=factor.dtype), left_...]
where the time goes in v9:
time: 125 us
  waiting for transfers between devices  73.3 us (59%)
  other arithmetic  15.7 us (13%)
  local copies, waits for them, and re-layouts  14.9 us (12%)
  starting transfers between devices  14.7 us (12%)
  matrix products  5.23 us (4%)
    ppermute x16, waiting for transfers between devices, tree_broadcast(): got = lax.ppermute(x, axes, pairs)  73.3 us
    ppermute x16, starting transfers between devices, tree_broadcast(): got = lax.ppermute(x, axes, pairs)  12.6 us
    another operation x3, other arithmetic, shards(): factor = jnp.linalg.cholesky(corner)  6.52 us
    unnamed x10, local copies, waits for them, and re-layouts  5.67 us
    another operation x1, other arithmetic, shards(): lax.linalg.triangular_solve(factor, jnp.eye(B, dtype=factor.dtype), left_...  4.9 us
    ppermute x4, local copies, waits for them, and re-layouts, tree_broadcast(): got = lax.ppermute(x, axes, pairs)  3.58 us
    dot_general x1, matrix products, shards(): lax.dot_general(lower_t, col_t, (((0,), (0,)), ((), ())), precision=lax.P...  2.84 us
  transfers between devices with their start and end apart: 19, of which 2 were waited for; matrix products, arithmetic and copies ran while one was open for 20% of the time, Pallas kernels for 0%

profile of v9, /device:TPU:104, one launch (start us, length us, event | category | flops | bytes accessed | tf_op | source)
XLA Modules:
  0.0 124.6 jit_solution(9346911857885229608)
XLA Ops:
  0.0 1.1 slice_bitcast_fusion
  1.1 0.7 collective-permute-start.3
  1.8 0.7 collective-permute-start.2
  2.5 0.7 collective-permute-start.1
  3.2 0.7 collective-permute-start.6
  3.9 0.7 collective-permute-start.5
  4.6 0.7 collective-permute-start.4
  5.3 0.7 collective-permute-start.8
  6.0 0.7 collective-permute-start.7
  6.7 0.2 copy.12
  6.9 0.7 collective-permute-start
  7.8 5.8 %cholesky.20 = f32[64,64]{1,0:T(8,128)S(1)} custom-call(f32[64,64]{1,0:T(8,128)S(1)} %fusion.9), custom_call_target="Cholesky" | custom-call | tf_op jit(solution)/shard_map/jit(cholesky)/cholesky | solution.py:56
  13.7 0.6 compare_reduce_fusion
  14.4 0.7 fusion.14
  15.0 4.9 %custom-call.6 = f32[1,64,64]{1,2,0:T(8,128)S(1)} custom-call(f32[1,64,64]{2,1,0:T(8,128)S(1)} %get-tuple-element.20), custom_call_target="InvertDiagBlocksLowerTriangular" | custom-call | tf_op jit(solution)/shard_map/triangular_solve | solution.py:57
  19.9 0.2 fusion.7
  20.2 0.7 collective-permute-start.9
  21.0 0.7 collective-permute-start.10
  21.6 0.7 collective-permute-start.11
  22.4 0.2 copy.13
  22.6 1.2 broadcast_select_fusion.2
  23.9 0.7 collective-permute-start.12
  24.6 0.7 collective-permute-start.13
  25.5 0.7 collective-permute-start.16
  26.3 1.4 %collective-permute-start.14 = (f32[64,512]{0,1:T(8,128)S(1)}, f32[64,512]{0,1:T(8,128)}, u32[]{:S(2)}, u32[]{:S(2)}) collective-permute-start(f32[64,512]{0,1:T(8,128)S(1)} %broadcast_select_fusion.4), channel_id=1, source_target_pairs={{0,64},{16,80},{32,96},{48,112},{256,320},{272,336},{288,352},{304... | collective-permute-start | bytes 393224 | tf_op jit(solution)/shard_map/ppermute | solution.py:22
  27.6 1.9 %copy.28 = f32[1280,384]{0,1:T(8,128)S(1)} copy(f32[1280,384]{1,0:T(8,128)} %param.1) | data formatting | bytes 3932160 | tf_op args[0]
  29.6 1.1 copy.18
  30.7 1.3 %collective-permute-start.15 = (f32[64,512]{0,1:T(8,128)S(1)}, f32[64,512]{0,1:T(8,128)}, u32[]{:S(2)}, u32[]{:S(2)}) collective-permute-start(f32[64,512]{0,1:T(8,128)S(1)} %broadcast_select_fusion.5), channel_id=1, source_target_pairs={{0,128},{16,144},{32,160},{48,176},{64,192},{80,208},{96,224},{112... | collective-permute-start | bytes 393224 | tf_op jit(solution)/shard_map/ppermute | solution.py:22
  32.3 0.7 collective-permute-start.17
  33.0 52.8 %collective-permute-done.15 = f32[64,512]{0,1:T(8,128)} collective-permute-done((f32[64,512]{0,1:T(8,128)S(1)}, f32[64,512]{0,1:T(8,128)}, u32[]{:S(2)}, u32[]{:S(2)}) %collective-permute-start.15) | collective-permute-done | bytes 131104 | tf_op jit(solution)/shard_map/ppermute | solution.py:22
  85.8 1.0 broadcast_select_fusion.6
  86.8 0.6 slice_dynamic-update-slice_fusion.5
  87.4 0.6 slice_dynamic-update-slice_fusion.4
  88.0 0.6 slice_dynamic-update-slice_fusion.3
  88.6 0.6 slice_dynamic-update-slice_fusion.2
  89.2 0.6 slice_dynamic-update-slice_fusion.1
  89.8 1.1 copy.20
  91.2 1.3 %collective-permute-start.18 = (f32[64,1280]{1,0:T(8,128)S(1)}, f32[64,1280]{1,0:T(8,128)}, u32[]{:S(2)}, u32[]{:S(2)}) collective-permute-start(f32[64,1280]{1,0:T(8,128)S(1)} %copy.21), channel_id=1, source_target_pairs={{0,8},{1,9},{2,10},{3,11},{4,12},{5,13},{6,14},{7,15},{16,24},{17,... | collective-permute-start | bytes 983048 | tf_op jit(solution)/shard_map/ppermute | solution.py:22
  92.5 0.6 slice_dynamic-update-slice_fusion
  93.1 1.3 %fusion.11 = f32[64,384]{1,0:T(8,128)S(1)} fusion(f32[64,384]{0,1:T(8,128)} %slice_dynamic-update-slice_fusion, f32[64,512]{0,1:T(8,128)S(1)} %broadcast_select_fusion.6), kind=kOutput, calls=%fused_computation.45 | convolution fusion | flops 18874368 | bytes 229376 | tf_op jit(solution)/shard_map/dot_general | solution.py:105
  94.4 0.7 slice.107
  95.2 0.7 copy.32
  95.9 20.4 %collective-permute-done.18 = f32[64,1280]{1,0:T(8,128)} collective-permute-done((f32[64,1280]{1,0:T(8,128)S(1)}, f32[64,1280]{1,0:T(8,128)}, u32[]{:S(2)}, u32[]{:S(2)}) %collective-permute-start.18) | collective-permute-done | bytes 327712 | tf_op jit(solution)/shard_map/ppermute | solution.py:22
  116.3 1.2 copy.22
  117.5 0.8 fusion.1
  118.6 0.8 slice_select_fusion.1
  119.5 2.8 %fusion = f32[1280,384]{0,1:T(8,128)S(1)} fusion(f32[1280,384]{0,1:T(8,128)S(1)} %copy.28, pred[1280]{0:T(1024)(128)(4,1)S(1)} %fusion.15, f32[64,1216]{1,0:T(8,128)S(1)} %slice.99, f32[64,64]{1,0:T(8,128)S(1)} %copy.24, f32[64,320]{1,0:T(8,128)} %slice.107, f32[64,64]{1,0:T(8,128)S(1)} %copy.26), kind=kOutput, calls=%fused_computation.1 | convolution fusion | flops 378576896 | bytes 4359424 | tf_op jit(solution)/shard_map/dot_general | solution.py:116
  122.8 1.8 %copy.29 = f32[1280,384]{1,0:T(8,128)} copy(f32[1280,384]{0,1:T(8,128)S(1)} %pad_maximum_fusion) | data formatting | bytes 3932160 | tf_op jit(solution)/shard_map/concatenate | solution.py:127
  (51 shorter events, 2.0 us)
Async XLA Ops:
  1.1 2.0 %collective-permute-start.3 = (f32[64,64]{0,1:T(8,128)S(1)}, f32[64,64]{0,1:T(8,128)S(1)}, u32[]{:S(2)}, u32[]{:S(2)}) collective-permute-start(f32[64,64]{0,1:T(8,128)S(1)} %slice.95), channel_id=1, source_target_pairs={{0,16}} | collective-permute-start | bytes 49160 | tf_op jit(solution)/shard_map/ppermute | solution.py:22
  1.8 1.4 %collective-permute-start.2 = (f32[64,64]{0,1:T(8,128)S(1)}, f32[64,64]{0,1:T(8,128)S(1)}, u32[]{:S(2)}, u32[]{:S(2)}) collective-permute-start(f32[64,64]{0,1:T(8,128)S(1)} %slice.95), channel_id=1, source_target_pairs={{0,32}} | collective-permute-start | bytes 49160 | tf_op jit(solution)/shard_map/ppermute | solution.py:22
  2.5 0.7 collective-permute-start.1
  3.2 2.0 %collective-permute-start.6 = (f32[64,64]{0,1:T(8,128)S(1)}, f32[64,64]{0,1:T(8,128)S(1)}, u32[]{:S(2)}, u32[]{:S(2)}) collective-permute-start(f32[64,64]{0,1:T(8,128)S(1)} %select_select_fusion.6), channel_id=1, source_target_pairs={{0,64},{16,80},{32,96},{48,112}} | collective-permute-start | bytes 49160 | tf_op jit(solution)/shard_map/ppermute | solution.py:22
  3.9 1.4 %collective-permute-start.5 = (f32[64,64]{0,1:T(8,128)S(1)}, f32[64,64]{0,1:T(8,128)S(1)}, u32[]{:S(2)}, u32[]{:S(2)}) collective-permute-start(f32[64,64]{0,1:T(8,128)S(1)} %select_select_fusion.6), channel_id=1, source_target_pairs={{0,128},{16,144},{32,160},{48,176}} | collective-permute-start | bytes 49160 | tf_op jit(solution)/shard_map/ppermute | solution.py:22
  4.6 0.7 collective-permute-start.4
  5.3 2.3 %collective-permute-start.8 = (f32[64,64]{0,1:T(8,128)S(1)}, f32[64,64]{0,1:T(8,128)S(1)}, u32[]{:S(2)}, u32[]{:S(2)}) collective-permute-start(f32[64,64]{0,1:T(8,128)S(1)} %select_select_fusion.5), channel_id=1, source_target_pairs={{0,256},{16,272},{32,288},{48,304},{64,320},{80,336},{96,352},{112... | collective-permute-start | bytes 49160 | tf_op jit(solution)/shard_map/ppermute | solution.py:22
  6.0 1.6 %collective-permute-start.7 = (f32[64,64]{0,1:T(8,128)S(1)}, f32[64,64]{0,1:T(8,128)S(1)}, u32[]{:S(2)}, u32[]{:S(2)}) collective-permute-start(f32[64,64]{0,1:T(8,128)S(1)} %select_select_fusion.5), channel_id=1, source_target_pairs={{0,512},{16,528},{32,544},{48,560},{64,576},{80,592},{96,608},{112... | collective-permute-start | bytes 49160 | tf_op jit(solution)/shard_map/ppermute | solution.py:22
  6.9 15.5 %collective-permute-start = (f32[64,1280]{1,0:T(8,128)S(1)}, f32[64,1280]{1,0:T(8,128)S(1)}, u32[]{:S(2)}, u32[]{:S(2)}) collective-permute-start(f32[64,1280]{1,0:T(8,128)S(1)} %copy.12), channel_id=1, source_target_pairs={{0,1},{16,17},{32,33},{48,49},{64,65},{80,81},{96,97},{112,113},{1... | collective-permute-start | bytes 983048 | tf_op jit(solution)/shard_map/ppermute | solution.py:22
  20.2 2.2 %collective-permute-start.9 = (f32[64,256]{0,1:T(8,128)S(1)}, f32[64,256]{0,1:T(8,128)S(1)}, u32[]{:S(2)}, u32[]{:S(2)}) collective-permute-start(f32[64,256]{0,1:T(8,128)S(1)} %pad_maximum_fusion.3), channel_id=1, source_target_pairs={{16,17},{32,34},{48,51},{64,68},{80,85},{96,102},{112,119},{128,13... | collective-permute-start | bytes 196616 | tf_op jit(solution)/shard_map/ppermute | solution.py:68
  21.0 2.8 %collective-permute-start.10 = (f32[64,256]{0,1:T(8,128)S(1)}, f32[64,256]{0,1:T(8,128)S(1)}, u32[]{:S(2)}, u32[]{:S(2)}) collective-permute-start(f32[64,256]{0,1:T(8,128)S(1)} %pad_maximum_fusion.3), channel_id=1, source_target_pairs={{0,256},{16,273},{32,290},{48,307},{64,324},{80,341},{96,358},{112... | collective-permute-start | bytes 196616 | tf_op jit(solution)/shard_map/ppermute | solution.py:68
  21.6 2.1 %collective-permute-start.11 = (f32[64,256]{0,1:T(8,128)S(1)}, f32[64,256]{0,1:T(8,128)S(1)}, u32[]{:S(2)}, u32[]{:S(2)}) collective-permute-start(f32[64,256]{0,1:T(8,128)S(1)} %pad_maximum_fusion.3), channel_id=1, source_target_pairs={{0,512},{16,529},{32,546},{48,563},{64,580},{80,597},{96,614},{112... | collective-permute-start | bytes 196616 | tf_op jit(solution)/shard_map/ppermute | solution.py:68
  23.9 0.7 collective-permute-start.12
  24.6 1.6 %collective-permute-start.13 = (f32[64,512]{0,1:T(8,128)S(1)}, f32[64,512]{0,1:T(8,128)S(1)}, u32[]{:S(2)}, u32[]{:S(2)}) collective-permute-start(f32[64,512]{0,1:T(8,128)S(1)} %broadcast_select_fusion.3), channel_id=1, source_target_pairs={{0,32},{16,48},{256,288},{272,304},{512,544},{528,560},{17,49},{33... | collective-permute-start | bytes 393224 | tf_op jit(solution)/shard_map/ppermute | solution.py:22
  25.5 4.0 %collective-permute-start.16 = (f32[64,1280]{1,0:T(8,128)S(1)}, f32[64,1280]{1,0:T(8,128)S(1)}, u32[]{:S(2)}, u32[]{:S(2)}) collective-permute-start(f32[64,1280]{1,0:T(8,128)S(1)} %copy.17), channel_id=1, source_target_pairs={{0,2},{1,3},{16,18},{17,19},{32,34},{33,35},{48,50},{49,51},{64,66... | collective-permute-start | bytes 983048 | tf_op jit(solution)/shard_map/ppermute | solution.py:22
  26.3 4.4 %collective-permute-start.14 = (f32[64,512]{0,1:T(8,128)S(1)}, f32[64,512]{0,1:T(8,128)}, u32[]{:S(2)}, u32[]{:S(2)}) collective-permute-start(f32[64,512]{0,1:T(8,128)S(1)} %broadcast_select_fusion.4), channel_id=1, source_target_pairs={{0,64},{16,80},{32,96},{48,112},{256,320},{272,336},{288,352},{304... | collective-permute-start | bytes 393224 | tf_op jit(solution)/shard_map/ppermute | solution.py:22
  30.7 2.3 %copy-start = (f32[64,512]{0,1:T(8,128)}, f32[64,512]{0,1:T(8,128)S(1)}, u32[]{:S(2)}) copy-start(f32[64,512]{0,1:T(8,128)S(1)} %broadcast_select_fusion.5) | copy-start | bytes 393220
  30.7 55.1 %collective-permute-start.15 = (f32[64,512]{0,1:T(8,128)S(1)}, f32[64,512]{0,1:T(8,128)}, u32[]{:S(2)}, u32[]{:S(2)}) collective-permute-start(f32[64,512]{0,1:T(8,128)S(1)} %broadcast_select_fusion.5), channel_id=1, source_target_pairs={{0,128},{16,144},{32,160},{48,176},{64,192},{80,208},{96,224},{112... | collective-permute-start | bytes 393224 | tf_op jit(solution)/shard_map/ppermute | solution.py:22
  32.3 57.5 %collective-permute-start.17 = (f32[64,1280]{1,0:T(8,128)S(1)}, f32[64,1280]{1,0:T(8,128)S(1)}, u32[]{:S(2)}, u32[]{:S(2)}) collective-permute-start(f32[64,1280]{1,0:T(8,128)S(1)} %copy.19), channel_id=1, source_target_pairs={{0,4},{1,5},{2,6},{3,7},{16,20},{17,21},{18,22},{19,23},{32,36},{3... | collective-permute-start | bytes 983048 | tf_op jit(solution)/shard_map/ppermute | solution.py:22
  91.2 25.1 %collective-permute-start.18 = (f32[64,1280]{1,0:T(8,128)S(1)}, f32[64,1280]{1,0:T(8,128)}, u32[]{:S(2)}, u32[]{:S(2)}) collective-permute-start(f32[64,1280]{1,0:T(8,128)S(1)} %copy.21), channel_id=1, source_target_pairs={{0,8},{1,9},{2,10},{3,11},{4,12},{5,13},{6,14},{7,15},{16,24},{17,... | collective-permute-start | bytes 983048 | tf_op jit(solution)/shard_map/ppermute | solution.py:22

commit v10 on v9

--- a/solution.py
+++ b/solution.py
@@ -70,7 +70,7 @@
             got = jnp.where(col_id == 0, first, got)
         pieces.append(got)
     panel_t, pieces = lax.optimization_barrier((panel_t, pieces))
-    panel_t = tree_broadcast(panel_t, ("row", "col"), n_col, col_groups, col_id, radix=2, have=2)
+    panel_t = tree_broadcast(panel_t, ("row", "col"), n_col // 2, col_groups, col_id, radix=2, have=2)
     fpack = pieces[0][:, window_cols:]
     pieces = [p[:, :window_cols] for p in pieces]
     ordered = []
@@ -91,6 +91,8 @@
         return out
 
     packet = tree_broadcast(packet, ("row", "col"), n_col, row_groups, rel % n_col)
+    panel_t = tree_broadcast(panel_t, ("row", "col"), n_col, col_groups, col_id, radix=2, have=n_col // 2)
+    panel_t, packet = lax.optimization_barrier((panel_t, packet))
     factor_t = packet[:, n_src * window_cols: n_src * window_cols + B]
     inverse = packet[:, n_src * window_cols + B:]
 

time: 125 us -> 120 us (0.960)
  the two profiles are of different devices: /device:TPU:104 before, /device:TPU:42 now
where the time goes in v10:
time: 120 us; the launch traced here: 119 us
  waiting for transfers between devices  75.3 us (63%)
  other arithmetic  15 us (12%)
  starting transfers between devices  14.6 us (12%)
  local copies, waits for them, and re-layouts  9.94 us (8%)
  matrix products  3.45 us (3%)
    ppermute x16, waiting for transfers between devices, tree_broadcast(): got = lax.ppermute(x, axes, pairs)  75.3 us
    ppermute x16, starting transfers between devices, tree_broadcast(): got = lax.ppermute(x, axes, pairs)  12.6 us
    another operation x3, other arithmetic, shards(): factor = jnp.linalg.cholesky(corner)  6.52 us
    another operation x1, other arithmetic, shards(): lax.linalg.triangular_solve(factor, jnp.eye(B, dtype=factor.dtype), left_...  4.9 us
    ppermute x4, local copies, waits for them, and re-layouts, tree_broadcast(): got = lax.ppermute(x, axes, pairs)  2.73 us
    select_n x11, other arithmetic, tree_broadcast(): fresh = jnp.where(take, got, fresh)  2.49 us
  transfers between devices with their start and end apart: 19, of which 2 were waited for; matrix products, arithmetic and copies ran while one was open for 17% of the time, Pallas kernels for 0%

profile of v10, /device:TPU:42, one launch (start us, length us, event | category | flops | bytes accessed | tf_op | source)
XLA Modules:
  0.0 119.2 jit_solution(3132425157313781210)
XLA Ops:
  0.0 1.1 slice_bitcast_fusion
  1.1 0.7 collective-permute-start.3
  1.8 0.7 collective-permute-start.2
  2.5 0.7 collective-permute-start.1
  3.2 0.7 collective-permute-start.6
  3.9 0.7 collective-permute-start.5
  4.6 0.7 collective-permute-start.4
  5.3 0.7 collective-permute-start.8
  6.0 0.7 collective-permute-start.7
  6.7 0.2 copy.12
  6.9 0.7 collective-permute-start
  7.8 5.8 %cholesky.20 = f32[64,64]{1,0:T(8,128)S(1)} custom-call(f32[64,64]{1,0:T(8,128)S(1)} %fusion.6), custom_call_target="Cholesky" | custom-call | tf_op jit(solution)/shard_map/jit(cholesky)/cholesky | solution.py:56
  13.7 0.6 compare_reduce_fusion
  14.4 0.7 fusion.12
  15.0 4.9 %custom-call.6 = f32[1,64,64]{1,2,0:T(8,128)S(1)} custom-call(f32[1,64,64]{2,1,0:T(8,128)S(1)} %get-tuple-element.24), custom_call_target="InvertDiagBlocksLowerTriangular" | custom-call | tf_op jit(solution)/shard_map/triangular_solve | solution.py:57
  19.9 0.2 fusion.4
  20.2 0.7 collective-permute-start.9
  21.0 0.7 collective-permute-start.10
  21.6 0.7 collective-permute-start.11
  22.4 0.2 copy.13
  22.6 1.2 broadcast_select_fusion
  23.9 0.7 collective-permute-start.15
  24.6 0.7 collective-permute-start.16
  25.3 0.2 copy.17
  25.5 0.7 collective-permute-start.12
  26.3 1.4 %collective-permute-start.17 = (f32[64,512]{0,1:T(8,128)S(1)}, f32[64,512]{0,1:T(8,128)}, u32[]{:S(2)}, u32[]{:S(2)}) collective-permute-start(f32[64,512]{0,1:T(8,128)S(1)} %broadcast_select_fusion.5), channel_id=1, source_target_pairs={{0,64},{16,80},{32,96},{48,112},{256,320},{272,336},{288,352},{304... | collective-permute-start | bytes 393224 | tf_op jit(solution)/shard_map/ppermute | solution.py:22
  27.6 0.2 copy.18
  27.9 0.9 copy.19
  28.9 0.7 collective-permute-start.13
  29.6 1.9 %copy.28 = f32[1280,384]{0,1:T(8,128)S(1)} copy(f32[1280,384]{1,0:T(8,128)} %param.1) | data formatting | bytes 3932160 | tf_op args[0]
  31.6 1.3 %collective-permute-start.18 = (f32[64,512]{0,1:T(8,128)S(1)}, f32[64,512]{0,1:T(8,128)}, u32[]{:S(2)}, u32[]{:S(2)}) collective-permute-start(f32[64,512]{0,1:T(8,128)S(1)} %broadcast_select_fusion.6), channel_id=1, source_target_pairs={{0,128},{16,144},{32,160},{48,176},{64,192},{80,208},{96,224},{112... | collective-permute-start | bytes 393224 | tf_op jit(solution)/shard_map/ppermute | solution.py:22
  32.9 1.1 copy.20
  34.0 0.2 copy.21
  34.3 1.3 %collective-permute-start.14 = (f32[64,1280]{1,0:T(8,128)S(1)}, f32[64,1280]{1,0:T(8,128)}, u32[]{:S(2)}, u32[]{:S(2)}) collective-permute-start(f32[64,1280]{1,0:T(8,128)S(1)} %copy.21), channel_id=1, source_target_pairs={{0,8},{1,9},{2,10},{3,11},{4,12},{5,13},{6,14},{7,15},{16,24},{17,... | collective-permute-start | bytes 983048 | tf_op jit(solution)/shard_map/ppermute | solution.py:22
  35.6 45.6 %collective-permute-done.18 = f32[64,512]{0,1:T(8,128)} collective-permute-done((f32[64,512]{0,1:T(8,128)S(1)}, f32[64,512]{0,1:T(8,128)}, u32[]{:S(2)}, u32[]{:S(2)}) %collective-permute-start.18) | collective-permute-done | bytes 131104 | tf_op jit(solution)/shard_map/ppermute | solution.py:22
  81.2 1.0 broadcast_select_fusion.7
  82.2 29.7 %collective-permute-done.14 = f32[64,1280]{1,0:T(8,128)} collective-permute-done((f32[64,1280]{1,0:T(8,128)S(1)}, f32[64,1280]{1,0:T(8,128)}, u32[]{:S(2)}, u32[]{:S(2)}) %collective-permute-start.14) | collective-permute-done | bytes 327712 | tf_op jit(solution)/shard_map/ppermute | solution.py:22
  111.8 1.2 %copy.22 = f32[64,1280]{0,1:T(8,128)S(1)} copy(f32[64,1280]{1,0:T(8,128)} %collective-permute-done.14) | data formatting | bytes 655360 | tf_op jit(solution)/shard_map/ppermute | solution.py:22
  113.1 0.9 fusion.10
  114.0 0.1 slice.97
  114.2 0.4 fusion.8
  114.7 0.1 slice.99
  114.8 0.1 copy.32
  115.1 1.9 %fusion = f32[1280,384]{0,1:T(8,128)S(1)} fusion(f32[1280,384]{0,1:T(8,128)S(1)} %copy.28, pred[1280]{0:T(1024)(128)(4,1)S(1)} %fusion.13, f32[64,1216]{1,0:T(8,128)S(1)} %slice.97, f32[64,64]{1,0:T(8,128)S(1)} %copy.24, f32[64,320]{1,0:T(8,128)S(1)} %slice.99, f32[64,64]{1,0:T(8,128)S(1)} %copy.26), kind=kOutput, calls=%fused_computation.1 | convolution fusion | flops 378576896 | bytes 4359424 | tf_op jit(solution)/shard_map/dot_general | solution.py:118
  117.0 0.2 slice_select_fusion
  117.2 0.1 slice.101
  117.3 0.1 pad_maximum_fusion
  117.4 1.8 %copy.29 = f32[1280,384]{1,0:T(8,128)} copy(f32[1280,384]{0,1:T(8,128)S(1)} %pad_maximum_fusion) | data formatting | bytes 3932160 | tf_op jit(solution)/shard_map/concatenate | solution.py:129
  (52 shorter events, 1.0 us)
Async XLA Ops:
  1.1 2.0 %collective-permute-start.3 = (f32[64,64]{0,1:T(8,128)S(1)}, f32[64,64]{0,1:T(8,128)S(1)}, u32[]{:S(2)}, u32[]{:S(2)}) collective-permute-start(f32[64,64]{0,1:T(8,128)S(1)} %slice.95), channel_id=1, source_target_pairs={{0,16}} | collective-permute-start | bytes 49160 | tf_op jit(solution)/shard_map/ppermute | solution.py:22
  1.8 1.4 %collective-permute-start.2 = (f32[64,64]{0,1:T(8,128)S(1)}, f32[64,64]{0,1:T(8,128)S(1)}, u32[]{:S(2)}, u32[]{:S(2)}) collective-permute-start(f32[64,64]{0,1:T(8,128)S(1)} %slice.95), channel_id=1, source_target_pairs={{0,32}} | collective-permute-start | bytes 49160 | tf_op jit(solution)/shard_map/ppermute | solution.py:22
  2.5 0.7 collective-permute-start.1
  3.2 2.0 %collective-permute-start.6 = (f32[64,64]{0,1:T(8,128)S(1)}, f32[64,64]{0,1:T(8,128)S(1)}, u32[]{:S(2)}, u32[]{:S(2)}) collective-permute-start(f32[64,64]{0,1:T(8,128)S(1)} %select_select_fusion.6), channel_id=1, source_target_pairs={{0,64},{16,80},{32,96},{48,112}} | collective-permute-start | bytes 49160 | tf_op jit(solution)/shard_map/ppermute | solution.py:22
  3.9 1.4 %collective-permute-start.5 = (f32[64,64]{0,1:T(8,128)S(1)}, f32[64,64]{0,1:T(8,128)S(1)}, u32[]{:S(2)}, u32[]{:S(2)}) collective-permute-start(f32[64,64]{0,1:T(8,128)S(1)} %select_select_fusion.6), channel_id=1, source_target_pairs={{0,128},{16,144},{32,160},{48,176}} | collective-permute-start | bytes 49160 | tf_op jit(solution)/shard_map/ppermute | solution.py:22
  4.6 0.7 collective-permute-start.4
  5.3 2.3 %collective-permute-start.8 = (f32[64,64]{0,1:T(8,128)S(1)}, f32[64,64]{0,1:T(8,128)S(1)}, u32[]{:S(2)}, u32[]{:S(2)}) collective-permute-start(f32[64,64]{0,1:T(8,128)S(1)} %select_select_fusion.5), channel_id=1, source_target_pairs={{0,256},{16,272},{32,288},{48,304},{64,320},{80,336},{96,352},{112... | collective-permute-start | bytes 49160 | tf_op jit(solution)/shard_map/ppermute | solution.py:22
  6.0 1.6 %collective-permute-start.7 = (f32[64,64]{0,1:T(8,128)S(1)}, f32[64,64]{0,1:T(8,128)S(1)}, u32[]{:S(2)}, u32[]{:S(2)}) collective-permute-start(f32[64,64]{0,1:T(8,128)S(1)} %select_select_fusion.5), channel_id=1, source_target_pairs={{0,512},{16,528},{32,544},{48,560},{64,576},{80,592},{96,608},{112... | collective-permute-start | bytes 49160 | tf_op jit(solution)/shard_map/ppermute | solution.py:22
  6.9 15.5 %collective-permute-start = (f32[64,1280]{1,0:T(8,128)S(1)}, f32[64,1280]{1,0:T(8,128)S(1)}, u32[]{:S(2)}, u32[]{:S(2)}) collective-permute-start(f32[64,1280]{1,0:T(8,128)S(1)} %copy.12), channel_id=1, source_target_pairs={{0,1},{16,17},{32,33},{48,49},{64,65},{80,81},{96,97},{112,113},{1... | collective-permute-start | bytes 983048 | tf_op jit(solution)/shard_map/ppermute | solution.py:22
  20.2 2.2 %collective-permute-start.9 = (f32[64,256]{0,1:T(8,128)S(1)}, f32[64,256]{0,1:T(8,128)S(1)}, u32[]{:S(2)}, u32[]{:S(2)}) collective-permute-start(f32[64,256]{0,1:T(8,128)S(1)} %pad_maximum_fusion.3), channel_id=1, source_target_pairs={{16,17},{32,34},{48,51},{64,68},{80,85},{96,102},{112,119},{128,13... | collective-permute-start | bytes 196616 | tf_op jit(solution)/shard_map/ppermute | solution.py:68
  21.0 2.8 %collective-permute-start.10 = (f32[64,256]{0,1:T(8,128)S(1)}, f32[64,256]{0,1:T(8,128)S(1)}, u32[]{:S(2)}, u32[]{:S(2)}) collective-permute-start(f32[64,256]{0,1:T(8,128)S(1)} %pad_maximum_fusion.3), channel_id=1, source_target_pairs={{0,256},{16,273},{32,290},{48,307},{64,324},{80,341},{96,358},{112... | collective-permute-start | bytes 196616 | tf_op jit(solution)/shard_map/ppermute | solution.py:68
  21.6 2.1 %collective-permute-start.11 = (f32[64,256]{0,1:T(8,128)S(1)}, f32[64,256]{0,1:T(8,128)S(1)}, u32[]{:S(2)}, u32[]{:S(2)}) collective-permute-start(f32[64,256]{0,1:T(8,128)S(1)} %pad_maximum_fusion.3), channel_id=1, source_target_pairs={{0,512},{16,529},{32,546},{48,563},{64,580},{80,597},{96,614},{112... | collective-permute-start | bytes 196616 | tf_op jit(solution)/shard_map/ppermute | solution.py:68
  23.9 0.7 collective-permute-start.15
  24.6 1.6 %collective-permute-start.16 = (f32[64,512]{0,1:T(8,128)S(1)}, f32[64,512]{0,1:T(8,128)S(1)}, u32[]{:S(2)}, u32[]{:S(2)}) collective-permute-start(f32[64,512]{0,1:T(8,128)S(1)} %broadcast_select_fusion.4), channel_id=1, source_target_pairs={{0,32},{16,48},{256,288},{272,304},{512,544},{528,560},{17,49},{33... | collective-permute-start | bytes 393224 | tf_op jit(solution)/shard_map/ppermute | solution.py:22
  25.5 2.1 %collective-permute-start.12 = (f32[64,1280]{1,0:T(8,128)S(1)}, f32[64,1280]{1,0:T(8,128)S(1)}, u32[]{:S(2)}, u32[]{:S(2)}) collective-permute-start(f32[64,1280]{1,0:T(8,128)S(1)} %copy.17), channel_id=1, source_target_pairs={{0,2},{1,3},{16,18},{17,19},{32,34},{33,35},{48,50},{49,51},{64,66... | collective-permute-start | bytes 983048 | tf_op jit(solution)/shard_map/ppermute | solution.py:22
  26.3 5.2 %collective-permute-start.17 = (f32[64,512]{0,1:T(8,128)S(1)}, f32[64,512]{0,1:T(8,128)}, u32[]{:S(2)}, u32[]{:S(2)}) collective-permute-start(f32[64,512]{0,1:T(8,128)S(1)} %broadcast_select_fusion.5), channel_id=1, source_target_pairs={{0,64},{16,80},{32,96},{48,112},{256,320},{272,336},{288,352},{304... | collective-permute-start | bytes 393224 | tf_op jit(solution)/shard_map/ppermute | solution.py:22
  28.9 4.0 %collective-permute-start.13 = (f32[64,1280]{1,0:T(8,128)}, f32[64,1280]{1,0:T(8,128)S(1)}, u32[]{:S(2)}, u32[]{:S(2)}) collective-permute-start(f32[64,1280]{1,0:T(8,128)} %copy.19), channel_id=1, source_target_pairs={{0,4},{1,5},{2,6},{3,7},{16,20},{17,21},{18,22},{19,23},{32,36},{3... | collective-permute-start | bytes 983048 | tf_op jit(solution)/shard_map/ppermute | solution.py:22
  31.6 4.0 %copy-start = (f32[64,512]{0,1:T(8,128)}, f32[64,512]{0,1:T(8,128)S(1)}, u32[]{:S(2)}) copy-start(f32[64,512]{0,1:T(8,128)S(1)} %broadcast_select_fusion.6) | copy-start | bytes 393220
  31.6 49.6 %collective-permute-start.18 = (f32[64,512]{0,1:T(8,128)S(1)}, f32[64,512]{0,1:T(8,128)}, u32[]{:S(2)}, u32[]{:S(2)}) collective-permute-start(f32[64,512]{0,1:T(8,128)S(1)} %broadcast_select_fusion.6), channel_id=1, source_target_pairs={{0,128},{16,144},{32,160},{48,176},{64,192},{80,208},{96,224},{112... | collective-permute-start | bytes 393224 | tf_op jit(solution)/shard_map/ppermute | solution.py:22
  34.3 77.6 %collective-permute-start.14 = (f32[64,1280]{1,0:T(8,128)S(1)}, f32[64,1280]{1,0:T(8,128)}, u32[]{:S(2)}, u32[]{:S(2)}) collective-permute-start(f32[64,1280]{1,0:T(8,128)S(1)} %copy.21), channel_id=1, source_target_pairs={{0,8},{1,9},{2,10},{3,11},{4,12},{5,13},{6,14},{7,15},{16,24},{17,... | collective-permute-start | bytes 983048 | tf_op jit(solution)/shard_map/ppermute | solution.py:22

commit v11 on v10

--- a/solution.py
+++ b/solution.py
@@ -39,11 +39,6 @@
     panel_t = matrix[:, :B].T
     head = panel_t[:, :window_cols]
 
-    def col0_group(_):
-        return [lambda m: m * n_col]
-
-    corner_t = tree_broadcast(panel_t[:, :B], ("row", "col"), n_row, col0_group, row_id, radix=4)
-
     def col_groups(_):
         return [lambda m, r=r: r * n_col + m for r in range(n_row)]
 
@@ -52,12 +47,6 @@
     rel = (row_id - col_id) % n_row
     my_j = rel // n_col
     is_src = rel % n_col == 0
-    corner = (corner_t + corner_t.T) / 2.0
-    factor = jnp.linalg.cholesky(corner)
-    inverse = lax.linalg.triangular_solve(
-        factor, jnp.eye(B, dtype=factor.dtype), left_side=True, lower=True
-    )
-    first = jnp.concatenate([head, factor.T, inverse], axis=1)
     pieces = []
     for c in range(n_src):
         pairs = []
@@ -65,14 +54,27 @@
             q = r % n_col
             if c or q:
                 pairs.append((r * n_col, ((r + n_col * c) % n_row) * n_col + q))
-        got = lax.ppermute(first, ("row", "col"), pairs)
+        got = lax.ppermute(head, ("row", "col"), pairs)
         if c == 0:
-            got = jnp.where(col_id == 0, first, got)
+            got = jnp.where(col_id == 0, head, got)
         pieces.append(got)
+
+    corner_t = panel_t[:, :B]
+    corner = (corner_t + corner_t.T) / 2.0
+    factor = jnp.linalg.cholesky(corner)
+    inverse = lax.linalg.triangular_solve(
+        factor, jnp.eye(B, dtype=factor.dtype), left_side=True, lower=True
+    )
+    fpack = jnp.concatenate([factor.T, inverse], axis=1)
+
+    def src_group(_):
+        return [lambda m: m * n_col + m % n_col]
+
+    src_member = jnp.where(is_src, row_id, n_row)
+    fpack = tree_broadcast(fpack, ("row", "col"), n_row, src_group, src_member, radix=4)
+
     panel_t, pieces = lax.optimization_barrier((panel_t, pieces))
     panel_t = tree_broadcast(panel_t, ("row", "col"), n_col // 2, col_groups, col_id, radix=2, have=2)
-    fpack = pieces[0][:, window_cols:]
-    pieces = [p[:, :window_cols] for p in pieces]
     ordered = []
     for jj in range(n_src):
         pick = pieces[0]

time: 120 us -> 136 us (1.13)
  the two profiles are of different devices: /device:TPU:42 before, /device:TPU:44 now
where the time goes in v11:
time: 136 us; the launch traced here: 135 us
  waiting for transfers between devices  91.4 us (67%)
  other arithmetic  15.7 us (12%)
  starting transfers between devices  14.6 us (11%)
  local copies, waits for them, and re-layouts  9.28 us (7%)
  matrix products  3.45 us (3%)
    ppermute x16, waiting for transfers between devices, tree_broadcast(): got = lax.ppermute(x, axes, pairs)  91.4 us
    ppermute x16, starting transfers between devices, tree_broadcast(): got = lax.ppermute(x, axes, pairs)  12.7 us
    another operation x3, other arithmetic, shards(): factor = jnp.linalg.cholesky(corner)  6.53 us
    another operation x1, other arithmetic, shards(): lax.linalg.triangular_solve(factor, jnp.eye(B, dtype=factor.dtype), left_...  4.9 us
    select_n x11, other arithmetic, tree_broadcast(): fresh = jnp.where(take, got, fresh)  3.21 us
    ppermute x4, local copies, waits for them, and re-layouts, tree_broadcast(): got = lax.ppermute(x, axes, pairs)  2.73 us
  transfers between devices with their start and end apart: 19, of which 2 were waited for; matrix products, arithmetic and copies ran while one was open for 4% of the time, Pallas kernels for 0%

profile of v11, /device:TPU:44, one launch (start us, length us, event | category | flops | bytes accessed | tf_op | source)
XLA Modules:
  0.0 135.3 jit_solution(15934524567854853958)
XLA Ops:
  0.0 1.1 slice_bitcast_fusion
  1.1 0.2 copy.13
  1.4 0.7 collective-permute-start
  2.1 0.2 copy.14
  2.3 1.2 broadcast_select_fusion
  3.7 5.9 %cholesky.20 = f32[64,64]{1,0:T(8,128)S(1)} custom-call(f32[64,64]{1,0:T(8,128)S(1)} %copy.23), custom_call_target="Cholesky" | custom-call | tf_op jit(solution)/shard_map/jit(cholesky)/cholesky | solution.py:64
  9.6 0.6 compare_reduce_fusion
  10.3 0.7 fusion.12
  10.9 4.9 %custom-call.6 = f32[1,64,64]{1,2,0:T(8,128)S(1)} custom-call(f32[1,64,64]{2,1,0:T(8,128)S(1)} %get-tuple-element.23), custom_call_target="InvertDiagBlocksLowerTriangular" | custom-call | tf_op jit(solution)/shard_map/triangular_solve | solution.py:65
  15.8 0.2 fusion.4
  16.1 0.7 collective-permute-start.9
  16.8 0.7 collective-permute-start.8
  17.4 0.7 collective-permute-start.7
  18.1 0.7 collective-permute-start.2
  18.8 0.7 collective-permute-start.3
  19.6 0.7 collective-permute-start.1
  20.4 0.7 collective-permute-start.12
  21.0 0.7 collective-permute-start.11
  21.7 0.7 collective-permute-start.10
  22.5 0.7 collective-permute-start.14
  23.2 0.7 collective-permute-start.13
  23.9 0.7 collective-permute-start.15
  24.6 0.2 copy.15
  24.9 0.7 collective-permute-start.4
  25.6 0.7 collective-permute-start.16
  26.3 0.2 copy.16
  26.6 1.4 %collective-permute-start.17 = (f32[64,512]{0,1:T(8,128)S(1)}, f32[64,512]{0,1:T(8,128)}, u32[]{:S(2)}, u32[]{:S(2)}) collective-permute-start(f32[64,512]{0,1:T(8,128)S(1)} %broadcast_select_fusion.5), channel_id=1, source_target_pairs={{0,64},{16,80},{32,96},{48,112},{256,320},{272,336},{288,352},{304... | collective-permute-start | bytes 393224 | tf_op jit(solution)/shard_map/ppermute | solution.py:22
  28.0 0.2 copy.17
  28.3 0.7 collective-permute-start.5
  29.0 1.9 %copy.30 = f32[1280,384]{0,1:T(8,128)S(1)} copy(f32[1280,384]{1,0:T(8,128)} %param.1) | data formatting | bytes 3932160 | tf_op args[0]
  30.9 0.7 broadcast_select_fusion.6
  31.6 1.3 collective-permute-start.18
  32.9 1.1 copy.18
  34.1 0.2 copy.19
  34.3 1.3 collective-permute-start.6
  35.6 66.2 %collective-permute-done.18 = f32[64,512]{0,1:T(8,128)} collective-permute-done((f32[64,512]{0,1:T(8,128)}, f32[64,512]{0,1:T(8,128)}, u32[]{:S(2)}, u32[]{:S(2)}) %collective-permute-start.18) | collective-permute-done | bytes 131104 | tf_op jit(solution)/shard_map/ppermute | solution.py:22
  101.8 1.0 broadcast_select_fusion.7
  102.8 25.2 %collective-permute-done.6 = f32[64,1280]{1,0:T(8,128)} collective-permute-done((f32[64,1280]{1,0:T(8,128)S(1)}, f32[64,1280]{1,0:T(8,128)}, u32[]{:S(2)}, u32[]{:S(2)}) %collective-permute-start.6) | collective-permute-done | bytes 327712 | tf_op jit(solution)/shard_map/ppermute | solution.py:22
  128.0 1.2 copy.20
  129.2 0.9 fusion.10
  130.1 0.1 slice.81
  130.3 0.4 fusion.8
  130.8 0.1 slice.83
  131.2 1.9 %fusion = f32[1280,384]{0,1:T(8,128)S(1)} fusion(f32[1280,384]{0,1:T(8,128)S(1)} %copy.30, pred[1280]{0:T(1024)(128)(4,1)S(1)} %fusion.13, f32[64,1216]{1,0:T(8,128)S(1)} %slice.81, f32[64,64]{1,0:T(8,128)S(1)} %copy.26, f32[64,320]{1,0:T(8,128)S(1)} %slice.83, f32[64,64]{1,0:T(8,128)S(1)} %copy.28), kind=kOutput, calls=%fused_computation.1 | convolution fusion | flops 378576896 | bytes 4359424 | tf_op jit(solution)/shard_map/dot_general | solution.py:120
  133.1 0.2 slice_select_fusion
  133.3 0.1 slice.85
  133.4 0.1 pad_maximum_fusion
  133.5 1.8 %copy.31 = f32[1280,384]{1,0:T(8,128)} copy(f32[1280,384]{0,1:T(8,128)S(1)} %pad_maximum_fusion) | data formatting | bytes 3932160 | tf_op jit(solution)/shard_map/concatenate | solution.py:131
  (51 shorter events, 1.1 us)
Async XLA Ops:
  1.4 0.7 collective-permute-start
  16.1 3.5 %collective-permute-start.9 = (f32[64,128]{0,1:T(8,128)S(1)}, f32[64,128]{0,1:T(8,128)S(1)}, u32[]{:S(2)}, u32[]{:S(2)}) collective-permute-start(f32[64,128]{0,1:T(8,128)S(1)} %pad_maximum_fusion.3), channel_id=1, source_target_pairs={{0,17}} | collective-permute-start | bytes 98312 | tf_op jit(solution)/shard_map/ppermute | solution.py:22
  16.8 3.5 %collective-permute-start.8 = (f32[64,128]{0,1:T(8,128)S(1)}, f32[64,128]{0,1:T(8,128)S(1)}, u32[]{:S(2)}, u32[]{:S(2)}) collective-permute-start(f32[64,128]{0,1:T(8,128)S(1)} %pad_maximum_fusion.3), channel_id=1, source_target_pairs={{0,34}} | collective-permute-start | bytes 98312 | tf_op jit(solution)/shard_map/ppermute | solution.py:22
  17.4 2.9 %collective-permute-start.7 = (f32[64,128]{0,1:T(8,128)S(1)}, f32[64,128]{0,1:T(8,128)S(1)}, u32[]{:S(2)}, u32[]{:S(2)}) collective-permute-start(f32[64,128]{0,1:T(8,128)S(1)} %pad_maximum_fusion.3), channel_id=1, source_target_pairs={{0,51}} | collective-permute-start | bytes 98312 | tf_op jit(solution)/shard_map/ppermute | solution.py:22
  18.1 4.3 %collective-permute-start.2 = (f32[64,128]{0,1:T(8,128)S(1)}, f32[64,128]{0,1:T(8,128)S(1)}, u32[]{:S(2)}, u32[]{:S(2)}) collective-permute-start(f32[64,128]{0,1:T(8,128)S(1)} %slice.78), channel_id=1, source_target_pairs={{0,256},{16,273},{32,290},{48,307},{64,324},{80,341},{96,358},{112... | collective-permute-start | bytes 98312 | tf_op jit(solution)/shard_map/ppermute | solution.py:57
  18.8 3.6 %collective-permute-start.3 = (f32[64,128]{0,1:T(8,128)S(1)}, f32[64,128]{0,1:T(8,128)S(1)}, u32[]{:S(2)}, u32[]{:S(2)}) collective-permute-start(f32[64,128]{0,1:T(8,128)S(1)} %slice.78), channel_id=1, source_target_pairs={{0,512},{16,529},{32,546},{48,563},{64,580},{80,597},{96,614},{112... | collective-permute-start | bytes 98312 | tf_op jit(solution)/shard_map/ppermute | solution.py:57
  19.6 2.1 %collective-permute-start.1 = (f32[64,128]{0,1:T(8,128)S(1)}, f32[64,128]{0,1:T(8,128)S(1)}, u32[]{:S(2)}, u32[]{:S(2)}) collective-permute-start(f32[64,128]{0,1:T(8,128)S(1)} %slice.78), channel_id=1, source_target_pairs={{16,17},{32,34},{48,51},{64,68},{80,85},{96,102},{112,119},{128,13... | collective-permute-start | bytes 98312 | tf_op jit(solution)/shard_map/ppermute | solution.py:57
  20.4 2.1 %collective-permute-start.12 = (f32[64,128]{0,1:T(8,128)S(1)}, f32[64,128]{0,1:T(8,128)S(1)}, u32[]{:S(2)}, u32[]{:S(2)}) collective-permute-start(f32[64,128]{0,1:T(8,128)S(1)} %select_select_fusion.2), channel_id=1, source_target_pairs={{0,68},{17,85},{34,102},{51,119}} | collective-permute-start | bytes 98312 | tf_op jit(solution)/shard_map/ppermute | solution.py:22
  21.0 1.4 %collective-permute-start.11 = (f32[64,128]{0,1:T(8,128)S(1)}, f32[64,128]{0,1:T(8,128)S(1)}, u32[]{:S(2)}, u32[]{:S(2)}) collective-permute-start(f32[64,128]{0,1:T(8,128)S(1)} %select_select_fusion.2), channel_id=1, source_target_pairs={{0,136},{17,153},{34,170},{51,187}} | collective-permute-start | bytes 98312 | tf_op jit(solution)/shard_map/ppermute | solution.py:22
  21.7 0.7 collective-permute-start.10
  22.5 1.4 %collective-permute-start.14 = (f32[64,128]{0,1:T(8,128)S(1)}, f32[64,128]{0,1:T(8,128)S(1)}, u32[]{:S(2)}, u32[]{:S(2)}) collective-permute-start(f32[64,128]{0,1:T(8,128)S(1)} %select_select_fusion.1), channel_id=1, source_target_pairs={{0,256},{17,273},{34,290},{51,307},{68,324},{85,341},{102,358},{11... | collective-permute-start | bytes 98312 | tf_op jit(solution)/shard_map/ppermute | solution.py:22
  23.2 0.7 collective-permute-start.13
  23.9 1.6 %collective-permute-start.15 = (f32[64,512]{0,1:T(8,128)S(1)}, f32[64,512]{0,1:T(8,128)S(1)}, u32[]{:S(2)}, u32[]{:S(2)}) collective-permute-start(f32[64,512]{0,1:T(8,128)S(1)} %maximum_select_fusion), channel_id=1, source_target_pairs={{0,16},{256,272},{512,528},{17,33},{273,289},{529,545},{34,50},{29... | collective-permute-start | bytes 393224 | tf_op jit(solution)/shard_map/ppermute | solution.py:22
  24.9 1.4 %collective-permute-start.4 = (f32[64,1280]{1,0:T(8,128)S(1)}, f32[64,1280]{1,0:T(8,128)S(1)}, u32[]{:S(2)}, u32[]{:S(2)}) collective-permute-start(f32[64,1280]{1,0:T(8,128)S(1)} %copy.15), channel_id=1, source_target_pairs={{0,2},{1,3},{16,18},{17,19},{32,34},{33,35},{48,50},{49,51},{64,66... | collective-permute-start | bytes 983048 | tf_op jit(solution)/shard_map/ppermute | solution.py:22
  25.6 0.9 collective-permute-start.16
  26.6 4.3 %collective-permute-start.17 = (f32[64,512]{0,1:T(8,128)S(1)}, f32[64,512]{0,1:T(8,128)}, u32[]{:S(2)}, u32[]{:S(2)}) collective-permute-start(f32[64,512]{0,1:T(8,128)S(1)} %broadcast_select_fusion.5), channel_id=1, source_target_pairs={{0,64},{16,80},{32,96},{48,112},{256,320},{272,336},{288,352},{304... | collective-permute-start | bytes 393224 | tf_op jit(solution)/shard_map/ppermute | solution.py:22
  28.3 4.7 %collective-permute-start.5 = (f32[64,1280]{1,0:T(8,128)S(1)}, f32[64,1280]{1,0:T(8,128)S(1)}, u32[]{:S(2)}, u32[]{:S(2)}) collective-permute-start(f32[64,1280]{1,0:T(8,128)S(1)} %copy.17), channel_id=1, source_target_pairs={{0,4},{1,5},{2,6},{3,7},{16,20},{17,21},{18,22},{19,23},{32,36},{3... | collective-permute-start | bytes 983048 | tf_op jit(solution)/shard_map/ppermute | solution.py:22
  31.6 70.2 %collective-permute-start.18 = (f32[64,512]{0,1:T(8,128)}, f32[64,512]{0,1:T(8,128)}, u32[]{:S(2)}, u32[]{:S(2)}) collective-permute-start(f32[64,512]{0,1:T(8,128)} %broadcast_select_fusion.6), channel_id=1, source_target_pairs={{0,128},{16,144},{32,160},{48,176},{64,192},{80,208},{96,224},{112... | collective-permute-start | bytes 393224 | tf_op jit(solution)/shard_map/ppermute | solution.py:22
  34.3 93.7 %collective-permute-start.6 = (f32[64,1280]{1,0:T(8,128)S(1)}, f32[64,1280]{1,0:T(8,128)}, u32[]{:S(2)}, u32[]{:S(2)}) collective-permute-start(f32[64,1280]{1,0:T(8,128)S(1)} %copy.19), channel_id=1, source_target_pairs={{0,8},{1,9},{2,10},{3,11},{4,12},{5,13},{6,14},{7,15},{16,24},{17,... | collective-permute-start | bytes 983048 | tf_op jit(solution)/shard_map/ppermute | solution.py:22

commit v12 on v10

--- a/solution.py
+++ b/solution.py
@@ -108,12 +108,12 @@
                        preferred_element_type=jnp.float32)
 
     col_t = apply(window_t)
-    col_t = jnp.concatenate(
-        [jnp.where(col_id == 0, factor_t, col_t[:, :B]), col_t[:, B:]], axis=1
+    col_t = lax.dynamic_update_slice(
+        col_t, jnp.where(col_id == 0, factor_t, col_t[:, :B]), (0, 0)
     )
     lower_t = apply(panel_t)
-    lower_t = jnp.concatenate(
-        [jnp.where(row_id == 0, factor_t, lower_t[:, :B]), lower_t[:, B:]], axis=1
+    lower_t = lax.dynamic_update_slice(
+        lower_t, jnp.where(row_id == 0, factor_t, lower_t[:, :B]), (0, 0)
     )
     change = lax.dot_general(
         lower_t,
@@ -126,7 +126,7 @@
     keep_rows = jnp.logical_and(row_id == 0, local_rows < B)
     stepped = jnp.where(keep_rows[:, None], matrix, matrix - change)
     first_cols = jnp.where(col_id == 0, lower_t.T, stepped[:, :B])
-    return jnp.concatenate([first_cols, stepped[:, B:]], axis=1)
+    return lax.dynamic_update_slice(stepped, first_cols, (0, 0))
 
 
 def solution(mesh):

time: 120 us -> 122 us (1.017)
  starting transfers between devices: 14.6 us -> 17.5 us
  other arithmetic: 15 us -> 13.6 us
  waiting for transfers between devices: 75.3 us -> 73.9 us
  local copies, waits for them, and re-layouts: 9.94 us -> 11.3 us
  matrix products: 3.45 us -> 4.8 us
    dynamic_update_slice x0 -> x3, local copies, waits for them, and re-layouts: none -> 2.61 us  [the longest x1 1.78 us: shards(): return lax.dynamic_update_slice(stepped, first_cols, (0, 0))]
    select_n x11, other arithmetic: 2.49 us -> 0.44 us  [tree_broadcast(): fresh = jnp.where(take, got, fresh)]
    concatenate x1 -> x0, local copies, waits for them, and re-layouts: 1.78 us -> none  [shards(): return jnp.concatenate([first_cols, stepped[:, B:]], axis=1)]
    ppermute x16, starting transfers between devices: 12.6 us -> 14.2 us  [tree_broadcast(): got = lax.ppermute(x, axes, pairs)]
    ppermute x16, waiting for transfers between devices: 75.3 us -> 73.9 us  [tree_broadcast(): got = lax.ppermute(x, axes, pairs)]
    dot_general x1, matrix products: 1.94 us -> 3.29 us  [shards(): lax.dot_general(lower_t, col_t, (((0,), (0,)), ((), ())), precision=lax.P...]
    ppermute x3, starting transfers between devices: 2.01 us -> 3.28 us  [shards(): got = lax.ppermute(first, ('row', 'col'), pairs)]
  transfers between devices with their start and end apart: 19 -> 19, of which waited for: 2 -> 2; matrix products, arithmetic and copies ran while one was open for 17% -> 16% of each run, Pallas kernels for 0% -> 0%
where the time goes in v12:
time: 122 us
  waiting for transfers between devices  73.9 us (61%)
  starting transfers between devices  17.5 us (14%)
  other arithmetic  13.6 us (11%)
  local copies, waits for them, and re-layouts  11.3 us (9%)
  matrix products  4.8 us (4%)
    ppermute x16, waiting for transfers between devices, tree_broadcast(): got = lax.ppermute(x, axes, pairs)  73.9 us
    ppermute x16, starting transfers between devices, tree_broadcast(): got = lax.ppermute(x, axes, pairs)  14.2 us
    another operation x3, other arithmetic, shards(): factor = jnp.linalg.cholesky(corner)  6.52 us
    another operation x1, other arithmetic, shards(): lax.linalg.triangular_solve(factor, jnp.eye(B, dtype=factor.dtype), left_...  4.9 us
    ppermute x4, local copies, waits for them, and re-layouts, tree_broadcast(): got = lax.ppermute(x, axes, pairs)  3.7 us
    dot_general x1, matrix products, shards(): lax.dot_general(lower_t, col_t, (((0,), (0,)), ((), ())), precision=lax.P...  3.29 us
    ppermute x3, starting transfers between devices, shards(): got = lax.ppermute(first, ('row', 'col'), pairs)  3.28 us
  transfers between devices with their start and end apart: 19, of which 2 were waited for; matrix products, arithmetic and copies ran while one was open for 16% of the time, Pallas kernels for 0%

profile of v12, /device:TPU:42, one launch (start us, length us, event | category | flops | bytes accessed | tf_op | source)
XLA Modules:
  0.0 121.7 jit_solution(6133232643093094387)
XLA Ops:
  0.0 1.1 slice_bitcast_fusion
  1.2 0.8 collective-permute-start.3
  2.0 0.7 collective-permute-start.2
  2.6 0.7 collective-permute-start.1
  3.4 0.7 collective-permute-start.6
  4.0 0.7 collective-permute-start.5
  4.7 0.7 collective-permute-start.4
  5.5 0.7 collective-permute-start.8
  6.1 0.7 collective-permute-start.7
  6.8 0.2 copy.12
  7.0 1.4 %collective-permute-start = (f32[64,1280]{1,0:T(8,128)S(1)}, f32[64,1280]{1,0:T(8,128)}, u32[]{:S(2)}, u32[]{:S(2)}) collective-permute-start(f32[64,1280]{1,0:T(8,128)S(1)} %copy.12), channel_id=1, source_target_pairs={{0,1},{16,17},{32,33},{48,49},{64,65},{80,81},{96,97},{112,113},{1... | collective-permute-start | bytes 983048 | tf_op jit(solution)/shard_map/ppermute | solution.py:22
  8.4 0.1 copy.14
  8.5 0.1 copy.15
  8.6 5.8 %cholesky.20 = f32[64,64]{1,0:T(8,128)S(1)} custom-call(f32[64,64]{1,0:T(8,128)S(1)} %fusion.4), custom_call_target="Cholesky" | custom-call | tf_op jit(solution)/shard_map/jit(cholesky)/cholesky | solution.py:56
  14.5 0.6 compare_reduce_fusion
  15.2 0.7 fusion.10
  15.8 4.9 %custom-call.6 = f32[1,64,64]{1,2,0:T(8,128)S(1)} custom-call(f32[1,64,64]{2,1,0:T(8,128)S(1)} %get-tuple-element.24), custom_call_target="InvertDiagBlocksLowerTriangular" | custom-call | tf_op jit(solution)/shard_map/triangular_solve | solution.py:57
  20.7 0.2 fusion.2
  21.0 0.7 collective-permute-start.9
  21.8 1.3 %collective-permute-start.10 = (f32[64,256]{0,1:T(8,128)S(1)}, f32[64,256]{0,1:T(8,128)}, u32[]{:S(2)}, u32[]{:S(2)}) collective-permute-start(f32[64,256]{0,1:T(8,128)S(1)} %pad_maximum_fusion), channel_id=1, source_target_pairs={{0,256},{16,273},{32,290},{48,307},{64,324},{80,341},{96,358},{112... | collective-permute-start | bytes 196616 | tf_op jit(solution)/shard_map/ppermute | solution.py:68
  23.1 1.3 %collective-permute-start.11 = (f32[64,256]{0,1:T(8,128)S(1)}, f32[64,256]{0,1:T(8,128)}, u32[]{:S(2)}, u32[]{:S(2)}) collective-permute-start(f32[64,256]{0,1:T(8,128)S(1)} %pad_maximum_fusion), channel_id=1, source_target_pairs={{0,512},{16,529},{32,546},{48,563},{64,580},{80,597},{96,614},{112... | collective-permute-start | bytes 196616 | tf_op jit(solution)/shard_map/ppermute | solution.py:68
  24.4 1.2 copy.13
  25.7 0.9 select_select_fusion.2
  26.7 0.7 collective-permute-start.15
  27.4 0.7 collective-permute-start.16
  28.1 0.9 copy.17
  29.1 1.4 %collective-permute-start.12 = (f32[64,1280]{1,0:T(8,128)}, f32[64,1280]{1,0:T(8,128)}, u32[]{:S(2)}, u32[]{:S(2)}) collective-permute-start(f32[64,1280]{1,0:T(8,128)} %copy.17), channel_id=1, source_target_pairs={{0,2},{1,3},{16,18},{17,19},{32,34},{33,35},{48,50},{49,51},{64,66... | collective-permute-start | bytes 983048 | tf_op jit(solution)/shard_map/ppermute | solution.py:22
  30.5 1.4 %collective-permute-start.17 = (f32[64,512]{0,1:T(8,128)S(1)}, f32[64,512]{0,1:T(8,128)}, u32[]{:S(2)}, u32[]{:S(2)}) collective-permute-start(f32[64,512]{0,1:T(8,128)S(1)} %broadcast_select_fusion.5), channel_id=1, source_target_pairs={{0,64},{16,80},{32,96},{48,112},{256,320},{272,336},{288,352},{304... | collective-permute-start | bytes 393224 | tf_op jit(solution)/shard_map/ppermute | solution.py:22
  31.8 2.0 %copy.18 = f32[64,1280]{0,1:T(8,128)} copy(f32[64,1280]{1,0:T(8,128)} %collective-permute-done.12) | data formatting | bytes 655360 | tf_op jit(solution)/shard_map/ppermute | solution.py:22
  33.9 0.2 copy.19
  34.2 0.7 collective-permute-start.13
  34.9 1.8 %copy.28 = f32[1280,384]{0,1:T(8,128)} copy(f32[1280,384]{1,0:T(8,128)S(1)} %copy-done) | data formatting | bytes 3932160 | tf_op args[0]
  36.7 1.3 %collective-permute-start.18 = (f32[64,512]{0,1:T(8,128)S(1)}, f32[64,512]{0,1:T(8,128)S(1)}, u32[]{:S(2)}, u32[]{:S(2)}) collective-permute-start(f32[64,512]{0,1:T(8,128)S(1)} %broadcast_select_fusion.6), channel_id=1, source_target_pairs={{0,128},{16,144},{32,160},{48,176},{64,192},{80,208},{96,224},{112... | collective-permute-start | bytes 393224 | tf_op jit(solution)/shard_map/ppermute | solution.py:22
  38.0 0.2 copy.20
  38.3 0.2 copy.21
  38.6 1.3 %collective-permute-start.14 = (f32[64,1280]{1,0:T(8,128)S(1)}, f32[64,1280]{1,0:T(8,128)S(1)}, u32[]{:S(2)}, u32[]{:S(2)}) collective-permute-start(f32[64,1280]{1,0:T(8,128)S(1)} %copy.21), channel_id=1, source_target_pairs={{0,8},{1,9},{2,10},{3,11},{4,12},{5,13},{6,14},{7,15},{16,24},{17,... | collective-permute-start | bytes 983048 | tf_op jit(solution)/shard_map/ppermute | solution.py:22
  39.9 42.1 %collective-permute-done.18 = f32[64,512]{0,1:T(8,128)S(1)} collective-permute-done((f32[64,512]{0,1:T(8,128)S(1)}, f32[64,512]{0,1:T(8,128)S(1)}, u32[]{:S(2)}, u32[]{:S(2)}) %collective-permute-start.18) | collective-permute-done | bytes 131104 | tf_op jit(solution)/shard_map/ppermute | solution.py:22
  82.0 31.7 %collective-permute-done.14 = f32[64,1280]{1,0:T(8,128)S(1)} collective-permute-done((f32[64,1280]{1,0:T(8,128)S(1)}, f32[64,1280]{1,0:T(8,128)S(1)}, u32[]{:S(2)}, u32[]{:S(2)}) %collective-permute-start.14) | collective-permute-done | bytes 327712 | tf_op jit(solution)/shard_map/ppermute | solution.py:22
  113.7 0.2 copy.22
  114.1 0.9 fusion.8
  114.9 0.1 copy.31
  115.1 0.4 fusion.6
  115.5 0.1 copy.32
  115.6 0.1 copy.26
  115.7 0.4 dynamic_update_slice.10
  116.2 0.4 dynamic_update_slice.9
  116.6 3.3 %fusion = f32[1280,384]{0,1:T(8,128)S(1)} fusion(f32[1280,384]{0,1:T(8,128)} %copy.28, f32[64,1280]{1,0:T(8,128)S(1)} %dynamic_update_slice.9, f32[64,384]{1,0:T(8,128)S(1)} %dynamic_update_slice.10, pred[1280]{0:T(1024)(128)(4,1)S(1)} %fusion.11), kind=kOutput, calls=%fused_computation.1 | convolution fusion | flops 378470400 | bytes 4359424 | tf_op jit(solution)/shard_map/dot_general | solution.py:118
  120.0 1.8 %copy.29 = f32[1280,384]{1,0:T(8,128)} copy(f32[1280,384]{0,1:T(8,128)S(1)} %fusion.1) | data formatting | bytes 3932160 | tf_op jit(solution)/shard_map/dynamic_update_slice | solution.py:129
  (50 shorter events, 0.8 us)
Async XLA Ops:
  1.1 24.5 %copy-start = (f32[1280,384]{1,0:T(8,128)S(1)}, f32[1280,384]{1,0:T(8,128)}, u32[]{:S(2)}) copy-start(f32[1280,384]{1,0:T(8,128)} %param.1) | copy-start | bytes 5898244
  1.2 2.2 %collective-permute-start.3 = (f32[64,64]{0,1:T(8,128)S(1)}, f32[64,64]{0,1:T(8,128)S(1)}, u32[]{:S(2)}, u32[]{:S(2)}) collective-permute-start(f32[64,64]{0,1:T(8,128)S(1)} %slice.83), channel_id=1, source_target_pairs={{0,16}} | collective-permute-start | bytes 49160 | tf_op jit(solution)/shard_map/ppermute | solution.py:22
  2.0 1.4 %collective-permute-start.2 = (f32[64,64]{0,1:T(8,128)S(1)}, f32[64,64]{0,1:T(8,128)S(1)}, u32[]{:S(2)}, u32[]{:S(2)}) collective-permute-start(f32[64,64]{0,1:T(8,128)S(1)} %slice.83), channel_id=1, source_target_pairs={{0,32}} | collective-permute-start | bytes 49160 | tf_op jit(solution)/shard_map/ppermute | solution.py:22
  2.6 0.7 collective-permute-start.1
  3.4 2.0 %collective-permute-start.6 = (f32[64,64]{0,1:T(8,128)S(1)}, f32[64,64]{0,1:T(8,128)S(1)}, u32[]{:S(2)}, u32[]{:S(2)}) collective-permute-start(f32[64,64]{0,1:T(8,128)S(1)} %select_select_fusion.6), channel_id=1, source_target_pairs={{0,64},{16,80},{32,96},{48,112}} | collective-permute-start | bytes 49160 | tf_op jit(solution)/shard_map/ppermute | solution.py:22
  4.0 1.4 %collective-permute-start.5 = (f32[64,64]{0,1:T(8,128)S(1)}, f32[64,64]{0,1:T(8,128)S(1)}, u32[]{:S(2)}, u32[]{:S(2)}) collective-permute-start(f32[64,64]{0,1:T(8,128)S(1)} %select_select_fusion.6), channel_id=1, source_target_pairs={{0,128},{16,144},{32,160},{48,176}} | collective-permute-start | bytes 49160 | tf_op jit(solution)/shard_map/ppermute | solution.py:22
  4.7 0.7 collective-permute-start.4
  5.5 3.0 %collective-permute-start.8 = (f32[64,64]{0,1:T(8,128)S(1)}, f32[64,64]{0,1:T(8,128)S(1)}, u32[]{:S(2)}, u32[]{:S(2)}) collective-permute-start(f32[64,64]{0,1:T(8,128)S(1)} %select_select_fusion.5), channel_id=1, source_target_pairs={{0,256},{16,272},{32,288},{48,304},{64,320},{80,336},{96,352},{112... | collective-permute-start | bytes 49160 | tf_op jit(solution)/shard_map/ppermute | solution.py:22
  6.1 2.3 %collective-permute-start.7 = (f32[64,64]{0,1:T(8,128)S(1)}, f32[64,64]{0,1:T(8,128)S(1)}, u32[]{:S(2)}, u32[]{:S(2)}) collective-permute-start(f32[64,64]{0,1:T(8,128)S(1)} %select_select_fusion.5), channel_id=1, source_target_pairs={{0,512},{16,528},{32,544},{48,560},{64,576},{80,592},{96,608},{112... | collective-permute-start | bytes 49160 | tf_op jit(solution)/shard_map/ppermute | solution.py:22
  7.0 17.4 %collective-permute-start = (f32[64,1280]{1,0:T(8,128)S(1)}, f32[64,1280]{1,0:T(8,128)}, u32[]{:S(2)}, u32[]{:S(2)}) collective-permute-start(f32[64,1280]{1,0:T(8,128)S(1)} %copy.12), channel_id=1, source_target_pairs={{0,1},{16,17},{32,33},{48,49},{64,65},{80,81},{96,97},{112,113},{1... | collective-permute-start | bytes 983048 | tf_op jit(solution)/shard_map/ppermute | solution.py:22
  21.0 3.4 %collective-permute-start.9 = (f32[64,256]{0,1:T(8,128)S(1)}, f32[64,256]{0,1:T(8,128)S(1)}, u32[]{:S(2)}, u32[]{:S(2)}) collective-permute-start(f32[64,256]{0,1:T(8,128)S(1)} %pad_maximum_fusion), channel_id=1, source_target_pairs={{16,17},{32,34},{48,51},{64,68},{80,85},{96,102},{112,119},{128,13... | collective-permute-start | bytes 196616 | tf_op jit(solution)/shard_map/ppermute | solution.py:68
  21.8 3.9 %collective-permute-start.10 = (f32[64,256]{0,1:T(8,128)S(1)}, f32[64,256]{0,1:T(8,128)}, u32[]{:S(2)}, u32[]{:S(2)}) collective-permute-start(f32[64,256]{0,1:T(8,128)S(1)} %pad_maximum_fusion), channel_id=1, source_target_pairs={{0,256},{16,273},{32,290},{48,307},{64,324},{80,341},{96,358},{112... | collective-permute-start | bytes 196616 | tf_op jit(solution)/shard_map/ppermute | solution.py:68
  23.1 2.6 %collective-permute-start.11 = (f32[64,256]{0,1:T(8,128)S(1)}, f32[64,256]{0,1:T(8,128)}, u32[]{:S(2)}, u32[]{:S(2)}) collective-permute-start(f32[64,256]{0,1:T(8,128)S(1)} %pad_maximum_fusion), channel_id=1, source_target_pairs={{0,512},{16,529},{32,546},{48,563},{64,580},{80,597},{96,614},{112... | collective-permute-start | bytes 196616 | tf_op jit(solution)/shard_map/ppermute | solution.py:68
  26.7 0.7 collective-permute-start.15
  27.4 3.0 %collective-permute-start.16 = (f32[64,512]{0,1:T(8,128)S(1)}, f32[64,512]{0,1:T(8,128)S(1)}, u32[]{:S(2)}, u32[]{:S(2)}) collective-permute-start(f32[64,512]{0,1:T(8,128)S(1)} %broadcast_select_fusion.4), channel_id=1, source_target_pairs={{0,32},{16,48},{256,288},{272,304},{512,544},{528,560},{17,49},{33... | collective-permute-start | bytes 393224 | tf_op jit(solution)/shard_map/ppermute | solution.py:22
  29.1 2.8 %collective-permute-start.12 = (f32[64,1280]{1,0:T(8,128)}, f32[64,1280]{1,0:T(8,128)}, u32[]{:S(2)}, u32[]{:S(2)}) collective-permute-start(f32[64,1280]{1,0:T(8,128)} %copy.17), channel_id=1, source_target_pairs={{0,2},{1,3},{16,18},{17,19},{32,34},{33,35},{48,50},{49,51},{64,66... | collective-permute-start | bytes 983048 | tf_op jit(solution)/shard_map/ppermute | solution.py:22
  30.5 6.2 %collective-permute-start.17 = (f32[64,512]{0,1:T(8,128)S(1)}, f32[64,512]{0,1:T(8,128)}, u32[]{:S(2)}, u32[]{:S(2)}) collective-permute-start(f32[64,512]{0,1:T(8,128)S(1)} %broadcast_select_fusion.5), channel_id=1, source_target_pairs={{0,64},{16,80},{32,96},{48,112},{256,320},{272,336},{288,352},{304... | collective-permute-start | bytes 393224 | tf_op jit(solution)/shard_map/ppermute | solution.py:22
  34.2 3.8 %collective-permute-start.13 = (f32[64,1280]{1,0:T(8,128)S(1)}, f32[64,1280]{1,0:T(8,128)S(1)}, u32[]{:S(2)}, u32[]{:S(2)}) collective-permute-start(f32[64,1280]{1,0:T(8,128)S(1)} %copy.19), channel_id=1, source_target_pairs={{0,4},{1,5},{2,6},{3,7},{16,20},{17,21},{18,22},{19,23},{32,36},{3... | collective-permute-start | bytes 983048 | tf_op jit(solution)/shard_map/ppermute | solution.py:22
  36.7 45.3 %collective-permute-start.18 = (f32[64,512]{0,1:T(8,128)S(1)}, f32[64,512]{0,1:T(8,128)S(1)}, u32[]{:S(2)}, u32[]{:S(2)}) collective-permute-start(f32[64,512]{0,1:T(8,128)S(1)} %broadcast_select_fusion.6), channel_id=1, source_target_pairs={{0,128},{16,144},{32,160},{48,176},{64,192},{80,208},{96,224},{112... | collective-permute-start | bytes 393224 | tf_op jit(solution)/shard_map/ppermute | solution.py:22
  38.6 75.2 %collective-permute-start.14 = (f32[64,1280]{1,0:T(8,128)S(1)}, f32[64,1280]{1,0:T(8,128)S(1)}, u32[]{:S(2)}, u32[]{:S(2)}) collective-permute-start(f32[64,1280]{1,0:T(8,128)S(1)} %copy.21), channel_id=1, source_target_pairs={{0,8},{1,9},{2,10},{3,11},{4,12},{5,13},{6,14},{7,15},{16,24},{17,... | collective-permute-start | bytes 983048 | tf_op jit(solution)/shard_map/ppermute | solution.py:22

commit v13 on v10

--- a/solution.py
+++ b/solution.py
@@ -44,10 +44,20 @@
 
     corner_t = tree_broadcast(panel_t[:, :B], ("row", "col"), n_row, col0_group, row_id, radix=4)
 
+    bits = n_col.bit_length() - 1
+
+    def spread(m):
+        out = m & 1
+        for b in range(1, bits):
+            out = out | (((m >> b) & 1) << (bits - b))
+        return out
+
     def col_groups(_):
-        return [lambda m, r=r: r * n_col + m for r in range(n_row)]
+        return [lambda m, r=r: r * n_col + spread(m) for r in range(n_row)]
 
-    panel_t = tree_broadcast(panel_t, ("row", "col"), 2, col_groups, col_id, radix=2, have=1)
+    col_member = spread(col_id)
+
+    panel_t = tree_broadcast(panel_t, ("row", "col"), 2, col_groups, col_member, radix=2, have=1)
 
     rel = (row_id - col_id) % n_row
     my_j = rel // n_col
@@ -70,7 +80,7 @@
             got = jnp.where(col_id == 0, first, got)
         pieces.append(got)
     panel_t, pieces = lax.optimization_barrier((panel_t, pieces))
-    panel_t = tree_broadcast(panel_t, ("row", "col"), n_col // 2, col_groups, col_id, radix=2, have=2)
+    panel_t = tree_broadcast(panel_t, ("row", "col"), n_col // 2, col_groups, col_member, radix=2, have=2)
     fpack = pieces[0][:, window_cols:]
     pieces = [p[:, :window_cols] for p in pieces]
     ordered = []
@@ -91,7 +101,7 @@
         return out
 
     packet = tree_broadcast(packet, ("row", "col"), n_col, row_groups, rel % n_col)
-    panel_t = tree_broadcast(panel_t, ("row", "col"), n_col, col_groups, col_id, radix=2, have=n_col // 2)
+    panel_t = tree_broadcast(panel_t, ("row", "col"), n_col, col_groups, col_member, radix=2, have=n_col // 2)
     panel_t, packet = lax.optimization_barrier((panel_t, packet))
     factor_t = packet[:, n_src * window_cols: n_src * window_cols + B]
     inverse = packet[:, n_src * window_cols + B:]

time: 120 us -> 106 us (0.88)
  the two profiles are of different devices: /device:TPU:42 before, /device:TPU:120 now
where the time goes in v13:
time: 106 us; the launch traced here: 105 us
  waiting for transfers between devices  61.5 us (58%)
  other arithmetic  15 us (14%)
  starting transfers between devices  14.6 us (14%)
  local copies, waits for them, and re-layouts  9.94 us (9%)
  matrix products  3.45 us (3%)
    ppermute x16, waiting for transfers between devices, tree_broadcast(): got = lax.ppermute(x, axes, pairs)  61.5 us
    ppermute x16, starting transfers between devices, tree_broadcast(): got = lax.ppermute(x, axes, pairs)  12.6 us
    another operation x3, other arithmetic, shards(): factor = jnp.linalg.cholesky(corner)  6.52 us
    another operation x1, other arithmetic, shards(): lax.linalg.triangular_solve(factor, jnp.eye(B, dtype=factor.dtype), left_...  4.9 us
    ppermute x4, local copies, waits for them, and re-layouts, tree_broadcast(): got = lax.ppermute(x, axes, pairs)  2.73 us
    select_n x11, other arithmetic, tree_broadcast(): fresh = jnp.where(take, got, fresh)  2.5 us
  transfers between devices with their start and end apart: 19, of which 2 were waited for; matrix products, arithmetic and copies ran while one was open for 19% of the time, Pallas kernels for 0%

profile of v13, /device:TPU:120, one launch (start us, length us, event | category | flops | bytes accessed | tf_op | source)
XLA Modules:
  0.0 105.4 jit_solution(15176027553095596062)
XLA Ops:
  0.0 1.1 %slice_bitcast_fusion = f32[64,1280]{0,1:T(8,128)S(1)} fusion(f32[1280,384]{1,0:T(8,128)} %param.1), kind=kLoop, calls=%fused_computation.3 | loop fusion | bytes 655360 | tf_op jit(solution)/shard_map/transpose | solution.py:39
  1.1 0.7 collective-permute-start.3
  1.8 0.7 collective-permute-start.2
  2.5 0.7 collective-permute-start.1
  3.2 0.7 collective-permute-start.6
  3.9 0.7 collective-permute-start.5
  4.6 0.7 collective-permute-start.4
  5.3 0.7 collective-permute-start.8
  6.0 0.7 collective-permute-start.7
  6.7 0.2 copy.12
  6.9 0.7 collective-permute-start
  7.8 5.8 %cholesky.20 = f32[64,64]{1,0:T(8,128)S(1)} custom-call(f32[64,64]{1,0:T(8,128)S(1)} %fusion.6), custom_call_target="Cholesky" | custom-call | tf_op jit(solution)/shard_map/jit(cholesky)/cholesky | solution.py:66
  13.7 0.6 compare_reduce_fusion
  14.4 0.7 fusion.12
  15.0 4.9 %custom-call.6 = f32[1,64,64]{1,2,0:T(8,128)S(1)} custom-call(f32[1,64,64]{2,1,0:T(8,128)S(1)} %get-tuple-element.24), custom_call_target="InvertDiagBlocksLowerTriangular" | custom-call | tf_op jit(solution)/shard_map/triangular_solve | solution.py:67
  19.9 0.2 fusion.4
  20.2 0.7 collective-permute-start.9
  21.0 0.7 collective-permute-start.10
  21.7 0.7 collective-permute-start.11
  22.4 0.2 copy.13
  22.6 1.2 %broadcast_select_fusion = f32[64,1280]{0,1:T(8,128)S(1)} fusion(f32[64,1280]{0,1:T(8,128)S(1)} %copy.13, pred[]{:T(512)S(6)} %and.104, f32[1280,384]{1,0:T(8,128)} %param.1), kind=kLoop, calls=%fused_computation.6 | loop fusion | flops 81920 | bytes 983041 | tf_op jit(solution)/shard_map/jit(_where)/select_n | solution.py:24
  23.9 0.7 collective-permute-start.15
  24.6 0.7 collective-permute-start.16
  25.3 0.2 copy.17
  25.5 0.7 collective-permute-start.12
  26.3 1.4 %collective-permute-start.17 = (f32[64,512]{0,1:T(8,128)S(1)}, f32[64,512]{0,1:T(8,128)}, u32[]{:S(2)}, u32[]{:S(2)}) collective-permute-start(f32[64,512]{0,1:T(8,128)S(1)} %broadcast_select_fusion.5), channel_id=1, source_target_pairs={{0,64},{16,80},{32,96},{48,112},{256,320},{272,336},{288,352},{304... | collective-permute-start | bytes 393224 | tf_op jit(solution)/shard_map/ppermute | solution.py:22
  27.6 0.2 copy.18
  28.0 0.9 copy.19
  28.9 0.7 collective-permute-start.13
  29.6 1.9 %copy.28 = f32[1280,384]{0,1:T(8,128)S(1)} copy(f32[1280,384]{1,0:T(8,128)} %param.1) | data formatting | bytes 3932160 | tf_op args[0]
  31.6 1.3 %collective-permute-start.18 = (f32[64,512]{0,1:T(8,128)S(1)}, f32[64,512]{0,1:T(8,128)}, u32[]{:S(2)}, u32[]{:S(2)}) collective-permute-start(f32[64,512]{0,1:T(8,128)S(1)} %broadcast_select_fusion.6), channel_id=1, source_target_pairs={{0,128},{16,144},{32,160},{48,176},{64,192},{80,208},{96,224},{112... | collective-permute-start | bytes 393224 | tf_op jit(solution)/shard_map/ppermute | solution.py:22
  32.9 1.1 %copy.20 = f32[64,1280]{0,1:T(8,128)} copy(f32[64,1280]{1,0:T(8,128)S(1)} %collective-permute-done.13) | data formatting | bytes 655360 | tf_op jit(solution)/shard_map/ppermute | solution.py:22
  34.0 0.2 copy.21
  34.3 1.3 %collective-permute-start.14 = (f32[64,1280]{1,0:T(8,128)S(1)}, f32[64,1280]{1,0:T(8,128)}, u32[]{:S(2)}, u32[]{:S(2)}) collective-permute-start(f32[64,1280]{1,0:T(8,128)S(1)} %copy.21), channel_id=1, source_target_pairs={{0,2},{1,3},{8,10},{9,11},{4,6},{5,7},{12,14},{13,15},{16,18},{17,... | collective-permute-start | bytes 983048 | tf_op jit(solution)/shard_map/ppermute | solution.py:22
  35.6 51.7 %collective-permute-done.18 = f32[64,512]{0,1:T(8,128)} collective-permute-done((f32[64,512]{0,1:T(8,128)S(1)}, f32[64,512]{0,1:T(8,128)}, u32[]{:S(2)}, u32[]{:S(2)}) %collective-permute-start.18) | collective-permute-done | bytes 131104 | tf_op jit(solution)/shard_map/ppermute | solution.py:22
  87.3 1.0 broadcast_select_fusion.7
  88.3 9.7 %collective-permute-done.14 = f32[64,1280]{1,0:T(8,128)} collective-permute-done((f32[64,1280]{1,0:T(8,128)S(1)}, f32[64,1280]{1,0:T(8,128)}, u32[]{:S(2)}, u32[]{:S(2)}) %collective-permute-start.14) | collective-permute-done | bytes 327712 | tf_op jit(solution)/shard_map/ppermute | solution.py:22
  98.0 1.2 %copy.22 = f32[64,1280]{0,1:T(8,128)S(1)} copy(f32[64,1280]{1,0:T(8,128)} %collective-permute-done.14) | data formatting | bytes 655360 | tf_op jit(solution)/shard_map/ppermute | solution.py:22
  99.3 0.9 fusion.10
  100.2 0.1 slice.97
  100.4 0.4 fusion.8
  100.9 0.1 slice.99
  101.0 0.1 copy.32
  101.3 1.9 %fusion = f32[1280,384]{0,1:T(8,128)S(1)} fusion(f32[1280,384]{0,1:T(8,128)S(1)} %copy.28, pred[1280]{0:T(1024)(128)(4,1)S(1)} %fusion.13, f32[64,1216]{1,0:T(8,128)S(1)} %slice.97, f32[64,64]{1,0:T(8,128)S(1)} %copy.24, f32[64,320]{1,0:T(8,128)S(1)} %slice.99, f32[64,64]{1,0:T(8,128)S(1)} %copy.26), kind=kOutput, calls=%fused_computation.1 | convolution fusion | flops 378576896 | bytes 4359424 | tf_op jit(solution)/shard_map/dot_general | solution.py:128
  103.2 0.2 slice_select_fusion
  103.4 0.1 slice.101
  103.5 0.1 pad_maximum_fusion
  103.6 1.8 %copy.29 = f32[1280,384]{1,0:T(8,128)} copy(f32[1280,384]{0,1:T(8,128)S(1)} %pad_maximum_fusion) | data formatting | bytes 3932160 | tf_op jit(solution)/shard_map/concatenate | solution.py:139
  (52 shorter events, 1.0 us)
Async XLA Ops:
  1.1 2.0 %collective-permute-start.3 = (f32[64,64]{0,1:T(8,128)S(1)}, f32[64,64]{0,1:T(8,128)S(1)}, u32[]{:S(2)}, u32[]{:S(2)}) collective-permute-start(f32[64,64]{0,1:T(8,128)S(1)} %slice.95), channel_id=1, source_target_pairs={{0,16}} | collective-permute-start | bytes 49160 | tf_op jit(solution)/shard_map/ppermute | solution.py:22
  1.8 1.4 %collective-permute-start.2 = (f32[64,64]{0,1:T(8,128)S(1)}, f32[64,64]{0,1:T(8,128)S(1)}, u32[]{:S(2)}, u32[]{:S(2)}) collective-permute-start(f32[64,64]{0,1:T(8,128)S(1)} %slice.95), channel_id=1, source_target_pairs={{0,32}} | collective-permute-start | bytes 49160 | tf_op jit(solution)/shard_map/ppermute | solution.py:22
  2.5 0.7 collective-permute-start.1
  3.2 2.0 %collective-permute-start.6 = (f32[64,64]{0,1:T(8,128)S(1)}, f32[64,64]{0,1:T(8,128)S(1)}, u32[]{:S(2)}, u32[]{:S(2)}) collective-permute-start(f32[64,64]{0,1:T(8,128)S(1)} %select_select_fusion.6), channel_id=1, source_target_pairs={{0,64},{16,80},{32,96},{48,112}} | collective-permute-start | bytes 49160 | tf_op jit(solution)/shard_map/ppermute | solution.py:22
  3.9 1.4 %collective-permute-start.5 = (f32[64,64]{0,1:T(8,128)S(1)}, f32[64,64]{0,1:T(8,128)S(1)}, u32[]{:S(2)}, u32[]{:S(2)}) collective-permute-start(f32[64,64]{0,1:T(8,128)S(1)} %select_select_fusion.6), channel_id=1, source_target_pairs={{0,128},{16,144},{32,160},{48,176}} | collective-permute-start | bytes 49160 | tf_op jit(solution)/shard_map/ppermute | solution.py:22
  4.6 0.7 collective-permute-start.4
  5.3 2.3 %collective-permute-start.8 = (f32[64,64]{0,1:T(8,128)S(1)}, f32[64,64]{0,1:T(8,128)S(1)}, u32[]{:S(2)}, u32[]{:S(2)}) collective-permute-start(f32[64,64]{0,1:T(8,128)S(1)} %select_select_fusion.5), channel_id=1, source_target_pairs={{0,256},{16,272},{32,288},{48,304},{64,320},{80,336},{96,352},{112... | collective-permute-start | bytes 49160 | tf_op jit(solution)/shard_map/ppermute | solution.py:22
  6.0 1.6 %collective-permute-start.7 = (f32[64,64]{0,1:T(8,128)S(1)}, f32[64,64]{0,1:T(8,128)S(1)}, u32[]{:S(2)}, u32[]{:S(2)}) collective-permute-start(f32[64,64]{0,1:T(8,128)S(1)} %select_select_fusion.5), channel_id=1, source_target_pairs={{0,512},{16,528},{32,544},{48,560},{64,576},{80,592},{96,608},{112... | collective-permute-start | bytes 49160 | tf_op jit(solution)/shard_map/ppermute | solution.py:22
  6.9 15.5 %collective-permute-start = (f32[64,1280]{1,0:T(8,128)S(1)}, f32[64,1280]{1,0:T(8,128)S(1)}, u32[]{:S(2)}, u32[]{:S(2)}) collective-permute-start(f32[64,1280]{1,0:T(8,128)S(1)} %copy.12), channel_id=1, source_target_pairs={{0,1},{16,17},{32,33},{48,49},{64,65},{80,81},{96,97},{112,113},{1... | collective-permute-start | bytes 983048 | tf_op jit(solution)/shard_map/ppermute | solution.py:22
  20.2 2.2 %collective-permute-start.9 = (f32[64,256]{0,1:T(8,128)S(1)}, f32[64,256]{0,1:T(8,128)S(1)}, u32[]{:S(2)}, u32[]{:S(2)}) collective-permute-start(f32[64,256]{0,1:T(8,128)S(1)} %pad_maximum_fusion.3), channel_id=1, source_target_pairs={{16,17},{32,34},{48,51},{64,68},{80,85},{96,102},{112,119},{128,13... | collective-permute-start | bytes 196616 | tf_op jit(solution)/shard_map/ppermute | solution.py:78
  21.0 2.8 %collective-permute-start.10 = (f32[64,256]{0,1:T(8,128)S(1)}, f32[64,256]{0,1:T(8,128)S(1)}, u32[]{:S(2)}, u32[]{:S(2)}) collective-permute-start(f32[64,256]{0,1:T(8,128)S(1)} %pad_maximum_fusion.3), channel_id=1, source_target_pairs={{0,256},{16,273},{32,290},{48,307},{64,324},{80,341},{96,358},{112... | collective-permute-start | bytes 196616 | tf_op jit(solution)/shard_map/ppermute | solution.py:78
  21.7 2.1 %collective-permute-start.11 = (f32[64,256]{0,1:T(8,128)S(1)}, f32[64,256]{0,1:T(8,128)S(1)}, u32[]{:S(2)}, u32[]{:S(2)}) collective-permute-start(f32[64,256]{0,1:T(8,128)S(1)} %pad_maximum_fusion.3), channel_id=1, source_target_pairs={{0,512},{16,529},{32,546},{48,563},{64,580},{80,597},{96,614},{112... | collective-permute-start | bytes 196616 | tf_op jit(solution)/shard_map/ppermute | solution.py:78
  23.9 0.7 collective-permute-start.15
  24.6 1.6 %collective-permute-start.16 = (f32[64,512]{0,1:T(8,128)S(1)}, f32[64,512]{0,1:T(8,128)S(1)}, u32[]{:S(2)}, u32[]{:S(2)}) collective-permute-start(f32[64,512]{0,1:T(8,128)S(1)} %broadcast_select_fusion.4), channel_id=1, source_target_pairs={{0,32},{16,48},{256,288},{272,304},{512,544},{528,560},{17,49},{33... | collective-permute-start | bytes 393224 | tf_op jit(solution)/shard_map/ppermute | solution.py:22
  25.5 2.1 %collective-permute-start.12 = (f32[64,1280]{1,0:T(8,128)S(1)}, f32[64,1280]{1,0:T(8,128)S(1)}, u32[]{:S(2)}, u32[]{:S(2)}) collective-permute-start(f32[64,1280]{1,0:T(8,128)S(1)} %copy.17), channel_id=1, source_target_pairs={{0,8},{1,9},{16,24},{17,25},{32,40},{33,41},{48,56},{49,57},{64,72... | collective-permute-start | bytes 983048 | tf_op jit(solution)/shard_map/ppermute | solution.py:22
  26.3 5.2 %collective-permute-start.17 = (f32[64,512]{0,1:T(8,128)S(1)}, f32[64,512]{0,1:T(8,128)}, u32[]{:S(2)}, u32[]{:S(2)}) collective-permute-start(f32[64,512]{0,1:T(8,128)S(1)} %broadcast_select_fusion.5), channel_id=1, source_target_pairs={{0,64},{16,80},{32,96},{48,112},{256,320},{272,336},{288,352},{304... | collective-permute-start | bytes 393224 | tf_op jit(solution)/shard_map/ppermute | solution.py:22
  28.9 4.0 %collective-permute-start.13 = (f32[64,1280]{1,0:T(8,128)}, f32[64,1280]{1,0:T(8,128)S(1)}, u32[]{:S(2)}, u32[]{:S(2)}) collective-permute-start(f32[64,1280]{1,0:T(8,128)} %copy.19), channel_id=1, source_target_pairs={{0,4},{1,5},{8,12},{9,13},{16,20},{17,21},{24,28},{25,29},{32,36},... | collective-permute-start | bytes 983048 | tf_op jit(solution)/shard_map/ppermute | solution.py:22
  31.6 4.0 %copy-start = (f32[64,512]{0,1:T(8,128)}, f32[64,512]{0,1:T(8,128)S(1)}, u32[]{:S(2)}) copy-start(f32[64,512]{0,1:T(8,128)S(1)} %broadcast_select_fusion.6) | copy-start | bytes 393220
  31.6 55.7 %collective-permute-start.18 = (f32[64,512]{0,1:T(8,128)S(1)}, f32[64,512]{0,1:T(8,128)}, u32[]{:S(2)}, u32[]{:S(2)}) collective-permute-start(f32[64,512]{0,1:T(8,128)S(1)} %broadcast_select_fusion.6), channel_id=1, source_target_pairs={{0,128},{16,144},{32,160},{48,176},{64,192},{80,208},{96,224},{112... | collective-permute-start | bytes 393224 | tf_op jit(solution)/shard_map/ppermute | solution.py:22
  34.3 63.8 %collective-permute-start.14 = (f32[64,1280]{1,0:T(8,128)S(1)}, f32[64,1280]{1,0:T(8,128)}, u32[]{:S(2)}, u32[]{:S(2)}) collective-permute-start(f32[64,1280]{1,0:T(8,128)S(1)} %copy.21), channel_id=1, source_target_pairs={{0,2},{1,3},{8,10},{9,11},{4,6},{5,7},{12,14},{13,15},{16,18},{17,... | collective-permute-start | bytes 983048 | tf_op jit(solution)/shard_map/ppermute | solution.py:22

commit v14 on v13

--- a/solution.py
+++ b/solution.py
@@ -92,15 +92,21 @@
     packet = jnp.concatenate(ordered + [fpack], axis=1)
     packet = jnp.where(is_src, packet, jnp.zeros_like(packet))
 
+    def flip(m):
+        out = 0
+        for b in range(bits):
+            out = out | (((m >> b) & 1) << (bits - 1 - b))
+        return out
+
     def row_groups(_):
         out = []
         for q in range(n_col):
             for j in range(n_src):
                 base = q + n_col * j
-                out.append(lambda m, base=base, q=q: ((base + m) % n_row) * n_col + q)
+                out.append(lambda m, base=base, q=q: ((base + flip(m)) % n_row) * n_col + q)
         return out
 
-    packet = tree_broadcast(packet, ("row", "col"), n_col, row_groups, rel % n_col)
+    packet = tree_broadcast(packet, ("row", "col"), n_col, row_groups, flip(rel % n_col))
     panel_t = tree_broadcast(panel_t, ("row", "col"), n_col, col_groups, col_member, radix=2, have=n_col // 2)
     panel_t, packet = lax.optimization_barrier((panel_t, packet))
     factor_t = packet[:, n_src * window_cols: n_src * window_cols + B]

time: 106 us -> 108 us (1.019)
  the two profiles are of different devices: /device:TPU:120 before, /device:TPU:56 now
where the time goes in v14:
time: 108 us
  waiting for transfers between devices  62 us (57%)
  other arithmetic  15.9 us (15%)
  starting transfers between devices  15.3 us (14%)
  local copies, waits for them, and re-layouts  9.94 us (9%)
  matrix products  3.44 us (3%)
    ppermute x16, waiting for transfers between devices, tree_broadcast(): got = lax.ppermute(x, axes, pairs)  62 us
    ppermute x16, starting transfers between devices, tree_broadcast(): got = lax.ppermute(x, axes, pairs)  13.3 us
    another operation x3, other arithmetic, shards(): factor = jnp.linalg.cholesky(corner)  6.52 us
    another operation x1, other arithmetic, shards(): lax.linalg.triangular_solve(factor, jnp.eye(B, dtype=factor.dtype), left_...  4.9 us
    select_n x11, other arithmetic, tree_broadcast(): fresh = jnp.where(take, got, fresh)  3.45 us
    ppermute x4, local copies, waits for them, and re-layouts, tree_broadcast(): got = lax.ppermute(x, axes, pairs)  2.73 us
  transfers between devices with their start and end apart: 19, of which 2 were waited for; matrix products, arithmetic and copies ran while one was open for 19% of the time, Pallas kernels for 0%

profile of v14, /device:TPU:56, one launch (start us, length us, event | category | flops | bytes accessed | tf_op | source)
XLA Modules:
  0.0 107.5 jit_solution(7701205611820964807)
XLA Ops:
  0.0 1.1 %slice_bitcast_fusion = f32[64,1280]{0,1:T(8,128)S(1)} fusion(f32[1280,384]{1,0:T(8,128)} %param.1), kind=kLoop, calls=%fused_computation.3 | loop fusion | bytes 655360 | tf_op jit(solution)/shard_map/transpose | solution.py:39
  1.1 0.7 collective-permute-start.3
  1.8 0.7 collective-permute-start.2
  2.5 0.7 collective-permute-start.1
  3.2 0.7 collective-permute-start.6
  3.9 0.7 collective-permute-start.5
  4.6 0.7 collective-permute-start.4
  5.3 0.7 collective-permute-start.8
  6.0 0.7 collective-permute-start.7
  6.7 0.2 copy.12
  6.9 0.7 collective-permute-start
  7.8 5.8 %cholesky.20 = f32[64,64]{1,0:T(8,128)S(1)} custom-call(f32[64,64]{1,0:T(8,128)S(1)} %fusion.6), custom_call_target="Cholesky" | custom-call | tf_op jit(solution)/shard_map/jit(cholesky)/cholesky | solution.py:66
  13.7 0.6 compare_reduce_fusion
  14.4 0.7 fusion.12
  15.0 4.9 %custom-call.6 = f32[1,64,64]{1,2,0:T(8,128)S(1)} custom-call(f32[1,64,64]{2,1,0:T(8,128)S(1)} %get-tuple-element.24), custom_call_target="InvertDiagBlocksLowerTriangular" | custom-call | tf_op jit(solution)/shard_map/triangular_solve | solution.py:67
  19.9 0.2 fusion.4
  20.2 0.7 collective-permute-start.9
  21.0 0.7 collective-permute-start.10
  21.7 0.7 collective-permute-start.11
  22.4 0.2 copy.13
  22.6 1.2 %broadcast_select_fusion = f32[64,1280]{0,1:T(8,128)S(1)} fusion(f32[64,1280]{0,1:T(8,128)S(1)} %copy.13, pred[]{:T(512)S(6)} %and.116, f32[1280,384]{1,0:T(8,128)} %param.1), kind=kLoop, calls=%fused_computation.6 | loop fusion | flops 81920 | bytes 983041 | tf_op jit(solution)/shard_map/jit(_where)/select_n | solution.py:24
  23.9 0.7 collective-permute-start.15
  24.6 0.7 collective-permute-start.16
  25.3 0.2 copy.17
  25.5 0.7 collective-permute-start.12
  26.3 1.3 %collective-permute-start.17 = (f32[64,512]{0,1:T(8,128)S(1)}, f32[64,512]{0,1:T(8,128)}, u32[]{:S(2)}, u32[]{:S(2)}) collective-permute-start(f32[64,512]{0,1:T(8,128)S(1)} %broadcast_select_fusion.5), channel_id=1, source_target_pairs={{0,32},{128,160},{64,96},{192,224},{256,288},{384,416},{320,352},{... | collective-permute-start | bytes 393224 | tf_op jit(solution)/shard_map/ppermute | solution.py:22
  27.6 0.2 copy.18
  27.9 0.9 copy.19
  28.9 0.7 collective-permute-start.13
  29.6 1.9 %copy.28 = f32[1280,384]{0,1:T(8,128)S(1)} copy(f32[1280,384]{1,0:T(8,128)} %param.1) | data formatting | bytes 3932160 | tf_op args[0]
  31.5 47.5 %collective-permute-done.17 = f32[64,512]{0,1:T(8,128)} collective-permute-done((f32[64,512]{0,1:T(8,128)S(1)}, f32[64,512]{0,1:T(8,128)}, u32[]{:S(2)}, u32[]{:S(2)}) %collective-permute-start.17) | collective-permute-done | bytes 131104 | tf_op jit(solution)/shard_map/ppermute | solution.py:22
  79.0 1.0 broadcast_select_fusion.6
  80.0 2.0 %collective-permute-start.18 = (f32[64,512]{0,1:T(8,128)S(1)}, f32[64,512]{0,1:T(8,128)}, u32[]{:S(2)}, u32[]{:S(2)}) collective-permute-start(f32[64,512]{0,1:T(8,128)S(1)} %broadcast_select_fusion.6), channel_id=1, source_target_pairs={{0,16},{128,144},{64,80},{192,208},{32,48},{160,176},{96,112},{224... | collective-permute-start | bytes 393224 | tf_op jit(solution)/shard_map/ppermute | solution.py:22
  82.0 1.1 %copy.20 = f32[64,1280]{0,1:T(8,128)} copy(f32[64,1280]{1,0:T(8,128)S(1)} %collective-permute-done.13) | data formatting | bytes 655360 | tf_op jit(solution)/shard_map/ppermute | solution.py:22
  83.1 0.2 copy.21
  83.3 1.3 %collective-permute-start.14 = (f32[64,1280]{1,0:T(8,128)S(1)}, f32[64,1280]{1,0:T(8,128)}, u32[]{:S(2)}, u32[]{:S(2)}) collective-permute-start(f32[64,1280]{1,0:T(8,128)S(1)} %copy.21), channel_id=1, source_target_pairs={{0,2},{1,3},{8,10},{9,11},{4,6},{5,7},{12,14},{13,15},{16,18},{17,... | collective-permute-start | bytes 983048 | tf_op jit(solution)/shard_map/ppermute | solution.py:22
  84.7 1.0 broadcast_select_fusion.7
  85.7 14.5 %collective-permute-done.14 = f32[64,1280]{1,0:T(8,128)} collective-permute-done((f32[64,1280]{1,0:T(8,128)S(1)}, f32[64,1280]{1,0:T(8,128)}, u32[]{:S(2)}, u32[]{:S(2)}) %collective-permute-start.14) | collective-permute-done | bytes 327712 | tf_op jit(solution)/shard_map/ppermute | solution.py:22
  100.2 1.2 %copy.22 = f32[64,1280]{0,1:T(8,128)S(1)} copy(f32[64,1280]{1,0:T(8,128)} %collective-permute-done.14) | data formatting | bytes 655360 | tf_op jit(solution)/shard_map/ppermute | solution.py:22
  101.4 0.9 fusion.10
  102.3 0.1 slice.97
  102.5 0.4 fusion.8
  103.0 0.1 slice.99
  103.4 1.9 %fusion = f32[1280,384]{0,1:T(8,128)S(1)} fusion(f32[1280,384]{0,1:T(8,128)S(1)} %copy.28, pred[1280]{0:T(1024)(128)(4,1)S(1)} %fusion.13, f32[64,1216]{1,0:T(8,128)S(1)} %slice.97, f32[64,64]{1,0:T(8,128)S(1)} %copy.24, f32[64,320]{1,0:T(8,128)S(1)} %slice.99, f32[64,64]{1,0:T(8,128)S(1)} %copy.26), kind=kOutput, calls=%fused_computation.1 | convolution fusion | flops 378576896 | bytes 4359424 | tf_op jit(solution)/shard_map/dot_general | solution.py:134
  105.3 0.2 slice_select_fusion
  105.5 0.1 slice.101
  105.6 0.1 pad_maximum_fusion
  105.8 1.8 %copy.29 = f32[1280,384]{1,0:T(8,128)} copy(f32[1280,384]{0,1:T(8,128)S(1)} %pad_maximum_fusion) | data formatting | bytes 3932160 | tf_op jit(solution)/shard_map/concatenate | solution.py:145
  (52 shorter events, 1.0 us)
Async XLA Ops:
  1.1 2.0 %collective-permute-start.3 = (f32[64,64]{0,1:T(8,128)S(1)}, f32[64,64]{0,1:T(8,128)S(1)}, u32[]{:S(2)}, u32[]{:S(2)}) collective-permute-start(f32[64,64]{0,1:T(8,128)S(1)} %slice.95), channel_id=1, source_target_pairs={{0,16}} | collective-permute-start | bytes 49160 | tf_op jit(solution)/shard_map/ppermute | solution.py:22
  1.8 1.4 %collective-permute-start.2 = (f32[64,64]{0,1:T(8,128)S(1)}, f32[64,64]{0,1:T(8,128)S(1)}, u32[]{:S(2)}, u32[]{:S(2)}) collective-permute-start(f32[64,64]{0,1:T(8,128)S(1)} %slice.95), channel_id=1, source_target_pairs={{0,32}} | collective-permute-start | bytes 49160 | tf_op jit(solution)/shard_map/ppermute | solution.py:22
  2.5 0.7 collective-permute-start.1
  3.2 2.0 %collective-permute-start.6 = (f32[64,64]{0,1:T(8,128)S(1)}, f32[64,64]{0,1:T(8,128)S(1)}, u32[]{:S(2)}, u32[]{:S(2)}) collective-permute-start(f32[64,64]{0,1:T(8,128)S(1)} %select_select_fusion.6), channel_id=1, source_target_pairs={{0,64},{16,80},{32,96},{48,112}} | collective-permute-start | bytes 49160 | tf_op jit(solution)/shard_map/ppermute | solution.py:22
  3.9 1.4 %collective-permute-start.5 = (f32[64,64]{0,1:T(8,128)S(1)}, f32[64,64]{0,1:T(8,128)S(1)}, u32[]{:S(2)}, u32[]{:S(2)}) collective-permute-start(f32[64,64]{0,1:T(8,128)S(1)} %select_select_fusion.6), channel_id=1, source_target_pairs={{0,128},{16,144},{32,160},{48,176}} | collective-permute-start | bytes 49160 | tf_op jit(solution)/shard_map/ppermute | solution.py:22
  4.6 0.7 collective-permute-start.4
  5.3 2.3 %collective-permute-start.8 = (f32[64,64]{0,1:T(8,128)S(1)}, f32[64,64]{0,1:T(8,128)S(1)}, u32[]{:S(2)}, u32[]{:S(2)}) collective-permute-start(f32[64,64]{0,1:T(8,128)S(1)} %select_select_fusion.5), channel_id=1, source_target_pairs={{0,256},{16,272},{32,288},{48,304},{64,320},{80,336},{96,352},{112... | collective-permute-start | bytes 49160 | tf_op jit(solution)/shard_map/ppermute | solution.py:22
  6.0 1.6 %collective-permute-start.7 = (f32[64,64]{0,1:T(8,128)S(1)}, f32[64,64]{0,1:T(8,128)S(1)}, u32[]{:S(2)}, u32[]{:S(2)}) collective-permute-start(f32[64,64]{0,1:T(8,128)S(1)} %select_select_fusion.5), channel_id=1, source_target_pairs={{0,512},{16,528},{32,544},{48,560},{64,576},{80,592},{96,608},{112... | collective-permute-start | bytes 49160 | tf_op jit(solution)/shard_map/ppermute | solution.py:22
  6.9 15.5 %collective-permute-start = (f32[64,1280]{1,0:T(8,128)S(1)}, f32[64,1280]{1,0:T(8,128)S(1)}, u32[]{:S(2)}, u32[]{:S(2)}) collective-permute-start(f32[64,1280]{1,0:T(8,128)S(1)} %copy.12), channel_id=1, source_target_pairs={{0,1},{16,17},{32,33},{48,49},{64,65},{80,81},{96,97},{112,113},{1... | collective-permute-start | bytes 983048 | tf_op jit(solution)/shard_map/ppermute | solution.py:22
  20.2 2.2 %collective-permute-start.9 = (f32[64,256]{0,1:T(8,128)S(1)}, f32[64,256]{0,1:T(8,128)S(1)}, u32[]{:S(2)}, u32[]{:S(2)}) collective-permute-start(f32[64,256]{0,1:T(8,128)S(1)} %pad_maximum_fusion.3), channel_id=1, source_target_pairs={{16,17},{32,34},{48,51},{64,68},{80,85},{96,102},{112,119},{128,13... | collective-permute-start | bytes 196616 | tf_op jit(solution)/shard_map/ppermute | solution.py:78
  21.0 2.8 %collective-permute-start.10 = (f32[64,256]{0,1:T(8,128)S(1)}, f32[64,256]{0,1:T(8,128)S(1)}, u32[]{:S(2)}, u32[]{:S(2)}) collective-permute-start(f32[64,256]{0,1:T(8,128)S(1)} %pad_maximum_fusion.3), channel_id=1, source_target_pairs={{0,256},{16,273},{32,290},{48,307},{64,324},{80,341},{96,358},{112... | collective-permute-start | bytes 196616 | tf_op jit(solution)/shard_map/ppermute | solution.py:78
  21.7 2.1 %collective-permute-start.11 = (f32[64,256]{0,1:T(8,128)S(1)}, f32[64,256]{0,1:T(8,128)S(1)}, u32[]{:S(2)}, u32[]{:S(2)}) collective-permute-start(f32[64,256]{0,1:T(8,128)S(1)} %pad_maximum_fusion.3), channel_id=1, source_target_pairs={{0,512},{16,529},{32,546},{48,563},{64,580},{80,597},{96,614},{112... | collective-permute-start | bytes 196616 | tf_op jit(solution)/shard_map/ppermute | solution.py:78
  23.9 0.7 collective-permute-start.15
  24.6 1.6 %collective-permute-start.16 = (f32[64,512]{0,1:T(8,128)S(1)}, f32[64,512]{0,1:T(8,128)S(1)}, u32[]{:S(2)}, u32[]{:S(2)}) collective-permute-start(f32[64,512]{0,1:T(8,128)S(1)} %broadcast_select_fusion.4), channel_id=1, source_target_pairs={{0,64},{128,192},{256,320},{384,448},{512,576},{640,704},{17,81},{... | collective-permute-start | bytes 393224 | tf_op jit(solution)/shard_map/ppermute | solution.py:22
  25.5 2.1 %collective-permute-start.12 = (f32[64,1280]{1,0:T(8,128)S(1)}, f32[64,1280]{1,0:T(8,128)S(1)}, u32[]{:S(2)}, u32[]{:S(2)}) collective-permute-start(f32[64,1280]{1,0:T(8,128)S(1)} %copy.17), channel_id=1, source_target_pairs={{0,8},{1,9},{16,24},{17,25},{32,40},{33,41},{48,56},{49,57},{64,72... | collective-permute-start | bytes 983048 | tf_op jit(solution)/shard_map/ppermute | solution.py:22
  26.3 52.7 %collective-permute-start.17 = (f32[64,512]{0,1:T(8,128)S(1)}, f32[64,512]{0,1:T(8,128)}, u32[]{:S(2)}, u32[]{:S(2)}) collective-permute-start(f32[64,512]{0,1:T(8,128)S(1)} %broadcast_select_fusion.5), channel_id=1, source_target_pairs={{0,32},{128,160},{64,96},{192,224},{256,288},{384,416},{320,352},{... | collective-permute-start | bytes 393224 | tf_op jit(solution)/shard_map/ppermute | solution.py:22
  28.9 53.1 %collective-permute-start.13 = (f32[64,1280]{1,0:T(8,128)}, f32[64,1280]{1,0:T(8,128)S(1)}, u32[]{:S(2)}, u32[]{:S(2)}) collective-permute-start(f32[64,1280]{1,0:T(8,128)} %copy.19), channel_id=1, source_target_pairs={{0,4},{1,5},{8,12},{9,13},{16,20},{17,21},{24,28},{25,29},{32,36},... | collective-permute-start | bytes 983048 | tf_op jit(solution)/shard_map/ppermute | solution.py:22
  80.0 4.7 %copy-start = (f32[64,512]{0,1:T(8,128)}, f32[64,512]{0,1:T(8,128)S(1)}, u32[]{:S(2)}) copy-start(f32[64,512]{0,1:T(8,128)S(1)} %broadcast_select_fusion.6) | copy-start | bytes 393220
  80.0 4.7 %collective-permute-start.18 = (f32[64,512]{0,1:T(8,128)S(1)}, f32[64,512]{0,1:T(8,128)}, u32[]{:S(2)}, u32[]{:S(2)}) collective-permute-start(f32[64,512]{0,1:T(8,128)S(1)} %broadcast_select_fusion.6), channel_id=1, source_target_pairs={{0,16},{128,144},{64,80},{192,208},{32,48},{160,176},{96,112},{224... | collective-permute-start | bytes 393224 | tf_op jit(solution)/shard_map/ppermute | solution.py:22
  83.3 16.8 %collective-permute-start.14 = (f32[64,1280]{1,0:T(8,128)S(1)}, f32[64,1280]{1,0:T(8,128)}, u32[]{:S(2)}, u32[]{:S(2)}) collective-permute-start(f32[64,1280]{1,0:T(8,128)S(1)} %copy.21), channel_id=1, source_target_pairs={{0,2},{1,3},{8,10},{9,11},{4,6},{5,7},{12,14},{13,15},{16,18},{17,... | collective-permute-start | bytes 983048 | tf_op jit(solution)/shard_map/ppermute | solution.py:22

commit v15 on v13

--- a/solution.py
+++ b/solution.py
@@ -100,7 +100,7 @@
                 out.append(lambda m, base=base, q=q: ((base + m) % n_row) * n_col + q)
         return out
 
-    packet = tree_broadcast(packet, ("row", "col"), n_col, row_groups, rel % n_col)
+    packet = tree_broadcast(packet, ("row", "col"), n_col, row_groups, rel % n_col, radix=4)
     panel_t = tree_broadcast(panel_t, ("row", "col"), n_col, col_groups, col_member, radix=2, have=n_col // 2)
     panel_t, packet = lax.optimization_barrier((panel_t, packet))
     factor_t = packet[:, n_src * window_cols: n_src * window_cols + B]

time: 106 us -> 102 us (0.962)
  the two profiles are of different devices: /device:TPU:120 before, /device:TPU:38 now
where the time goes in v15:
time: 102 us
  waiting for transfers between devices  51.8 us (51%)
  starting transfers between devices  20 us (20%)
  other arithmetic  15 us (15%)
  local copies, waits for them, and re-layouts  10.6 us (10%)
  matrix products  3.44 us (3%)
    ppermute x18, waiting for transfers between devices, tree_broadcast(): got = lax.ppermute(x, axes, pairs)  51.8 us
    ppermute x18, starting transfers between devices, tree_broadcast(): got = lax.ppermute(x, axes, pairs)  18 us
    another operation x3, other arithmetic, shards(): factor = jnp.linalg.cholesky(corner)  6.52 us
    another operation x1, other arithmetic, shards(): lax.linalg.triangular_solve(factor, jnp.eye(B, dtype=factor.dtype), left_...  4.9 us
    unnamed x12, local copies, waits for them, and re-layouts  2.76 us
    ppermute x4, local copies, waits for them, and re-layouts, tree_broadcast(): got = lax.ppermute(x, axes, pairs)  2.73 us
    select_n x9, other arithmetic, tree_broadcast(): fresh = jnp.where(take, got, fresh)  2.55 us
  transfers between devices with their start and end apart: 21, of which 2 were waited for; matrix products, arithmetic and copies ran while one was open for 19% of the time, Pallas kernels for 0%

profile of v15, /device:TPU:38, one launch (start us, length us, event | category | flops | bytes accessed | tf_op | source)
XLA Modules:
  0.0 101.8 jit_solution(4985932727440580581)
XLA Ops:
  0.0 1.1 %slice_bitcast_fusion = f32[64,1280]{0,1:T(8,128)S(1)} fusion(f32[1280,384]{1,0:T(8,128)} %param.1), kind=kLoop, calls=%fused_computation.3 | loop fusion | bytes 655360 | tf_op jit(solution)/shard_map/transpose | solution.py:39
  1.1 0.7 collective-permute-start.3
  1.8 0.7 collective-permute-start.2
  2.5 0.7 collective-permute-start.1
  3.2 0.7 collective-permute-start.6
  3.9 0.7 collective-permute-start.5
  4.6 0.7 collective-permute-start.4
  5.3 0.7 collective-permute-start.8
  6.0 0.7 collective-permute-start.7
  6.7 0.2 copy.12
  6.9 0.7 collective-permute-start
  7.8 5.8 %cholesky.20 = f32[64,64]{1,0:T(8,128)S(1)} custom-call(f32[64,64]{1,0:T(8,128)S(1)} %fusion.6), custom_call_target="Cholesky" | custom-call | tf_op jit(solution)/shard_map/jit(cholesky)/cholesky | solution.py:66
  13.7 0.6 compare_reduce_fusion
  14.4 0.7 fusion.12
  15.0 4.9 %custom-call.6 = f32[1,64,64]{1,2,0:T(8,128)S(1)} custom-call(f32[1,64,64]{2,1,0:T(8,128)S(1)} %get-tuple-element.24), custom_call_target="InvertDiagBlocksLowerTriangular" | custom-call | tf_op jit(solution)/shard_map/triangular_solve | solution.py:67
  19.9 0.2 fusion.4
  20.2 0.7 collective-permute-start.9
  21.0 0.7 collective-permute-start.10
  21.7 0.7 collective-permute-start.11
  22.4 0.2 copy.13
  22.6 1.2 %broadcast_select_fusion = f32[64,1280]{0,1:T(8,128)S(1)} fusion(f32[64,1280]{0,1:T(8,128)S(1)} %copy.13, pred[]{:T(512)S(6)} %and.110, f32[1280,384]{1,0:T(8,128)} %param.1), kind=kLoop, calls=%fused_computation.6 | loop fusion | flops 81920 | bytes 983041 | tf_op jit(solution)/shard_map/jit(_where)/select_n | solution.py:24
  23.8 0.2 copy.17
  24.0 1.3 %collective-permute-start.12 = (f32[64,1280]{1,0:T(8,128)S(1)}, f32[64,1280]{1,0:T(8,128)S(1)}, u32[]{:S(2)}, u32[]{:S(2)}) collective-permute-start(f32[64,1280]{1,0:T(8,128)S(1)} %copy.17), channel_id=1, source_target_pairs={{0,8},{1,9},{16,24},{17,25},{32,40},{33,41},{48,56},{49,57},{64,72... | collective-permute-start | bytes 983048 | tf_op jit(solution)/shard_map/ppermute | solution.py:22
  25.4 1.4 %collective-permute-start.17 = (f32[64,512]{0,1:T(8,128)S(1)}, f32[64,512]{0,1:T(8,128)}, u32[]{:S(2)}, u32[]{:S(2)}) collective-permute-start(f32[64,512]{0,1:T(8,128)S(1)} %maximum_select_fusion), channel_id=1, source_target_pairs={{0,16},{256,272},{512,528},{17,33},{273,289},{529,545},{34,50},{29... | collective-permute-start | bytes 393224 | tf_op jit(solution)/shard_map/ppermute | solution.py:22
  26.8 0.7 collective-permute-start.16
  27.4 1.4 %collective-permute-start.15 = (f32[64,512]{0,1:T(8,128)S(1)}, f32[64,512]{0,1:T(8,128)}, u32[]{:S(2)}, u32[]{:S(2)}) collective-permute-start(f32[64,512]{0,1:T(8,128)S(1)} %maximum_select_fusion), channel_id=1, source_target_pairs={{0,48},{256,304},{512,560},{17,65},{273,321},{529,577},{34,82},{29... | collective-permute-start | bytes 393224 | tf_op jit(solution)/shard_map/ppermute | solution.py:22
  28.8 23.5 %collective-permute-done.12 = f32[64,1280]{1,0:T(8,128)S(1)} collective-permute-done((f32[64,1280]{1,0:T(8,128)S(1)}, f32[64,1280]{1,0:T(8,128)S(1)}, u32[]{:S(2)}, u32[]{:S(2)}) %collective-permute-start.12) | collective-permute-done | bytes 327712 | tf_op jit(solution)/shard_map/ppermute | solution.py:22
  52.4 0.2 copy.18
  52.7 0.9 copy.19
  53.6 1.3 %collective-permute-start.13 = (f32[64,1280]{1,0:T(8,128)}, f32[64,1280]{1,0:T(8,128)S(1)}, u32[]{:S(2)}, u32[]{:S(2)}) collective-permute-start(f32[64,1280]{1,0:T(8,128)} %copy.19), channel_id=1, source_target_pairs={{0,4},{1,5},{8,12},{9,13},{16,20},{17,21},{24,28},{25,29},{32,36},... | collective-permute-start | bytes 983048 | tf_op jit(solution)/shard_map/ppermute | solution.py:22
  55.0 1.9 %copy.28 = f32[1280,384]{0,1:T(8,128)S(1)} copy(f32[1280,384]{1,0:T(8,128)} %param.1) | data formatting | bytes 3932160 | tf_op args[0]
  56.9 0.7 copy-done.1
  57.7 1.4 %collective-permute-start.20 = (f32[64,512]{0,1:T(8,128)S(1)}, f32[64,512]{0,1:T(8,128)}, u32[]{:S(2)}, u32[]{:S(2)}) collective-permute-start(f32[64,512]{0,1:T(8,128)S(1)} %select_select_fusion.1), channel_id=1, source_target_pairs={{0,64},{16,80},{32,96},{48,112},{256,320},{272,336},{288,352},{304... | collective-permute-start | bytes 393224 | tf_op jit(solution)/shard_map/ppermute | solution.py:22
  59.1 1.4 %collective-permute-start.19 = (f32[64,512]{0,1:T(8,128)S(1)}, f32[64,512]{0,1:T(8,128)}, u32[]{:S(2)}, u32[]{:S(2)}) collective-permute-start(f32[64,512]{0,1:T(8,128)S(1)} %select_select_fusion.1), channel_id=1, source_target_pairs={{0,128},{16,144},{32,160},{48,176},{256,384},{272,400},{288,416},{... | collective-permute-start | bytes 393224 | tf_op jit(solution)/shard_map/ppermute | solution.py:22
  60.4 1.3 %collective-permute-start.18 = (f32[64,512]{0,1:T(8,128)S(1)}, f32[64,512]{0,1:T(8,128)}, u32[]{:S(2)}, u32[]{:S(2)}) collective-permute-start(f32[64,512]{0,1:T(8,128)S(1)} %select_select_fusion.1), channel_id=1, source_target_pairs={{0,192},{16,208},{32,224},{48,240},{256,448},{272,464},{288,480},{... | collective-permute-start | bytes 393224 | tf_op jit(solution)/shard_map/ppermute | solution.py:22
  61.8 1.1 %copy.20 = f32[64,1280]{0,1:T(8,128)} copy(f32[64,1280]{1,0:T(8,128)S(1)} %collective-permute-done.13) | data formatting | bytes 655360 | tf_op jit(solution)/shard_map/ppermute | solution.py:22
  62.9 0.2 copy.21
  63.1 2.0 %collective-permute-start.14 = (f32[64,1280]{1,0:T(8,128)S(1)}, f32[64,1280]{1,0:T(8,128)}, u32[]{:S(2)}, u32[]{:S(2)}) collective-permute-start(f32[64,1280]{1,0:T(8,128)S(1)} %copy.21), channel_id=1, source_target_pairs={{0,2},{1,3},{8,10},{9,11},{4,6},{5,7},{12,14},{13,15},{16,18},{17,... | collective-permute-start | bytes 983048 | tf_op jit(solution)/shard_map/ppermute | solution.py:22
  65.2 28.1 %collective-permute-done.18 = f32[64,512]{0,1:T(8,128)} collective-permute-done((f32[64,512]{0,1:T(8,128)S(1)}, f32[64,512]{0,1:T(8,128)}, u32[]{:S(2)}, u32[]{:S(2)}) %collective-permute-start.18) | collective-permute-done | bytes 131104 | tf_op jit(solution)/shard_map/ppermute | solution.py:22
  93.3 1.1 %select_select_fusion = f32[64,512]{0,1:T(8,128)S(1)} fusion(f32[64,512]{0,1:T(8,128)} %collective-permute-done.18, f32[64,512]{0,1:T(8,128)} %collective-permute-done.19, f32[64,512]{0,1:T(8,128)} %collective-permute-done.20, f32[64,512]{0,1:T(8,128)} %copy-done, pred[]{:T(512)S(6)} %and.130, pred[]{:T(512)S(6)} %and.129, pred[]{:T(512)S(6)} %and.121), kind=kLoop, calls=%fused_computation.11 | loop fusion | flops 98304 | bytes 655363 | tf_op jit(solution)/shard_map/jit(_where)/select_n | solution.py:24
  94.4 1.2 %copy.22 = f32[64,1280]{0,1:T(8,128)S(1)} copy(f32[64,1280]{1,0:T(8,128)} %collective-permute-done.14) | data formatting | bytes 655360 | tf_op jit(solution)/shard_map/ppermute | solution.py:22
  95.7 0.9 fusion.10
  96.6 0.1 slice.97
  96.8 0.4 fusion.8
  97.7 1.9 %fusion = f32[1280,384]{0,1:T(8,128)S(1)} fusion(f32[1280,384]{0,1:T(8,128)S(1)} %copy.28, pred[1280]{0:T(1024)(128)(4,1)S(1)} %fusion.13, f32[64,1216]{1,0:T(8,128)S(1)} %slice.97, f32[64,64]{1,0:T(8,128)S(1)} %copy.24, f32[64,320]{1,0:T(8,128)S(1)} %slice.99, f32[64,64]{1,0:T(8,128)S(1)} %copy.26), kind=kOutput, calls=%fused_computation.1 | convolution fusion | flops 378576896 | bytes 4359424 | tf_op jit(solution)/shard_map/dot_general | solution.py:128
  99.6 0.2 slice_select_fusion
  99.9 0.1 pad_maximum_fusion
  100.0 1.8 %copy.29 = f32[1280,384]{1,0:T(8,128)} copy(f32[1280,384]{0,1:T(8,128)S(1)} %pad_maximum_fusion) | data formatting | bytes 3932160 | tf_op jit(solution)/shard_map/concatenate | solution.py:139
  (56 shorter events, 1.2 us)
Async XLA Ops:
  1.1 2.0 %collective-permute-start.3 = (f32[64,64]{0,1:T(8,128)S(1)}, f32[64,64]{0,1:T(8,128)S(1)}, u32[]{:S(2)}, u32[]{:S(2)}) collective-permute-start(f32[64,64]{0,1:T(8,128)S(1)} %slice.95), channel_id=1, source_target_pairs={{0,16}} | collective-permute-start | bytes 49160 | tf_op jit(solution)/shard_map/ppermute | solution.py:22
  1.8 1.4 %collective-permute-start.2 = (f32[64,64]{0,1:T(8,128)S(1)}, f32[64,64]{0,1:T(8,128)S(1)}, u32[]{:S(2)}, u32[]{:S(2)}) collective-permute-start(f32[64,64]{0,1:T(8,128)S(1)} %slice.95), channel_id=1, source_target_pairs={{0,32}} | collective-permute-start | bytes 49160 | tf_op jit(solution)/shard_map/ppermute | solution.py:22
  2.5 0.7 collective-permute-start.1
  3.2 2.0 %collective-permute-start.6 = (f32[64,64]{0,1:T(8,128)S(1)}, f32[64,64]{0,1:T(8,128)S(1)}, u32[]{:S(2)}, u32[]{:S(2)}) collective-permute-start(f32[64,64]{0,1:T(8,128)S(1)} %select_select_fusion.8), channel_id=1, source_target_pairs={{0,64},{16,80},{32,96},{48,112}} | collective-permute-start | bytes 49160 | tf_op jit(solution)/shard_map/ppermute | solution.py:22
  3.9 1.4 %collective-permute-start.5 = (f32[64,64]{0,1:T(8,128)S(1)}, f32[64,64]{0,1:T(8,128)S(1)}, u32[]{:S(2)}, u32[]{:S(2)}) collective-permute-start(f32[64,64]{0,1:T(8,128)S(1)} %select_select_fusion.8), channel_id=1, source_target_pairs={{0,128},{16,144},{32,160},{48,176}} | collective-permute-start | bytes 49160 | tf_op jit(solution)/shard_map/ppermute | solution.py:22
  4.6 0.7 collective-permute-start.4
  5.3 2.3 %collective-permute-start.8 = (f32[64,64]{0,1:T(8,128)S(1)}, f32[64,64]{0,1:T(8,128)S(1)}, u32[]{:S(2)}, u32[]{:S(2)}) collective-permute-start(f32[64,64]{0,1:T(8,128)S(1)} %select_select_fusion.7), channel_id=1, source_target_pairs={{0,256},{16,272},{32,288},{48,304},{64,320},{80,336},{96,352},{112... | collective-permute-start | bytes 49160 | tf_op jit(solution)/shard_map/ppermute | solution.py:22
  6.0 1.6 %collective-permute-start.7 = (f32[64,64]{0,1:T(8,128)S(1)}, f32[64,64]{0,1:T(8,128)S(1)}, u32[]{:S(2)}, u32[]{:S(2)}) collective-permute-start(f32[64,64]{0,1:T(8,128)S(1)} %select_select_fusion.7), channel_id=1, source_target_pairs={{0,512},{16,528},{32,544},{48,560},{64,576},{80,592},{96,608},{112... | collective-permute-start | bytes 49160 | tf_op jit(solution)/shard_map/ppermute | solution.py:22
  6.9 15.5 %collective-permute-start = (f32[64,1280]{1,0:T(8,128)S(1)}, f32[64,1280]{1,0:T(8,128)S(1)}, u32[]{:S(2)}, u32[]{:S(2)}) collective-permute-start(f32[64,1280]{1,0:T(8,128)S(1)} %copy.12), channel_id=1, source_target_pairs={{0,1},{16,17},{32,33},{48,49},{64,65},{80,81},{96,97},{112,113},{1... | collective-permute-start | bytes 983048 | tf_op jit(solution)/shard_map/ppermute | solution.py:22
  20.2 2.2 %collective-permute-start.9 = (f32[64,256]{0,1:T(8,128)S(1)}, f32[64,256]{0,1:T(8,128)S(1)}, u32[]{:S(2)}, u32[]{:S(2)}) collective-permute-start(f32[64,256]{0,1:T(8,128)S(1)} %pad_maximum_fusion.3), channel_id=1, source_target_pairs={{16,17},{32,34},{48,51},{64,68},{80,85},{96,102},{112,119},{128,13... | collective-permute-start | bytes 196616 | tf_op jit(solution)/shard_map/ppermute | solution.py:78
  21.0 2.8 %collective-permute-start.10 = (f32[64,256]{0,1:T(8,128)S(1)}, f32[64,256]{0,1:T(8,128)S(1)}, u32[]{:S(2)}, u32[]{:S(2)}) collective-permute-start(f32[64,256]{0,1:T(8,128)S(1)} %pad_maximum_fusion.3), channel_id=1, source_target_pairs={{0,256},{16,273},{32,290},{48,307},{64,324},{80,341},{96,358},{112... | collective-permute-start | bytes 196616 | tf_op jit(solution)/shard_map/ppermute | solution.py:78
  21.7 2.1 %collective-permute-start.11 = (f32[64,256]{0,1:T(8,128)S(1)}, f32[64,256]{0,1:T(8,128)S(1)}, u32[]{:S(2)}, u32[]{:S(2)}) collective-permute-start(f32[64,256]{0,1:T(8,128)S(1)} %pad_maximum_fusion.3), channel_id=1, source_target_pairs={{0,512},{16,529},{32,546},{48,563},{64,580},{80,597},{96,614},{112... | collective-permute-start | bytes 196616 | tf_op jit(solution)/shard_map/ppermute | solution.py:78
  24.0 28.3 %collective-permute-start.12 = (f32[64,1280]{1,0:T(8,128)S(1)}, f32[64,1280]{1,0:T(8,128)S(1)}, u32[]{:S(2)}, u32[]{:S(2)}) collective-permute-start(f32[64,1280]{1,0:T(8,128)S(1)} %copy.17), channel_id=1, source_target_pairs={{0,8},{1,9},{16,24},{17,25},{32,40},{33,41},{48,56},{49,57},{64,72... | collective-permute-start | bytes 983048 | tf_op jit(solution)/shard_map/ppermute | solution.py:22
  25.4 31.5 %collective-permute-start.17 = (f32[64,512]{0,1:T(8,128)S(1)}, f32[64,512]{0,1:T(8,128)}, u32[]{:S(2)}, u32[]{:S(2)}) collective-permute-start(f32[64,512]{0,1:T(8,128)S(1)} %maximum_select_fusion), channel_id=1, source_target_pairs={{0,16},{256,272},{512,528},{17,33},{273,289},{529,545},{34,50},{29... | collective-permute-start | bytes 393224 | tf_op jit(solution)/shard_map/ppermute | solution.py:22
  26.8 30.1 %collective-permute-start.16 = (f32[64,512]{0,1:T(8,128)S(1)}, f32[64,512]{0,1:T(8,128)S(1)}, u32[]{:S(2)}, u32[]{:S(2)}) collective-permute-start(f32[64,512]{0,1:T(8,128)S(1)} %maximum_select_fusion), channel_id=1, source_target_pairs={{0,32},{256,288},{512,544},{17,49},{273,305},{529,561},{34,66},{29... | collective-permute-start | bytes 393224 | tf_op jit(solution)/shard_map/ppermute | solution.py:22
  27.4 30.2 %collective-permute-start.15 = (f32[64,512]{0,1:T(8,128)S(1)}, f32[64,512]{0,1:T(8,128)}, u32[]{:S(2)}, u32[]{:S(2)}) collective-permute-start(f32[64,512]{0,1:T(8,128)S(1)} %maximum_select_fusion), channel_id=1, source_target_pairs={{0,48},{256,304},{512,560},{17,65},{273,321},{529,577},{34,82},{29... | collective-permute-start | bytes 393224 | tf_op jit(solution)/shard_map/ppermute | solution.py:22
  53.6 8.1 %collective-permute-start.13 = (f32[64,1280]{1,0:T(8,128)}, f32[64,1280]{1,0:T(8,128)S(1)}, u32[]{:S(2)}, u32[]{:S(2)}) collective-permute-start(f32[64,1280]{1,0:T(8,128)} %copy.19), channel_id=1, source_target_pairs={{0,4},{1,5},{8,12},{9,13},{16,20},{17,21},{24,28},{25,29},{32,36},... | collective-permute-start | bytes 983048 | tf_op jit(solution)/shard_map/ppermute | solution.py:22
  56.9 0.7 copy-start.1
  57.7 7.5 %copy-start = (f32[64,512]{0,1:T(8,128)}, f32[64,512]{0,1:T(8,128)S(1)}, u32[]{:S(2)}) copy-start(f32[64,512]{0,1:T(8,128)S(1)} %select_select_fusion.1) | copy-start | bytes 393220
  57.7 7.5 %collective-permute-start.20 = (f32[64,512]{0,1:T(8,128)S(1)}, f32[64,512]{0,1:T(8,128)}, u32[]{:S(2)}, u32[]{:S(2)}) collective-permute-start(f32[64,512]{0,1:T(8,128)S(1)} %select_select_fusion.1), channel_id=1, source_target_pairs={{0,64},{16,80},{32,96},{48,112},{256,320},{272,336},{288,352},{304... | collective-permute-start | bytes 393224 | tf_op jit(solution)/shard_map/ppermute | solution.py:22
  59.1 6.1 %collective-permute-start.19 = (f32[64,512]{0,1:T(8,128)S(1)}, f32[64,512]{0,1:T(8,128)}, u32[]{:S(2)}, u32[]{:S(2)}) collective-permute-start(f32[64,512]{0,1:T(8,128)S(1)} %select_select_fusion.1), channel_id=1, source_target_pairs={{0,128},{16,144},{32,160},{48,176},{256,384},{272,400},{288,416},{... | collective-permute-start | bytes 393224 | tf_op jit(solution)/shard_map/ppermute | solution.py:22
  60.4 32.9 %collective-permute-start.18 = (f32[64,512]{0,1:T(8,128)S(1)}, f32[64,512]{0,1:T(8,128)}, u32[]{:S(2)}, u32[]{:S(2)}) collective-permute-start(f32[64,512]{0,1:T(8,128)S(1)} %select_select_fusion.1), channel_id=1, source_target_pairs={{0,192},{16,208},{32,224},{48,240},{256,448},{272,464},{288,480},{... | collective-permute-start | bytes 393224 | tf_op jit(solution)/shard_map/ppermute | solution.py:22
  63.1 31.3 %collective-permute-start.14 = (f32[64,1280]{1,0:T(8,128)S(1)}, f32[64,1280]{1,0:T(8,128)}, u32[]{:S(2)}, u32[]{:S(2)}) collective-permute-start(f32[64,1280]{1,0:T(8,128)S(1)} %copy.21), channel_id=1, source_target_pairs={{0,2},{1,3},{8,10},{9,11},{4,6},{5,7},{12,14},{13,15},{16,18},{17,... | collective-permute-start | bytes 983048 | tf_op jit(solution)/shard_map/ppermute | solution.py:22

commit v16 on v15

--- a/solution.py
+++ b/solution.py
@@ -42,7 +42,7 @@
     def col0_group(_):
         return [lambda m: m * n_col]
 
-    corner_t = tree_broadcast(panel_t[:, :B], ("row", "col"), n_row, col0_group, row_id, radix=4)
+    corner_t = tree_broadcast(panel_t[:, :B], ("row", "col"), n_row, col0_group, row_id, radix=8)
 
     bits = n_col.bit_length() - 1
 

time: 102 us -> 101 us (level)
  the two profiles are of different devices: /device:TPU:38 before, /device:TPU:104 now
where the time goes in v16:
time: 101 us; the launch traced here: 99.9 us
  waiting for transfers between devices  49.1 us (49%)
  starting transfers between devices  20.7 us (20%)
  other arithmetic  15 us (15%)
  local copies, waits for them, and re-layouts  10.6 us (10%)
  matrix products  3.45 us (3%)
    ppermute x22, waiting for transfers between devices, tree_broadcast(): got = lax.ppermute(x, axes, pairs)  49.1 us
    ppermute x22, starting transfers between devices, tree_broadcast(): got = lax.ppermute(x, axes, pairs)  18.7 us
    another operation x3, other arithmetic, shards(): factor = jnp.linalg.cholesky(corner)  6.52 us
    another operation x1, other arithmetic, shards(): lax.linalg.triangular_solve(factor, jnp.eye(B, dtype=factor.dtype), left_...  4.9 us
    unnamed x12, local copies, waits for them, and re-layouts  2.78 us
    ppermute x4, local copies, waits for them, and re-layouts, tree_broadcast(): got = lax.ppermute(x, axes, pairs)  2.73 us
    select_n x8, other arithmetic, tree_broadcast(): fresh = jnp.where(take, got, fresh)  2.55 us
  transfers between devices with their start and end apart: 25, of which 2 were waited for; matrix products, arithmetic and copies ran while one was open for 20% of the time, Pallas kernels for 0%

profile of v16, /device:TPU:104, one launch (start us, length us, event | category | flops | bytes accessed | tf_op | source)
XLA Modules:
  0.0 99.9 jit_solution(6751369847117643185)
XLA Ops:
  0.0 1.1 %slice_bitcast_fusion = f32[64,1280]{0,1:T(8,128)S(1)} fusion(f32[1280,384]{1,0:T(8,128)} %param.1), kind=kLoop, calls=%fused_computation.3 | loop fusion | bytes 655360 | tf_op jit(solution)/shard_map/transpose | solution.py:39
  1.1 0.7 collective-permute-start.7
  1.8 0.7 collective-permute-start.6
  2.5 0.7 collective-permute-start.5
  3.2 0.7 collective-permute-start.4
  3.8 0.7 collective-permute-start.3
  4.5 0.7 collective-permute-start.2
  5.2 0.7 collective-permute-start.1
  6.0 0.7 collective-permute-start.12
  6.7 0.7 collective-permute-start.11
  7.3 0.7 collective-permute-start.10
  8.0 0.7 collective-permute-start.9
  8.7 0.7 collective-permute-start.8
  9.4 0.2 copy.12
  9.6 0.7 collective-permute-start
  10.6 5.8 %cholesky.20 = f32[64,64]{1,0:T(8,128)S(1)} custom-call(f32[64,64]{1,0:T(8,128)S(1)} %fusion.6), custom_call_target="Cholesky" | custom-call | tf_op jit(solution)/shard_map/jit(cholesky)/cholesky | solution.py:66
  16.5 0.6 compare_reduce_fusion
  17.1 0.7 fusion.12
  17.8 4.9 %custom-call.6 = f32[1,64,64]{1,2,0:T(8,128)S(1)} custom-call(f32[1,64,64]{2,1,0:T(8,128)S(1)} %get-tuple-element.24), custom_call_target="InvertDiagBlocksLowerTriangular" | custom-call | tf_op jit(solution)/shard_map/triangular_solve | solution.py:67
  22.7 0.2 fusion.4
  22.9 0.7 collective-permute-start.13
  23.7 0.7 collective-permute-start.14
  24.4 0.7 collective-permute-start.15
  25.1 0.2 copy.13
  25.4 1.2 %broadcast_select_fusion = f32[64,1280]{0,1:T(8,128)S(1)} fusion(f32[64,1280]{0,1:T(8,128)S(1)} %copy.13, pred[]{:T(512)S(6)} %and.122, f32[1280,384]{1,0:T(8,128)} %param.1), kind=kLoop, calls=%fused_computation.6 | loop fusion | flops 81920 | bytes 983041 | tf_op jit(solution)/shard_map/jit(_where)/select_n | solution.py:24
  26.6 0.2 copy.17
  26.8 0.7 collective-permute-start.16
  27.5 1.4 %collective-permute-start.21 = (f32[64,512]{0,1:T(8,128)S(1)}, f32[64,512]{0,1:T(8,128)}, u32[]{:S(2)}, u32[]{:S(2)}) collective-permute-start(f32[64,512]{0,1:T(8,128)S(1)} %maximum_select_fusion), channel_id=1, source_target_pairs={{0,16},{256,272},{512,528},{17,33},{273,289},{529,545},{34,50},{29... | collective-permute-start | bytes 393224 | tf_op jit(solution)/shard_map/ppermute | solution.py:22
  28.9 0.7 collective-permute-start.20
  29.6 1.4 %collective-permute-start.19 = (f32[64,512]{0,1:T(8,128)S(1)}, f32[64,512]{0,1:T(8,128)}, u32[]{:S(2)}, u32[]{:S(2)}) collective-permute-start(f32[64,512]{0,1:T(8,128)S(1)} %maximum_select_fusion), channel_id=1, source_target_pairs={{0,48},{256,304},{512,560},{17,65},{273,321},{529,577},{34,82},{29... | collective-permute-start | bytes 393224 | tf_op jit(solution)/shard_map/ppermute | solution.py:22
  31.0 0.2 copy.18
  31.3 0.9 copy.19
  32.2 0.7 collective-permute-start.17
  33.0 1.9 %copy.28 = f32[1280,384]{0,1:T(8,128)S(1)} copy(f32[1280,384]{1,0:T(8,128)} %param.1) | data formatting | bytes 3932160 | tf_op args[0]
  34.9 0.7 copy-done.1
  35.7 1.4 %collective-permute-start.24 = (f32[64,512]{0,1:T(8,128)S(1)}, f32[64,512]{0,1:T(8,128)}, u32[]{:S(2)}, u32[]{:S(2)}) collective-permute-start(f32[64,512]{0,1:T(8,128)S(1)} %select_select_fusion.1), channel_id=1, source_target_pairs={{0,64},{16,80},{32,96},{48,112},{256,320},{272,336},{288,352},{304... | collective-permute-start | bytes 393224 | tf_op jit(solution)/shard_map/ppermute | solution.py:22
  37.1 1.4 %collective-permute-start.23 = (f32[64,512]{0,1:T(8,128)S(1)}, f32[64,512]{0,1:T(8,128)}, u32[]{:S(2)}, u32[]{:S(2)}) collective-permute-start(f32[64,512]{0,1:T(8,128)S(1)} %select_select_fusion.1), channel_id=1, source_target_pairs={{0,128},{16,144},{32,160},{48,176},{256,384},{272,400},{288,416},{... | collective-permute-start | bytes 393224 | tf_op jit(solution)/shard_map/ppermute | solution.py:22
  38.5 1.3 %collective-permute-start.22 = (f32[64,512]{0,1:T(8,128)S(1)}, f32[64,512]{0,1:T(8,128)}, u32[]{:S(2)}, u32[]{:S(2)}) collective-permute-start(f32[64,512]{0,1:T(8,128)S(1)} %select_select_fusion.1), channel_id=1, source_target_pairs={{0,192},{16,208},{32,224},{48,240},{256,448},{272,464},{288,480},{... | collective-permute-start | bytes 393224 | tf_op jit(solution)/shard_map/ppermute | solution.py:22
  39.8 1.1 %copy.20 = f32[64,1280]{0,1:T(8,128)} copy(f32[64,1280]{1,0:T(8,128)S(1)} %collective-permute-done.17) | data formatting | bytes 655360 | tf_op jit(solution)/shard_map/ppermute | solution.py:22
  41.1 1.3 %collective-permute-start.18 = (f32[64,1280]{1,0:T(8,128)S(1)}, f32[64,1280]{1,0:T(8,128)}, u32[]{:S(2)}, u32[]{:S(2)}) collective-permute-start(f32[64,1280]{1,0:T(8,128)S(1)} %copy.21), channel_id=1, source_target_pairs={{0,2},{1,3},{8,10},{9,11},{4,6},{5,7},{12,14},{13,15},{16,18},{17,... | collective-permute-start | bytes 983048 | tf_op jit(solution)/shard_map/ppermute | solution.py:22
  42.5 42.7 %collective-permute-done.22 = f32[64,512]{0,1:T(8,128)} collective-permute-done((f32[64,512]{0,1:T(8,128)S(1)}, f32[64,512]{0,1:T(8,128)}, u32[]{:S(2)}, u32[]{:S(2)}) %collective-permute-start.22) | collective-permute-done | bytes 131104 | tf_op jit(solution)/shard_map/ppermute | solution.py:22
  85.2 1.1 %select_select_fusion = f32[64,512]{0,1:T(8,128)S(1)} fusion(f32[64,512]{0,1:T(8,128)} %collective-permute-done.22, f32[64,512]{0,1:T(8,128)} %collective-permute-done.23, f32[64,512]{0,1:T(8,128)} %collective-permute-done.24, f32[64,512]{0,1:T(8,128)} %copy-done, pred[]{:T(512)S(6)} %and.146, pred[]{:T(512)S(6)} %and.145, pred[]{:T(512)S(6)} %and.137), kind=kLoop, calls=%fused_computation.11 | loop fusion | flops 98304 | bytes 655363 | tf_op jit(solution)/shard_map/jit(_where)/select_n | solution.py:24
  86.3 6.3 %collective-permute-done.18 = f32[64,1280]{1,0:T(8,128)} collective-permute-done((f32[64,1280]{1,0:T(8,128)S(1)}, f32[64,1280]{1,0:T(8,128)}, u32[]{:S(2)}, u32[]{:S(2)}) %collective-permute-start.18) | collective-permute-done | bytes 327712 | tf_op jit(solution)/shard_map/ppermute | solution.py:22
  92.6 1.2 %copy.22 = f32[64,1280]{0,1:T(8,128)S(1)} copy(f32[64,1280]{1,0:T(8,128)} %collective-permute-done.18) | data formatting | bytes 655360 | tf_op jit(solution)/shard_map/ppermute | solution.py:22
  93.8 0.9 fusion.10
  94.9 0.4 fusion.8
  95.8 1.9 %fusion = f32[1280,384]{0,1:T(8,128)S(1)} fusion(f32[1280,384]{0,1:T(8,128)S(1)} %copy.28, pred[1280]{0:T(1024)(128)(4,1)S(1)} %fusion.13, f32[64,1216]{1,0:T(8,128)S(1)} %slice.97, f32[64,64]{1,0:T(8,128)S(1)} %copy.24, f32[64,320]{1,0:T(8,128)S(1)} %slice.99, f32[64,64]{1,0:T(8,128)S(1)} %copy.26), kind=kOutput, calls=%fused_computation.1 | convolution fusion | flops 378576896 | bytes 4359424 | tf_op jit(solution)/shard_map/dot_general | solution.py:128
  98.2 1.8 %copy.29 = f32[1280,384]{1,0:T(8,128)} copy(f32[1280,384]{0,1:T(8,128)S(1)} %pad_maximum_fusion) | data formatting | bytes 3932160 | tf_op jit(solution)/shard_map/concatenate | solution.py:139
  (63 shorter events, 1.9 us)
Async XLA Ops:
  1.1 3.4 %collective-permute-start.7 = (f32[64,64]{0,1:T(8,128)S(1)}, f32[64,64]{0,1:T(8,128)S(1)}, u32[]{:S(2)}, u32[]{:S(2)}) collective-permute-start(f32[64,64]{0,1:T(8,128)S(1)} %slice.95), channel_id=1, source_target_pairs={{0,16}} | collective-permute-start | bytes 49160 | tf_op jit(solution)/shard_map/ppermute | solution.py:22
  1.8 3.4 %collective-permute-start.6 = (f32[64,64]{0,1:T(8,128)S(1)}, f32[64,64]{0,1:T(8,128)S(1)}, u32[]{:S(2)}, u32[]{:S(2)}) collective-permute-start(f32[64,64]{0,1:T(8,128)S(1)} %slice.95), channel_id=1, source_target_pairs={{0,32}} | collective-permute-start | bytes 49160 | tf_op jit(solution)/shard_map/ppermute | solution.py:22
  2.5 3.4 %collective-permute-start.5 = (f32[64,64]{0,1:T(8,128)S(1)}, f32[64,64]{0,1:T(8,128)S(1)}, u32[]{:S(2)}, u32[]{:S(2)}) collective-permute-start(f32[64,64]{0,1:T(8,128)S(1)} %slice.95), channel_id=1, source_target_pairs={{0,48}} | collective-permute-start | bytes 49160 | tf_op jit(solution)/shard_map/ppermute | solution.py:22
  3.2 2.8 %collective-permute-start.4 = (f32[64,64]{0,1:T(8,128)S(1)}, f32[64,64]{0,1:T(8,128)S(1)}, u32[]{:S(2)}, u32[]{:S(2)}) collective-permute-start(f32[64,64]{0,1:T(8,128)S(1)} %slice.95), channel_id=1, source_target_pairs={{0,64}} | collective-permute-start | bytes 49160 | tf_op jit(solution)/shard_map/ppermute | solution.py:22
  3.8 2.1 %collective-permute-start.3 = (f32[64,64]{0,1:T(8,128)S(1)}, f32[64,64]{0,1:T(8,128)S(1)}, u32[]{:S(2)}, u32[]{:S(2)}) collective-permute-start(f32[64,64]{0,1:T(8,128)S(1)} %slice.95), channel_id=1, source_target_pairs={{0,80}} | collective-permute-start | bytes 49160 | tf_op jit(solution)/shard_map/ppermute | solution.py:22
  4.5 1.4 %collective-permute-start.2 = (f32[64,64]{0,1:T(8,128)S(1)}, f32[64,64]{0,1:T(8,128)S(1)}, u32[]{:S(2)}, u32[]{:S(2)}) collective-permute-start(f32[64,64]{0,1:T(8,128)S(1)} %slice.95), channel_id=1, source_target_pairs={{0,96}} | collective-permute-start | bytes 49160 | tf_op jit(solution)/shard_map/ppermute | solution.py:22
  5.2 0.8 collective-permute-start.1
  6.0 3.6 %collective-permute-start.12 = (f32[64,64]{0,1:T(8,128)S(1)}, f32[64,64]{0,1:T(8,128)S(1)}, u32[]{:S(2)}, u32[]{:S(2)}) collective-permute-start(f32[64,64]{0,1:T(8,128)S(1)} %select_select_fusion.7), channel_id=1, source_target_pairs={{0,128},{16,144},{32,160},{48,176},{64,192},{80,208},{96,224},{112... | collective-permute-start | bytes 49160 | tf_op jit(solution)/shard_map/ppermute | solution.py:22
  6.7 3.7 %collective-permute-start.11 = (f32[64,64]{0,1:T(8,128)S(1)}, f32[64,64]{0,1:T(8,128)S(1)}, u32[]{:S(2)}, u32[]{:S(2)}) collective-permute-start(f32[64,64]{0,1:T(8,128)S(1)} %select_select_fusion.7), channel_id=1, source_target_pairs={{0,256},{16,272},{32,288},{48,304},{64,320},{80,336},{96,352},{112... | collective-permute-start | bytes 49160 | tf_op jit(solution)/shard_map/ppermute | solution.py:22
  7.3 3.0 %collective-permute-start.10 = (f32[64,64]{0,1:T(8,128)S(1)}, f32[64,64]{0,1:T(8,128)S(1)}, u32[]{:S(2)}, u32[]{:S(2)}) collective-permute-start(f32[64,64]{0,1:T(8,128)S(1)} %select_select_fusion.7), channel_id=1, source_target_pairs={{0,384},{16,400},{32,416},{48,432},{64,448},{80,464},{96,480},{112... | collective-permute-start | bytes 49160 | tf_op jit(solution)/shard_map/ppermute | solution.py:22
  8.0 2.4 %collective-permute-start.9 = (f32[64,64]{0,1:T(8,128)S(1)}, f32[64,64]{0,1:T(8,128)S(1)}, u32[]{:S(2)}, u32[]{:S(2)}) collective-permute-start(f32[64,64]{0,1:T(8,128)S(1)} %select_select_fusion.7), channel_id=1, source_target_pairs={{0,512},{16,528},{32,544},{48,560},{64,576},{80,592},{96,608},{112... | collective-permute-start | bytes 49160 | tf_op jit(solution)/shard_map/ppermute | solution.py:22
  8.7 1.7 %collective-permute-start.8 = (f32[64,64]{0,1:T(8,128)S(1)}, f32[64,64]{0,1:T(8,128)S(1)}, u32[]{:S(2)}, u32[]{:S(2)}) collective-permute-start(f32[64,64]{0,1:T(8,128)S(1)} %select_select_fusion.7), channel_id=1, source_target_pairs={{0,640},{16,656},{32,672},{48,688},{64,704},{80,720},{96,736},{112... | collective-permute-start | bytes 49160 | tf_op jit(solution)/shard_map/ppermute | solution.py:22
  9.6 15.5 %collective-permute-start = (f32[64,1280]{1,0:T(8,128)S(1)}, f32[64,1280]{1,0:T(8,128)S(1)}, u32[]{:S(2)}, u32[]{:S(2)}) collective-permute-start(f32[64,1280]{1,0:T(8,128)S(1)} %copy.12), channel_id=1, source_target_pairs={{0,1},{16,17},{32,33},{48,49},{64,65},{80,81},{96,97},{112,113},{1... | collective-permute-start | bytes 983048 | tf_op jit(solution)/shard_map/ppermute | solution.py:22
  22.9 2.2 %collective-permute-start.13 = (f32[64,256]{0,1:T(8,128)S(1)}, f32[64,256]{0,1:T(8,128)S(1)}, u32[]{:S(2)}, u32[]{:S(2)}) collective-permute-start(f32[64,256]{0,1:T(8,128)S(1)} %pad_maximum_fusion.3), channel_id=1, source_target_pairs={{16,17},{32,34},{48,51},{64,68},{80,85},{96,102},{112,119},{128,13... | collective-permute-start | bytes 196616 | tf_op jit(solution)/shard_map/ppermute | solution.py:78
  23.7 2.8 %collective-permute-start.14 = (f32[64,256]{0,1:T(8,128)S(1)}, f32[64,256]{0,1:T(8,128)S(1)}, u32[]{:S(2)}, u32[]{:S(2)}) collective-permute-start(f32[64,256]{0,1:T(8,128)S(1)} %pad_maximum_fusion.3), channel_id=1, source_target_pairs={{0,256},{16,273},{32,290},{48,307},{64,324},{80,341},{96,358},{112... | collective-permute-start | bytes 196616 | tf_op jit(solution)/shard_map/ppermute | solution.py:78
  24.4 2.1 %collective-permute-start.15 = (f32[64,256]{0,1:T(8,128)S(1)}, f32[64,256]{0,1:T(8,128)S(1)}, u32[]{:S(2)}, u32[]{:S(2)}) collective-permute-start(f32[64,256]{0,1:T(8,128)S(1)} %pad_maximum_fusion.3), channel_id=1, source_target_pairs={{0,512},{16,529},{32,546},{48,563},{64,580},{80,597},{96,614},{112... | collective-permute-start | bytes 196616 | tf_op jit(solution)/shard_map/ppermute | solution.py:78
  26.8 4.2 %collective-permute-start.16 = (f32[64,1280]{1,0:T(8,128)S(1)}, f32[64,1280]{1,0:T(8,128)S(1)}, u32[]{:S(2)}, u32[]{:S(2)}) collective-permute-start(f32[64,1280]{1,0:T(8,128)S(1)} %copy.17), channel_id=1, source_target_pairs={{0,8},{1,9},{16,24},{17,25},{32,40},{33,41},{48,56},{49,57},{64,72... | collective-permute-start | bytes 983048 | tf_op jit(solution)/shard_map/ppermute | solution.py:22
  27.5 7.4 %collective-permute-start.21 = (f32[64,512]{0,1:T(8,128)S(1)}, f32[64,512]{0,1:T(8,128)}, u32[]{:S(2)}, u32[]{:S(2)}) collective-permute-start(f32[64,512]{0,1:T(8,128)S(1)} %maximum_select_fusion), channel_id=1, source_target_pairs={{0,16},{256,272},{512,528},{17,33},{273,289},{529,545},{34,50},{29... | collective-permute-start | bytes 393224 | tf_op jit(solution)/shard_map/ppermute | solution.py:22
  28.9 6.0 %collective-permute-start.20 = (f32[64,512]{0,1:T(8,128)S(1)}, f32[64,512]{0,1:T(8,128)S(1)}, u32[]{:S(2)}, u32[]{:S(2)}) collective-permute-start(f32[64,512]{0,1:T(8,128)S(1)} %maximum_select_fusion), channel_id=1, source_target_pairs={{0,32},{256,288},{512,544},{17,49},{273,305},{529,561},{34,66},{29... | collective-permute-start | bytes 393224 | tf_op jit(solution)/shard_map/ppermute | solution.py:22
  29.6 6.0 %collective-permute-start.19 = (f32[64,512]{0,1:T(8,128)S(1)}, f32[64,512]{0,1:T(8,128)}, u32[]{:S(2)}, u32[]{:S(2)}) collective-permute-start(f32[64,512]{0,1:T(8,128)S(1)} %maximum_select_fusion), channel_id=1, source_target_pairs={{0,48},{256,304},{512,560},{17,65},{273,321},{529,577},{34,82},{29... | collective-permute-start | bytes 393224 | tf_op jit(solution)/shard_map/ppermute | solution.py:22
  32.2 7.5 %collective-permute-start.17 = (f32[64,1280]{1,0:T(8,128)}, f32[64,1280]{1,0:T(8,128)S(1)}, u32[]{:S(2)}, u32[]{:S(2)}) collective-permute-start(f32[64,1280]{1,0:T(8,128)} %copy.19), channel_id=1, source_target_pairs={{0,4},{1,5},{8,12},{9,13},{16,20},{17,21},{24,28},{25,29},{32,36},... | collective-permute-start | bytes 983048 | tf_op jit(solution)/shard_map/ppermute | solution.py:22
  34.9 0.7 copy-start.1
  35.7 6.8 %copy-start = (f32[64,512]{0,1:T(8,128)}, f32[64,512]{0,1:T(8,128)S(1)}, u32[]{:S(2)}) copy-start(f32[64,512]{0,1:T(8,128)S(1)} %select_select_fusion.1) | copy-start | bytes 393220
  35.7 6.7 %collective-permute-start.24 = (f32[64,512]{0,1:T(8,128)S(1)}, f32[64,512]{0,1:T(8,128)}, u32[]{:S(2)}, u32[]{:S(2)}) collective-permute-start(f32[64,512]{0,1:T(8,128)S(1)} %select_select_fusion.1), channel_id=1, source_target_pairs={{0,64},{16,80},{32,96},{48,112},{256,320},{272,336},{288,352},{304... | collective-permute-start | bytes 393224 | tf_op jit(solution)/shard_map/ppermute | solution.py:22
  37.1 5.4 %collective-permute-start.23 = (f32[64,512]{0,1:T(8,128)S(1)}, f32[64,512]{0,1:T(8,128)}, u32[]{:S(2)}, u32[]{:S(2)}) collective-permute-start(f32[64,512]{0,1:T(8,128)S(1)} %select_select_fusion.1), channel_id=1, source_target_pairs={{0,128},{16,144},{32,160},{48,176},{256,384},{272,400},{288,416},{... | collective-permute-start | bytes 393224 | tf_op jit(solution)/shard_map/ppermute | solution.py:22
  38.5 46.7 %collective-permute-start.22 = (f32[64,512]{0,1:T(8,128)S(1)}, f32[64,512]{0,1:T(8,128)}, u32[]{:S(2)}, u32[]{:S(2)}) collective-permute-start(f32[64,512]{0,1:T(8,128)S(1)} %select_select_fusion.1), channel_id=1, source_target_pairs={{0,192},{16,208},{32,224},{48,240},{256,448},{272,464},{288,480},{... | collective-permute-start | bytes 393224 | tf_op jit(solution)/shard_map/ppermute | solution.py:22
  41.1 51.4 %collective-permute-start.18 = (f32[64,1280]{1,0:T(8,128)S(1)}, f32[64,1280]{1,0:T(8,128)}, u32[]{:S(2)}, u32[]{:S(2)}) collective-permute-start(f32[64,1280]{1,0:T(8,128)S(1)} %copy.21), channel_id=1, source_target_pairs={{0,2},{1,3},{8,10},{9,11},{4,6},{5,7},{12,14},{13,15},{16,18},{17,... | collective-permute-start | bytes 983048 | tf_op jit(solution)/shard_map/ppermute | solution.py:22

commit v17 on v16

--- a/solution.py
+++ b/solution.py
@@ -100,7 +100,7 @@
                 out.append(lambda m, base=base, q=q: ((base + m) % n_row) * n_col + q)
         return out
 
-    packet = tree_broadcast(packet, ("row", "col"), n_col, row_groups, rel % n_col, radix=4)
+    packet = tree_broadcast(packet, ("row", "col"), n_col, row_groups, rel % n_col, radix=8)
     panel_t = tree_broadcast(panel_t, ("row", "col"), n_col, col_groups, col_member, radix=2, have=n_col // 2)
     panel_t, packet = lax.optimization_barrier((panel_t, packet))
     factor_t = packet[:, n_src * window_cols: n_src * window_cols + B]

time: 101 us -> 108 us (1.069)
  the two profiles are of different devices: /device:TPU:104 before, /device:TPU:61 now
where the time goes in v17:
time: 108 us; the launch traced here: 107 us
  waiting for transfers between devices  52.6 us (49%)
  starting transfers between devices  23.4 us (22%)
  other arithmetic  16.6 us (15%)
  local copies, waits for them, and re-layouts  9.91 us (9%)
  matrix products  3.45 us (3%)
    ppermute x24, waiting for transfers between devices, tree_broadcast(): got = lax.ppermute(x, axes, pairs)  52.5 us
    ppermute x24, starting transfers between devices, tree_broadcast(): got = lax.ppermute(x, axes, pairs)  21.4 us
    another operation x3, other arithmetic, shards(): factor = jnp.linalg.cholesky(corner)  6.52 us
    another operation x1, other arithmetic, shards(): lax.linalg.triangular_solve(factor, jnp.eye(B, dtype=factor.dtype), left_...  4.9 us
    select_n x8, other arithmetic, tree_broadcast(): fresh = jnp.where(take, got, fresh)  4.16 us
    unnamed x12, local copies, waits for them, and re-layouts  2.78 us
    ppermute x4, local copies, waits for them, and re-layouts, tree_broadcast(): got = lax.ppermute(x, axes, pairs)  2.73 us
  transfers between devices with their start and end apart: 27, of which 3 were waited for; matrix products, arithmetic and copies ran while one was open for 19% of the time, Pallas kernels for 0%

profile of v17, /device:TPU:61, one launch (start us, length us, event | category | flops | bytes accessed | tf_op | source)
XLA Modules:
  0.0 107.0 jit_solution(11980829992729901256)
XLA Ops:
  0.0 1.1 %slice_bitcast_fusion = f32[64,1280]{0,1:T(8,128)S(1)} fusion(f32[1280,384]{1,0:T(8,128)} %param.1), kind=kLoop, calls=%fused_computation.3 | loop fusion | bytes 655360 | tf_op jit(solution)/shard_map/transpose | solution.py:39
  1.1 0.7 collective-permute-start.7
  1.8 0.7 collective-permute-start.6
  2.5 0.7 collective-permute-start.5
  3.2 0.7 collective-permute-start.4
  3.8 0.7 collective-permute-start.3
  4.5 0.7 collective-permute-start.2
  5.2 0.7 collective-permute-start.1
  6.0 0.7 collective-permute-start.12
  6.7 0.7 collective-permute-start.11
  7.3 0.7 collective-permute-start.10
  8.0 0.7 collective-permute-start.9
  8.7 0.7 collective-permute-start.8
  9.6 0.7 collective-permute-start
  10.6 5.8 %cholesky.20 = f32[64,64]{1,0:T(8,128)S(1)} custom-call(f32[64,64]{1,0:T(8,128)S(1)} %fusion.6), custom_call_target="Cholesky" | custom-call | tf_op jit(solution)/shard_map/jit(cholesky)/cholesky | solution.py:66
  16.5 0.6 compare_reduce_fusion
  17.1 0.7 fusion.12
  17.8 4.9 %custom-call.6 = f32[1,64,64]{1,2,0:T(8,128)S(1)} custom-call(f32[1,64,64]{2,1,0:T(8,128)S(1)} %get-tuple-element.24), custom_call_target="InvertDiagBlocksLowerTriangular" | custom-call | tf_op jit(solution)/shard_map/triangular_solve | solution.py:67
  22.7 0.2 fusion.4
  22.9 0.7 collective-permute-start.13
  23.7 0.7 collective-permute-start.14
  24.4 0.7 collective-permute-start.15
  25.1 0.2 copy.13
  25.4 1.2 %broadcast_select_fusion = f32[64,1280]{0,1:T(8,128)S(1)} fusion(f32[64,1280]{0,1:T(8,128)S(1)} %copy.13, pred[]{:T(512)S(6)} %and.128, f32[1280,384]{1,0:T(8,128)} %param.1), kind=kLoop, calls=%fused_computation.6 | loop fusion | flops 81920 | bytes 983041 | tf_op jit(solution)/shard_map/jit(_where)/select_n | solution.py:24
  26.8 0.7 collective-permute-start.16
  27.5 0.7 collective-permute-start.25
  28.2 0.7 collective-permute-start.24
  28.9 1.4 %collective-permute-start.23 = (f32[64,512]{0,1:T(8,128)S(1)}, f32[64,512]{0,1:T(8,128)}, u32[]{:S(2)}, u32[]{:S(2)}) collective-permute-start(f32[64,512]{0,1:T(8,128)S(1)} %maximum_select_fusion), channel_id=1, source_target_pairs={{0,48},{256,304},{512,560},{17,65},{273,321},{529,577},{34,82},{29... | collective-permute-start | bytes 393224 | tf_op jit(solution)/shard_map/ppermute | solution.py:22
  30.3 1.4 %collective-permute-start.22 = (f32[64,512]{0,1:T(8,128)S(1)}, f32[64,512]{0,1:T(8,128)}, u32[]{:S(2)}, u32[]{:S(2)}) collective-permute-start(f32[64,512]{0,1:T(8,128)S(1)} %maximum_select_fusion), channel_id=1, source_target_pairs={{0,64},{256,320},{512,576},{17,81},{273,337},{529,593},{34,98},{29... | collective-permute-start | bytes 393224 | tf_op jit(solution)/shard_map/ppermute | solution.py:22
  31.7 1.4 %collective-permute-start.21 = (f32[64,512]{0,1:T(8,128)S(1)}, f32[64,512]{0,1:T(8,128)}, u32[]{:S(2)}, u32[]{:S(2)}) collective-permute-start(f32[64,512]{0,1:T(8,128)S(1)} %maximum_select_fusion), channel_id=1, source_target_pairs={{0,80},{256,336},{512,592},{17,97},{273,353},{529,609},{34,114},{2... | collective-permute-start | bytes 393224 | tf_op jit(solution)/shard_map/ppermute | solution.py:22
  33.3 1.4 %collective-permute-start.20 = (f32[64,512]{0,1:T(8,128)S(1)}, f32[64,512]{0,1:T(8,128)}, u32[]{:S(2)}, u32[]{:S(2)}) collective-permute-start(f32[64,512]{0,1:T(8,128)S(1)} %maximum_select_fusion), channel_id=1, source_target_pairs={{0,96},{256,352},{512,608},{17,113},{273,369},{529,625},{34,130},{... | collective-permute-start | bytes 393224 | tf_op jit(solution)/shard_map/ppermute | solution.py:22
  34.7 0.7 copy-done.1
  35.4 1.3 %collective-permute-start.19 = (f32[64,512]{0,1:T(8,128)S(1)}, f32[64,512]{0,1:T(8,128)}, u32[]{:S(2)}, u32[]{:S(2)}) collective-permute-start(f32[64,512]{0,1:T(8,128)S(1)} %maximum_select_fusion), channel_id=1, source_target_pairs={{0,112},{256,368},{512,624},{17,129},{273,385},{529,641},{34,146},... | collective-permute-start | bytes 393224 | tf_op jit(solution)/shard_map/ppermute | solution.py:22
  37.0 0.7 collective-permute-start.17
  37.7 1.9 %copy.28 = f32[1280,384]{0,1:T(8,128)S(1)} copy(f32[1280,384]{1,0:T(8,128)} %param.1) | data formatting | bytes 3932160 | tf_op args[0]
  39.7 45.0 %collective-permute-done.19 = f32[64,512]{0,1:T(8,128)} collective-permute-done((f32[64,512]{0,1:T(8,128)S(1)}, f32[64,512]{0,1:T(8,128)}, u32[]{:S(2)}, u32[]{:S(2)}) %collective-permute-start.19) | collective-permute-done | bytes 131104 | tf_op jit(solution)/shard_map/ppermute | solution.py:22
  84.7 1.8 %select_select_fusion = f32[64,512]{0,1:T(8,128)} fusion(f32[64,512]{0,1:T(8,128)} %collective-permute-done.19, f32[64,512]{0,1:T(8,128)} %collective-permute-done.20, f32[64,512]{0,1:T(8,128)} %collective-permute-done.21, f32[64,512]{0,1:T(8,128)} %collective-permute-done.22, f32[64,512]{0,1:T(8,128)} %collective-permute-done.23, f32[64,512]{0,1:T(8,128)} %copy-done.1, ...), kind=kLoop, calls=%fused_computation.11 | loop fusion | flops 229376 | bytes 1179655 | tf_op jit(solution)/shard_map/jit(_where)/select_n | solution.py:24
  86.4 2.0 %collective-permute-start.26 = (f32[64,512]{0,1:T(8,128)}, f32[64,512]{0,1:T(8,128)}, u32[]{:S(2)}, u32[]{:S(2)}) collective-permute-start(f32[64,512]{0,1:T(8,128)} %select_select_fusion), channel_id=1, source_target_pairs={{0,128},{16,144},{32,160},{48,176},{64,192},{80,208},{96,224},{112... | collective-permute-start | bytes 393224 | tf_op jit(solution)/shard_map/ppermute | solution.py:22
  88.5 1.1 %copy.20 = f32[64,1280]{0,1:T(8,128)} copy(f32[64,1280]{1,0:T(8,128)S(1)} %collective-permute-done.17) | data formatting | bytes 655360 | tf_op jit(solution)/shard_map/ppermute | solution.py:22
  89.8 1.3 %collective-permute-start.18 = (f32[64,1280]{1,0:T(8,128)S(1)}, f32[64,1280]{1,0:T(8,128)}, u32[]{:S(2)}, u32[]{:S(2)}) collective-permute-start(f32[64,1280]{1,0:T(8,128)S(1)} %copy.21), channel_id=1, source_target_pairs={{0,2},{1,3},{8,10},{9,11},{4,6},{5,7},{12,14},{13,15},{16,18},{17,... | collective-permute-start | bytes 983048 | tf_op jit(solution)/shard_map/ppermute | solution.py:22
  91.1 1.1 %collective-permute-done.26 = f32[64,512]{0,1:T(8,128)} collective-permute-done((f32[64,512]{0,1:T(8,128)}, f32[64,512]{0,1:T(8,128)}, u32[]{:S(2)}, u32[]{:S(2)}) %collective-permute-start.26) | collective-permute-done | bytes 131104 | tf_op jit(solution)/shard_map/ppermute | solution.py:22
  92.2 1.0 broadcast_select_fusion.4
  93.2 6.4 %collective-permute-done.18 = f32[64,1280]{1,0:T(8,128)} collective-permute-done((f32[64,1280]{1,0:T(8,128)S(1)}, f32[64,1280]{1,0:T(8,128)}, u32[]{:S(2)}, u32[]{:S(2)}) %collective-permute-start.18) | collective-permute-done | bytes 327712 | tf_op jit(solution)/shard_map/ppermute | solution.py:22
  99.6 1.2 %copy.22 = f32[64,1280]{0,1:T(8,128)S(1)} copy(f32[64,1280]{1,0:T(8,128)} %collective-permute-done.18) | data formatting | bytes 655360 | tf_op jit(solution)/shard_map/ppermute | solution.py:22
  100.9 0.9 fusion.10
  102.0 0.4 fusion.8
  102.8 1.9 %fusion = f32[1280,384]{0,1:T(8,128)S(1)} fusion(f32[1280,384]{0,1:T(8,128)S(1)} %copy.28, pred[1280]{0:T(1024)(128)(4,1)S(1)} %fusion.13, f32[64,1216]{1,0:T(8,128)S(1)} %slice.97, f32[64,64]{1,0:T(8,128)S(1)} %copy.24, f32[64,320]{1,0:T(8,128)S(1)} %slice.99, f32[64,64]{1,0:T(8,128)S(1)} %copy.26), kind=kOutput, calls=%fused_computation.1 | convolution fusion | flops 378576896 | bytes 4359424 | tf_op jit(solution)/shard_map/dot_general | solution.py:128
  105.2 1.8 %copy.29 = f32[1280,384]{1,0:T(8,128)} copy(f32[1280,384]{0,1:T(8,128)S(1)} %pad_maximum_fusion) | data formatting | bytes 3932160 | tf_op jit(solution)/shard_map/concatenate | solution.py:139
  (67 shorter events, 2.7 us)
Async XLA Ops:
  1.1 3.4 %collective-permute-start.7 = (f32[64,64]{0,1:T(8,128)S(1)}, f32[64,64]{0,1:T(8,128)S(1)}, u32[]{:S(2)}, u32[]{:S(2)}) collective-permute-start(f32[64,64]{0,1:T(8,128)S(1)} %slice.95), channel_id=1, source_target_pairs={{0,16}} | collective-permute-start | bytes 49160 | tf_op jit(solution)/shard_map/ppermute | solution.py:22
  1.8 3.4 %collective-permute-start.6 = (f32[64,64]{0,1:T(8,128)S(1)}, f32[64,64]{0,1:T(8,128)S(1)}, u32[]{:S(2)}, u32[]{:S(2)}) collective-permute-start(f32[64,64]{0,1:T(8,128)S(1)} %slice.95), channel_id=1, source_target_pairs={{0,32}} | collective-permute-start | bytes 49160 | tf_op jit(solution)/shard_map/ppermute | solution.py:22
  2.5 3.4 %collective-permute-start.5 = (f32[64,64]{0,1:T(8,128)S(1)}, f32[64,64]{0,1:T(8,128)S(1)}, u32[]{:S(2)}, u32[]{:S(2)}) collective-permute-start(f32[64,64]{0,1:T(8,128)S(1)} %slice.95), channel_id=1, source_target_pairs={{0,48}} | collective-permute-start | bytes 49160 | tf_op jit(solution)/shard_map/ppermute | solution.py:22
  3.2 2.8 %collective-permute-start.4 = (f32[64,64]{0,1:T(8,128)S(1)}, f32[64,64]{0,1:T(8,128)S(1)}, u32[]{:S(2)}, u32[]{:S(2)}) collective-permute-start(f32[64,64]{0,1:T(8,128)S(1)} %slice.95), channel_id=1, source_target_pairs={{0,64}} | collective-permute-start | bytes 49160 | tf_op jit(solution)/shard_map/ppermute | solution.py:22
  3.8 2.1 %collective-permute-start.3 = (f32[64,64]{0,1:T(8,128)S(1)}, f32[64,64]{0,1:T(8,128)S(1)}, u32[]{:S(2)}, u32[]{:S(2)}) collective-permute-start(f32[64,64]{0,1:T(8,128)S(1)} %slice.95), channel_id=1, source_target_pairs={{0,80}} | collective-permute-start | bytes 49160 | tf_op jit(solution)/shard_map/ppermute | solution.py:22
  4.5 1.4 %collective-permute-start.2 = (f32[64,64]{0,1:T(8,128)S(1)}, f32[64,64]{0,1:T(8,128)S(1)}, u32[]{:S(2)}, u32[]{:S(2)}) collective-permute-start(f32[64,64]{0,1:T(8,128)S(1)} %slice.95), channel_id=1, source_target_pairs={{0,96}} | collective-permute-start | bytes 49160 | tf_op jit(solution)/shard_map/ppermute | solution.py:22
  5.2 0.8 collective-permute-start.1
  6.0 3.6 %collective-permute-start.12 = (f32[64,64]{0,1:T(8,128)S(1)}, f32[64,64]{0,1:T(8,128)S(1)}, u32[]{:S(2)}, u32[]{:S(2)}) collective-permute-start(f32[64,64]{0,1:T(8,128)S(1)} %select_select_fusion.6), channel_id=1, source_target_pairs={{0,128},{16,144},{32,160},{48,176},{64,192},{80,208},{96,224},{112... | collective-permute-start | bytes 49160 | tf_op jit(solution)/shard_map/ppermute | solution.py:22
  6.7 3.7 %collective-permute-start.11 = (f32[64,64]{0,1:T(8,128)S(1)}, f32[64,64]{0,1:T(8,128)S(1)}, u32[]{:S(2)}, u32[]{:S(2)}) collective-permute-start(f32[64,64]{0,1:T(8,128)S(1)} %select_select_fusion.6), channel_id=1, source_target_pairs={{0,256},{16,272},{32,288},{48,304},{64,320},{80,336},{96,352},{112... | collective-permute-start | bytes 49160 | tf_op jit(solution)/shard_map/ppermute | solution.py:22
  7.3 3.0 %collective-permute-start.10 = (f32[64,64]{0,1:T(8,128)S(1)}, f32[64,64]{0,1:T(8,128)S(1)}, u32[]{:S(2)}, u32[]{:S(2)}) collective-permute-start(f32[64,64]{0,1:T(8,128)S(1)} %select_select_fusion.6), channel_id=1, source_target_pairs={{0,384},{16,400},{32,416},{48,432},{64,448},{80,464},{96,480},{112... | collective-permute-start | bytes 49160 | tf_op jit(solution)/shard_map/ppermute | solution.py:22
  8.0 2.4 %collective-permute-start.9 = (f32[64,64]{0,1:T(8,128)S(1)}, f32[64,64]{0,1:T(8,128)S(1)}, u32[]{:S(2)}, u32[]{:S(2)}) collective-permute-start(f32[64,64]{0,1:T(8,128)S(1)} %select_select_fusion.6), channel_id=1, source_target_pairs={{0,512},{16,528},{32,544},{48,560},{64,576},{80,592},{96,608},{112... | collective-permute-start | bytes 49160 | tf_op jit(solution)/shard_map/ppermute | solution.py:22
  8.7 1.7 %collective-permute-start.8 = (f32[64,64]{0,1:T(8,128)S(1)}, f32[64,64]{0,1:T(8,128)S(1)}, u32[]{:S(2)}, u32[]{:S(2)}) collective-permute-start(f32[64,64]{0,1:T(8,128)S(1)} %select_select_fusion.6), channel_id=1, source_target_pairs={{0,640},{16,656},{32,672},{48,688},{64,704},{80,720},{96,736},{112... | collective-permute-start | bytes 49160 | tf_op jit(solution)/shard_map/ppermute | solution.py:22
  9.6 15.5 %collective-permute-start = (f32[64,1280]{1,0:T(8,128)S(1)}, f32[64,1280]{1,0:T(8,128)S(1)}, u32[]{:S(2)}, u32[]{:S(2)}) collective-permute-start(f32[64,1280]{1,0:T(8,128)S(1)} %copy.12), channel_id=1, source_target_pairs={{0,1},{16,17},{32,33},{48,49},{64,65},{80,81},{96,97},{112,113},{1... | collective-permute-start | bytes 983048 | tf_op jit(solution)/shard_map/ppermute | solution.py:22
  22.9 2.2 %collective-permute-start.13 = (f32[64,256]{0,1:T(8,128)S(1)}, f32[64,256]{0,1:T(8,128)S(1)}, u32[]{:S(2)}, u32[]{:S(2)}) collective-permute-start(f32[64,256]{0,1:T(8,128)S(1)} %pad_maximum_fusion.3), channel_id=1, source_target_pairs={{16,17},{32,34},{48,51},{64,68},{80,85},{96,102},{112,119},{128,13... | collective-permute-start | bytes 196616 | tf_op jit(solution)/shard_map/ppermute | solution.py:78
  23.7 2.8 %collective-permute-start.14 = (f32[64,256]{0,1:T(8,128)S(1)}, f32[64,256]{0,1:T(8,128)S(1)}, u32[]{:S(2)}, u32[]{:S(2)}) collective-permute-start(f32[64,256]{0,1:T(8,128)S(1)} %pad_maximum_fusion.3), channel_id=1, source_target_pairs={{0,256},{16,273},{32,290},{48,307},{64,324},{80,341},{96,358},{112... | collective-permute-start | bytes 196616 | tf_op jit(solution)/shard_map/ppermute | solution.py:78
  24.4 2.1 %collective-permute-start.15 = (f32[64,256]{0,1:T(8,128)S(1)}, f32[64,256]{0,1:T(8,128)S(1)}, u32[]{:S(2)}, u32[]{:S(2)}) collective-permute-start(f32[64,256]{0,1:T(8,128)S(1)} %pad_maximum_fusion.3), channel_id=1, source_target_pairs={{0,512},{16,529},{32,546},{48,563},{64,580},{80,597},{96,614},{112... | collective-permute-start | bytes 196616 | tf_op jit(solution)/shard_map/ppermute | solution.py:78
  26.8 4.9 %collective-permute-start.16 = (f32[64,1280]{1,0:T(8,128)S(1)}, f32[64,1280]{1,0:T(8,128)S(1)}, u32[]{:S(2)}, u32[]{:S(2)}) collective-permute-start(f32[64,1280]{1,0:T(8,128)S(1)} %copy.17), channel_id=1, source_target_pairs={{0,8},{1,9},{16,24},{17,25},{32,40},{33,41},{48,56},{49,57},{64,72... | collective-permute-start | bytes 983048 | tf_op jit(solution)/shard_map/ppermute | solution.py:22
  27.5 5.7 %collective-permute-start.25 = (f32[64,512]{0,1:T(8,128)S(1)}, f32[64,512]{0,1:T(8,128)S(1)}, u32[]{:S(2)}, u32[]{:S(2)}) collective-permute-start(f32[64,512]{0,1:T(8,128)S(1)} %maximum_select_fusion), channel_id=1, source_target_pairs={{0,16},{256,272},{512,528},{17,33},{273,289},{529,545},{34,50},{29... | collective-permute-start | bytes 393224 | tf_op jit(solution)/shard_map/ppermute | solution.py:22
  28.2 6.4 %collective-permute-start.24 = (f32[64,512]{0,1:T(8,128)S(1)}, f32[64,512]{0,1:T(8,128)S(1)}, u32[]{:S(2)}, u32[]{:S(2)}) collective-permute-start(f32[64,512]{0,1:T(8,128)S(1)} %maximum_select_fusion), channel_id=1, source_target_pairs={{0,32},{256,288},{512,544},{17,49},{273,305},{529,561},{34,66},{29... | collective-permute-start | bytes 393224 | tf_op jit(solution)/shard_map/ppermute | solution.py:22
  28.9 8.0 %collective-permute-start.23 = (f32[64,512]{0,1:T(8,128)S(1)}, f32[64,512]{0,1:T(8,128)}, u32[]{:S(2)}, u32[]{:S(2)}) collective-permute-start(f32[64,512]{0,1:T(8,128)S(1)} %maximum_select_fusion), channel_id=1, source_target_pairs={{0,48},{256,304},{512,560},{17,65},{273,321},{529,577},{34,82},{29... | collective-permute-start | bytes 393224 | tf_op jit(solution)/shard_map/ppermute | solution.py:22
  30.3 9.4 %collective-permute-start.22 = (f32[64,512]{0,1:T(8,128)S(1)}, f32[64,512]{0,1:T(8,128)}, u32[]{:S(2)}, u32[]{:S(2)}) collective-permute-start(f32[64,512]{0,1:T(8,128)S(1)} %maximum_select_fusion), channel_id=1, source_target_pairs={{0,64},{256,320},{512,576},{17,81},{273,337},{529,593},{34,98},{29... | collective-permute-start | bytes 393224 | tf_op jit(solution)/shard_map/ppermute | solution.py:22
  31.7 8.0 %collective-permute-start.21 = (f32[64,512]{0,1:T(8,128)S(1)}, f32[64,512]{0,1:T(8,128)}, u32[]{:S(2)}, u32[]{:S(2)}) collective-permute-start(f32[64,512]{0,1:T(8,128)S(1)} %maximum_select_fusion), channel_id=1, source_target_pairs={{0,80},{256,336},{512,592},{17,97},{273,353},{529,609},{34,114},{2... | collective-permute-start | bytes 393224 | tf_op jit(solution)/shard_map/ppermute | solution.py:22
  33.3 4.4 %copy-start = (f32[64,512]{0,1:T(8,128)}, f32[64,512]{0,1:T(8,128)S(1)}, u32[]{:S(2)}) copy-start(f32[64,512]{0,1:T(8,128)S(1)} %collective-permute-done.25) | copy-start | bytes 393220
  33.3 6.4 %collective-permute-start.20 = (f32[64,512]{0,1:T(8,128)S(1)}, f32[64,512]{0,1:T(8,128)}, u32[]{:S(2)}, u32[]{:S(2)}) collective-permute-start(f32[64,512]{0,1:T(8,128)S(1)} %maximum_select_fusion), channel_id=1, source_target_pairs={{0,96},{256,352},{512,608},{17,113},{273,369},{529,625},{34,130},{... | collective-permute-start | bytes 393224 | tf_op jit(solution)/shard_map/ppermute | solution.py:22
  34.6 0.7 copy-start.1
  35.4 49.3 %collective-permute-start.19 = (f32[64,512]{0,1:T(8,128)S(1)}, f32[64,512]{0,1:T(8,128)}, u32[]{:S(2)}, u32[]{:S(2)}) collective-permute-start(f32[64,512]{0,1:T(8,128)S(1)} %maximum_select_fusion), channel_id=1, source_target_pairs={{0,112},{256,368},{512,624},{17,129},{273,385},{529,641},{34,146},... | collective-permute-start | bytes 393224 | tf_op jit(solution)/shard_map/ppermute | solution.py:22
  37.0 51.5 %collective-permute-start.17 = (f32[64,1280]{1,0:T(8,128)S(1)}, f32[64,1280]{1,0:T(8,128)S(1)}, u32[]{:S(2)}, u32[]{:S(2)}) collective-permute-start(f32[64,1280]{1,0:T(8,128)S(1)} %copy.19), channel_id=1, source_target_pairs={{0,4},{1,5},{8,12},{9,13},{16,20},{17,21},{24,28},{25,29},{32,36},... | collective-permute-start | bytes 983048 | tf_op jit(solution)/shard_map/ppermute | solution.py:22
  86.4 5.8 %collective-permute-start.26 = (f32[64,512]{0,1:T(8,128)}, f32[64,512]{0,1:T(8,128)}, u32[]{:S(2)}, u32[]{:S(2)}) collective-permute-start(f32[64,512]{0,1:T(8,128)} %select_select_fusion), channel_id=1, source_target_pairs={{0,128},{16,144},{32,160},{48,176},{64,192},{80,208},{96,224},{112... | collective-permute-start | bytes 393224 | tf_op jit(solution)/shard_map/ppermute | solution.py:22
  89.8 9.8 %collective-permute-start.18 = (f32[64,1280]{1,0:T(8,128)S(1)}, f32[64,1280]{1,0:T(8,128)}, u32[]{:S(2)}, u32[]{:S(2)}) collective-permute-start(f32[64,1280]{1,0:T(8,128)S(1)} %copy.21), channel_id=1, source_target_pairs={{0,2},{1,3},{8,10},{9,11},{4,6},{5,7},{12,14},{13,15},{16,18},{17,... | collective-permute-start | bytes 983048 | tf_op jit(solution)/shard_map/ppermute | solution.py:22
